TPU v7x, 256 devices: a whole 4x4x8 slice. The times are simulated.
256 devices in a mesh: dp: 128 (over z, x, y), group: 2 (over core).
Axes of the slice: x: 4, y: 4, z: 8, core: 2. Of those that a mesh axis runs over, the one named last changes fastest.
Arguments:
- queries: bfloat16 [2048, 1024], P(('dp', 'group')), may hold values from -6 to 6
- passage_hidden: bfloat16 [32768, 1024], P('dp'), may hold values from -24 to 24
- out_weight: bfloat16 [1024, 1024], replicated, may hold values from -0.1875 to 0.1875
- neg_owner: int32 [65536, 1], P(('dp', 'group')), may hold values from 0 to 127; in each aligned block of 256 rows (0 to 255, 256 to 511, ...) at most 4 rows name the same one
- neg_local: int32 [2048, 32], P(('dp', 'group')), may hold values from 0 to 255
Outputs:
- weight_grad: float32 [1024, 1024], P('dp')
- query_loss: float32 [2048], P(('dp', 'group'))
Inputs may be any that keep to these rules, and one draw needn't show every extreme that they name: `neg_owner`: the 256 rows of one device name one owner at most 4 times; some device names some owner exactly 4 times.
All inputs are finite; a program needn't handle non-finite values.
Results may differ from a plain program's by a relative error of at most 0.0045.
Values may be sent and summed in bfloat16 or wider, within the bound.
No kernel may reach another device: no remote copies, remote signals or barrier semaphores. Data moves between devices by JAX's collectives and lax.ppermute only.
A program may use at most 64 MiB of HBM per device.

v0:
```python
import math

import jax
import jax.numpy as jnp
from jax import lax
from jax.sharding import PartitionSpec as P


def transposed_dot(left, right):
    return lax.dot_general(
        left, right, (((0,), (0,)), ((), ())), preferred_element_type=jnp.float32
    )


def local(queries, passage_hidden, out_weight, neg_owner, neg_local):
    dp_count = lax.axis_size("dp")
    group_pos = lax.axis_index("group")
    query_rows, width = queries.shape
    passage_rows = passage_hidden.shape[0]
    neg_count = neg_local.shape[1]
    ref_count = query_rows * neg_count
    capacity = 2 * ref_count // dp_count
    score_scale = 1.5 / math.sqrt(width)
    embedded = jnp.dot(passage_hidden, out_weight, preferred_element_type=jnp.float32).astype(
        jnp.bfloat16
    )
    owners = neg_owner.reshape(ref_count)
    local_ids = neg_local.reshape(ref_count)
    one_hot = (owners[:, None] == jnp.arange(dp_count, dtype=jnp.int32)[None, :]).astype(jnp.int32)
    slot_rank = jnp.sum((jnp.cumsum(one_hot, axis=0) - one_hot) * one_hot, axis=1)
    position = owners * capacity + slot_rank
    requests = (
        jnp.zeros((dp_count * capacity,), jnp.int32)
        .at[position]
        .set(local_ids)
        .reshape(dp_count, capacity)
    )
    id_block = lax.all_to_all(requests, "dp", split_axis=0, concat_axis=0, tiled=True)
    key_block = jnp.take(embedded, id_block, axis=0)
    returned_keys = lax.all_to_all(key_block, "dp", split_axis=0, concat_axis=0, tiled=True)
    neg_keys = jnp.take(
        returned_keys.reshape(dp_count * capacity, width), position, axis=0
    ).reshape(query_rows, neg_count, width)
    own_rows = lax.dynamic_slice_in_dim(embedded, group_pos * query_rows, query_rows, 0)
    pos_logit = (
        jnp.einsum("qd,qd->q", queries, own_rows, preferred_element_type=jnp.float32) * score_scale
    )
    neg_logit = (
        jnp.einsum("qd,qjd->qj", queries, neg_keys, preferred_element_type=jnp.float32)
        * score_scale
    )
    logits = jnp.concatenate([pos_logit[:, None], neg_logit], axis=1)
    log_total = jnp.log(jnp.sum(jnp.exp(logits), axis=1))
    query_loss = log_total - pos_logit
    soft_prob = jnp.exp(logits - log_total[:, None])
    query_f32 = queries.astype(jnp.float32)
    neg_rows = (soft_prob[:, 1:, None] * score_scale * query_f32[:, None, :]).astype(jnp.bfloat16)
    outgoing = (
        jnp.zeros((dp_count * capacity, width), jnp.bfloat16)
        .at[position]
        .set(neg_rows.reshape(ref_count, width))
    )
    returned = lax.all_to_all(
        outgoing.reshape(dp_count, capacity, width), "dp", split_axis=0, concat_axis=0, tiled=True
    )
    embed_grad = jnp.zeros((passage_rows, width), jnp.float32)
    embed_grad = embed_grad.at[id_block.reshape(-1)].add(
        returned.reshape(-1, width).astype(jnp.float32)
    )
    pos_rows = ((soft_prob[:, 0] - 1.0) * score_scale)[:, None] * query_f32
    own_grad = (
        lax.dynamic_slice_in_dim(embed_grad, group_pos * query_rows, query_rows, 0) + pos_rows
    )
    embed_grad = lax.dynamic_update_slice_in_dim(embed_grad, own_grad, group_pos * query_rows, 0)
    grad_bf16 = embed_grad.astype(jnp.bfloat16)
    dw_rows = lax.psum_scatter(
        transposed_dot(passage_hidden, grad_bf16), "dp", scatter_dimension=0, tiled=True
    )
    weight_grad = lax.psum(dw_rows, "group")
    return (weight_grad, query_loss)


def solution(mesh):
    placed = (
        P(("dp", "group"), None),
        P("dp", None),
        P(),
        P(("dp", "group"), None),
        P(("dp", "group"), None),
    )
    return jax.shard_map(
        local,
        mesh=mesh,
        in_specs=placed,
        out_specs=(P("dp", None), P(("dp", "group"))),
        check_vma=False,
    )
```

profile of v0, /device:TPU:1, one launch (start us, length us, event | category | flops | bytes accessed | tf_op | source)
XLA Modules:
  0.0 857.7 jit_solution(9922702424454829848)
XLA Ops:
  7.2 0.0 copy-start
  7.2 0.9 reshape.152
  8.1 0.8 copy.18
  8.9 0.2 fusion.10
  9.2 0.9 fusion.12
  10.0 0.7 and_reduce_fusion
  10.8 1.4 scatter_custom_fusion
  12.2 0.7 all_to_all.16
  12.9 16.3 %all-to-all-start = ((s32[128,1,4]{2,1,0:T(1,128)}), s32[128,1,4]{2,1,0:T(1,128)S(1)}, u32[]{:S(2)}, u32[]{:S(2)}) async-start(s32[128,1,4]{2,1,0:T(1,128)} %bitcast.7), calls=%async_computation | async-start | bytes 131072 | tf_op jit(solution)/shard_map/all_to_all | solution.py:38
  29.2 1.8 convolution_convert_fusion
  31.0 9.0 %all-to-all-done = s32[128,1,4]{2,1,0:T(1,128)S(1)} async-done(((s32[128,1,4]{2,1,0:T(1,128)}), s32[128,1,4]{2,1,0:T(1,128)S(1)}, u32[]{:S(2)}, u32[]{:S(2)}) %all-to-all-start) | async-done | bytes 2080 | tf_op jit(solution)/shard_map/all_to_all | solution.py:38
  40.0 0.1 reshape.134
  40.1 2.8 gather_fusion
  42.9 2.3 reshape.133
  45.2 2.8 broadcast_select_fusion
  48.0 7.3 all-to-all-start.1
  55.4 0.1 broadcast_in_dim.42
  55.5 0.1 fusion.15
  55.6 0.1 copy.21
  55.7 26.7 %all-to-all-done.1 = bf16[128,4,1024]{2,1,0:T(4,128)(2,1)} async-done(((bf16[128,4,1024]{2,1,0:T(4,128)(2,1)}), bf16[128,4,1024]{2,1,0:T(4,128)(2,1)}, u32[]{:S(2)}, u32[]{:S(2)}) %all-to-all-start.1) | async-done | bytes 1048608 | tf_op jit(solution)/shard_map/all_to_all | solution.py:40
  82.4 1.3 reshape.129
  83.7 2.0 gather_fusion.1
  85.7 1.3 fusion.2
  87.0 0.2 exponential_reduce_fusion
  87.2 0.5 multiply_subtract_fusion
  87.8 0.1 subtract_exponential_fusion
  87.8 0.1 slice_multiply_fusion
  87.9 0.1 mul.70
  88.0 0.9 fusion
  88.9 2.4 scatter_custom_fusion.1
  91.3 1.2 reshape.130
  92.6 8.7 %all-to-all-start.2 = ((bf16[128,4,1024]{2,1,0:T(4,128)(2,1)}), bf16[128,4,1024]{2,1,0:T(4,128)(2,1)S(1)}, u32[]{:S(2)}, u32[]{:S(2)}) async-start(bf16[128,4,1024]{2,1,0:T(4,128)(2,1)} %reshape.130), calls=%async_computation.2 | async-start | bytes 2097152 | tf_op jit(solution)/shard_map/all_to_all | solution.py:63
  101.2 0.0 reduce-scatter.4.cloned.1.call-start
  101.3 0.5 broadcast.126
  101.8 0.8 reduce.9
  102.6 0.1 reshape.128
  102.7 0.1 multiply_reduce_fusion
  102.8 25.4 %all-to-all-done.2 = bf16[128,4,1024]{2,1,0:T(4,128)(2,1)S(1)} async-done(((bf16[128,4,1024]{2,1,0:T(4,128)(2,1)}), bf16[128,4,1024]{2,1,0:T(4,128)(2,1)S(1)}, u32[]{:S(2)}, u32[]{:S(2)}) %all-to-all-start.2) | async-done | bytes 1048608 | tf_op jit(solution)/shard_map/all_to_all | solution.py:63
  128.2 1.4 reshape.168
  129.7 5.9 scatter_custom_fusion.2
  135.6 0.1 add_dynamic-update-slice_fusion
  135.7 3.8 convolution_bitcast_fusion
  139.4 5.3 copy.30
  144.8 0.0 reduce-scatter.4.cloned.1.call-update
  144.8 594.1 %reduce-scatter.4.cloned.1.call-done = f32[8,1024]{1,0:T(8,128)} async-done(((f32[1024,1024]{1,0:T(8,128)}), f32[8,1024]{1,0:T(8,128)}) %reduce-scatter.4.cloned.1.call-update) | async-done | bytes 32784
  738.9 0.9 copy.31
  739.8 110.2 %psum.7 = f32[8,1024]{0,1:T(8,128)S(1)} all-reduce(f32[8,1024]{0,1:T(8,128)S(1)} %copy.31), channel_id=1, replica_groups=mesh['dp'=128,'group'=2] {'group'}, use_global_device_ids=true, to_apply=%region_8.9 | all-reduce | flops 8192 | bytes 65536 | tf_op jit(solution)/shard_map/psum | solution.py:79
  850.1 0.8 copy.22
  (17 shorter events, 0.2 us)
Async XLA Ops:
  7.2 22.1 %copy-start = (bf16[1024,1024]{1,0:T(8,128)(2,1)S(1)}, bf16[1024,1024]{1,0:T(8,128)(2,1)}, u32[]{:S(2)}) copy-start(bf16[1024,1024]{1,0:T(8,128)(2,1)} %param.7) | copy-start | bytes 6291460
  12.9 27.1 %all-to-all-start = ((s32[128,1,4]{2,1,0:T(1,128)}), s32[128,1,4]{2,1,0:T(1,128)S(1)}, u32[]{:S(2)}, u32[]{:S(2)}) async-start(s32[128,1,4]{2,1,0:T(1,128)} %bitcast.7), calls=%async_computation | async-start | bytes 131072 | tf_op jit(solution)/shard_map/all_to_all | solution.py:38
  45.2 10.2 %copy-start.1 = (bf16[8,1024]{1,0:T(8,128)(2,1)S(1)}, bf16[8,1024]{1,0:T(8,128)(2,1)}, u32[]{:S(2)}) copy-start(bf16[8,1024]{1,0:T(8,128)(2,1)} %param.5) | copy-start | bytes 49156
  48.0 34.3 %all-to-all-start.1 = ((bf16[128,4,1024]{2,1,0:T(4,128)(2,1)}), bf16[128,4,1024]{2,1,0:T(4,128)(2,1)}, u32[]{:S(2)}, u32[]{:S(2)}) async-start(bf16[128,4,1024]{2,1,0:T(4,128)(2,1)} %broadcast_select_fusion), calls=%async_computation.1 | async-start | bytes 2097152 | tf_op jit(solution)/shard_map/all_to_all | solution.py:40
  92.6 35.7 %all-to-all-start.2 = ((bf16[128,4,1024]{2,1,0:T(4,128)(2,1)}), bf16[128,4,1024]{2,1,0:T(4,128)(2,1)S(1)}, u32[]{:S(2)}, u32[]{:S(2)}) async-start(bf16[128,4,1024]{2,1,0:T(4,128)(2,1)} %reshape.130), calls=%async_computation.2 | async-start | bytes 2097152 | tf_op jit(solution)/shard_map/all_to_all | solution.py:63
  101.2 637.7 %reduce-scatter.4.cloned.1.call-start = ((), (), s32[]{:S(2)}) async-start(), calls=%async_computation.4 | async-start | bytes 4227072
Sparse Core Ops, SparseCore 0:
  144.9 593.8 reduce-scatter.3
where the time goes:
time: 858 us
  waiting for transfers between devices  655 us (76%)
  blocking collectives  110 us (13%)
  starting transfers between devices  32.4 us (4%)
  local copies, waits for them, and re-layouts  25.3 us (3%)
  between operations  14.2 us (2%)
  other arithmetic  13.6 us (2%)
    unnamed x2, waiting for transfers between devices  594 us
    psum x1, blocking collectives, local(): weight_grad = lax.psum(dw_rows, 'group')  110 us
    all_to_all x1, waiting for transfers between devices, local(): lax.all_to_all(key_block, 'dp', split_axis=0, concat_axis=0, tiled=True)  26.7 us
    all_to_all x1, waiting for transfers between devices, local(): lax.all_to_all(outgoing.reshape(dp_count, capacity, width), 'dp', split_a...  25.4 us
  transfers between devices with their start and end apart: 4, of which 4 were waited for; matrix products, arithmetic and copies ran while one was open for 0% of the time, Pallas kernels for 0%

commit v1 on v0

--- a/solution.py
+++ b/solution.py
@@ -74,9 +74,9 @@
     embed_grad = lax.dynamic_update_slice_in_dim(embed_grad, own_grad, group_pos * query_rows, 0)
     grad_bf16 = embed_grad.astype(jnp.bfloat16)
     dw_rows = lax.psum_scatter(
-        transposed_dot(passage_hidden, grad_bf16), "dp", scatter_dimension=0, tiled=True
+        transposed_dot(passage_hidden, grad_bf16), ("dp", "group"), scatter_dimension=0, tiled=True
     )
-    weight_grad = lax.psum(dw_rows, "group")
+    weight_grad = lax.all_gather(dw_rows, "group", axis=0, tiled=True)
     return (weight_grad, query_loss)
 
 

time: 858 us -> 418 us (0.49)
  waiting for transfers between devices: 655 us -> 326 us
  blocking collectives: 110 us -> 3.72 us
    unnamed x2, waiting for transfers between devices: 594 us -> 265 us
    psum x1 -> x0, blocking collectives: 110 us -> none  [local(): weight_grad = lax.psum(dw_rows, 'group')]
  transfers between devices with their start and end apart: 4 -> 4, of which waited for: 4 -> 4; matrix products, arithmetic and copies ran while one was open for 0% -> 1% of each run, Pallas kernels for 0% -> 0%
where the time goes in v1:
time: 418 us; the launch traced here: 417 us
  waiting for transfers between devices  326 us (78%)
  starting transfers between devices  32.3 us (8%)
  local copies, waits for them, and re-layouts  20.3 us (5%)
  between operations  14.2 us (3%)
  other arithmetic  13.6 us (3%)
  matrix products  6.86 us (2%)
    unnamed x2, waiting for transfers between devices  265 us
    all_to_all x1, waiting for transfers between devices, local(): lax.all_to_all(key_block, 'dp', split_axis=0, concat_axis=0, tiled=True)  26.7 us
    all_to_all x1, waiting for transfers between devices, local(): lax.all_to_all(outgoing.reshape(dp_count, capacity, width), 'dp', split_a...  25.4 us
    all_to_all x1, starting transfers between devices, local(): lax.all_to_all(requests, 'dp', split_axis=0, concat_axis=0, tiled=True)  16.3 us
    all_to_all x1, waiting for transfers between devices, local(): lax.all_to_all(requests, 'dp', split_axis=0, concat_axis=0, tiled=True)  8.97 us
    all_to_all x1, starting transfers between devices, local(): lax.all_to_all(outgoing.reshape(dp_count, capacity, width), 'dp', split_a...  8.66 us
  transfers between devices with their start and end apart: 4, of which 4 were waited for; matrix products, arithmetic and copies ran while one was open for 1% of the time, Pallas kernels for 0%

profile of v1, /device:TPU:1, one launch (start us, length us, event | category | flops | bytes accessed | tf_op | source)
XLA Modules:
  0.0 417.0 jit_solution(4072435347960978484)
XLA Ops:
  7.2 0.0 copy-start
  7.2 0.9 copy.17
  8.1 0.2 fusion.10
  8.4 0.9 fusion.12
  9.3 0.7 and_reduce_fusion
  10.0 0.8 reshape.152
  10.8 1.4 scatter_custom_fusion
  12.2 0.7 all_to_all.16
  12.9 16.3 %all-to-all-start = ((s32[128,1,4]{2,1,0:T(1,128)}), s32[128,1,4]{2,1,0:T(1,128)S(1)}, u32[]{:S(2)}, u32[]{:S(2)}) async-start(s32[128,1,4]{2,1,0:T(1,128)} %bitcast.7), calls=%async_computation | async-start | bytes 131072 | tf_op jit(solution)/shard_map/all_to_all | solution.py:38
  29.2 1.8 convolution_convert_fusion
  31.0 9.0 %all-to-all-done = s32[128,1,4]{2,1,0:T(1,128)S(1)} async-done(((s32[128,1,4]{2,1,0:T(1,128)}), s32[128,1,4]{2,1,0:T(1,128)S(1)}, u32[]{:S(2)}, u32[]{:S(2)}) %all-to-all-start) | async-done | bytes 2080 | tf_op jit(solution)/shard_map/all_to_all | solution.py:38
  40.0 0.1 reshape.134
  40.1 2.8 gather_fusion
  42.9 2.3 reshape.133
  45.2 2.8 broadcast_select_fusion
  48.0 7.3 %all-to-all-start.1 = ((bf16[128,4,1024]{2,1,0:T(4,128)(2,1)}), bf16[128,4,1024]{2,1,0:T(4,128)(2,1)}, u32[]{:S(2)}, u32[]{:S(2)}) async-start(bf16[128,4,1024]{2,1,0:T(4,128)(2,1)} %broadcast_select_fusion), calls=%async_computation.1 | async-start | bytes 2097152 | tf_op jit(solution)/shard_map/all_to_all | solution.py:40
  55.4 0.1 broadcast_in_dim.42
  55.5 0.1 fusion.15
  55.6 0.1 copy.20
  55.7 26.7 %all-to-all-done.1 = bf16[128,4,1024]{2,1,0:T(4,128)(2,1)} async-done(((bf16[128,4,1024]{2,1,0:T(4,128)(2,1)}), bf16[128,4,1024]{2,1,0:T(4,128)(2,1)}, u32[]{:S(2)}, u32[]{:S(2)}) %all-to-all-start.1) | async-done | bytes 1048608 | tf_op jit(solution)/shard_map/all_to_all | solution.py:40
  82.4 1.3 reshape.129
  83.7 2.0 gather_fusion.1
  85.7 1.3 fusion.2
  87.0 0.2 exponential_reduce_fusion
  87.2 0.5 multiply_subtract_fusion
  87.8 0.1 subtract_exponential_fusion
  87.8 0.1 slice_multiply_fusion
  87.9 0.1 mul.70
  88.0 0.9 fusion
  88.9 2.4 scatter_custom_fusion.1
  91.3 1.2 reshape.130
  92.6 8.7 %all-to-all-start.2 = ((bf16[128,4,1024]{2,1,0:T(4,128)(2,1)}), bf16[128,4,1024]{2,1,0:T(4,128)(2,1)S(1)}, u32[]{:S(2)}, u32[]{:S(2)}) async-start(bf16[128,4,1024]{2,1,0:T(4,128)(2,1)} %reshape.130), calls=%async_computation.2 | async-start | bytes 2097152 | tf_op jit(solution)/shard_map/all_to_all | solution.py:63
  101.2 0.0 all-reduce.3.cloned.1.call-start
  101.3 0.5 broadcast.126
  101.8 0.8 reduce.9
  102.6 0.1 reshape.128
  102.7 0.1 multiply_reduce_fusion
  102.8 25.4 %all-to-all-done.2 = bf16[128,4,1024]{2,1,0:T(4,128)(2,1)S(1)} async-done(((bf16[128,4,1024]{2,1,0:T(4,128)(2,1)}), bf16[128,4,1024]{2,1,0:T(4,128)(2,1)S(1)}, u32[]{:S(2)}, u32[]{:S(2)}) %all-to-all-start.2) | async-done | bytes 1048608 | tf_op jit(solution)/shard_map/all_to_all | solution.py:63
  128.2 1.4 reshape.168
  129.7 5.9 %scatter_custom_fusion.2 = f32[256,1024]{1,0:T(8,128)S(1)} fusion(s32[512]{0:T(512)S(1)} %bitcast.56, f32[512,1024]{1,0:T(8,128)} %reshape.168, f32[]{:T(128)} %constant.17.clone.1), kind=kCustom, calls=%fused_computation.16 | custom fusion | flops 524288 | bytes 1049088 | tf_op jit(solution)/shard_map/scatter-add | solution.py:67
  135.6 0.1 add_dynamic-update-slice_fusion
  135.7 3.8 convolution_bitcast_fusion
  139.4 0.0 all-reduce.3.cloned.1.call-update
  139.5 264.9 %all-reduce.3.cloned.1.call-done = f32[1024,1024]{0,1:T(8,128)} async-done(((f32[1024,1024]{0,1:T(8,128)}), f32[1024,1024]{0,1:T(8,128)}) %all-reduce.3.cloned.1.call-update) | async-done | bytes 4194320
  404.4 1.2 dynamic-slice_bitcast_fusion
  405.6 0.2 copy.21
  405.8 3.7 all-gather
  409.6 0.6 reshape.174
  (17 shorter events, 0.2 us)
Async XLA Ops:
  7.2 22.1 %copy-start = (bf16[1024,1024]{1,0:T(8,128)(2,1)S(1)}, bf16[1024,1024]{1,0:T(8,128)(2,1)}, u32[]{:S(2)}) copy-start(bf16[1024,1024]{1,0:T(8,128)(2,1)} %param.7) | copy-start | bytes 6291460
  12.9 27.1 %all-to-all-start = ((s32[128,1,4]{2,1,0:T(1,128)}), s32[128,1,4]{2,1,0:T(1,128)S(1)}, u32[]{:S(2)}, u32[]{:S(2)}) async-start(s32[128,1,4]{2,1,0:T(1,128)} %bitcast.7), calls=%async_computation | async-start | bytes 131072 | tf_op jit(solution)/shard_map/all_to_all | solution.py:38
  45.2 10.3 %copy-start.1 = (bf16[8,1024]{1,0:T(8,128)(2,1)S(1)}, bf16[8,1024]{1,0:T(8,128)(2,1)}, u32[]{:S(2)}) copy-start(bf16[8,1024]{1,0:T(8,128)(2,1)} %param.5) | copy-start | bytes 49156
  48.0 34.3 %all-to-all-start.1 = ((bf16[128,4,1024]{2,1,0:T(4,128)(2,1)}), bf16[128,4,1024]{2,1,0:T(4,128)(2,1)}, u32[]{:S(2)}, u32[]{:S(2)}) async-start(bf16[128,4,1024]{2,1,0:T(4,128)(2,1)} %broadcast_select_fusion), calls=%async_computation.1 | async-start | bytes 2097152 | tf_op jit(solution)/shard_map/all_to_all | solution.py:40
  92.6 35.7 %all-to-all-start.2 = ((bf16[128,4,1024]{2,1,0:T(4,128)(2,1)}), bf16[128,4,1024]{2,1,0:T(4,128)(2,1)S(1)}, u32[]{:S(2)}, u32[]{:S(2)}) async-start(bf16[128,4,1024]{2,1,0:T(4,128)(2,1)} %reshape.130), calls=%async_computation.2 | async-start | bytes 2097152 | tf_op jit(solution)/shard_map/all_to_all | solution.py:63
  101.2 303.2 %all-reduce.3.cloned.1.call-start = ((), (), s32[]{:S(2)}) async-start(), calls=%async_computation.3 | async-start | bytes 8388608
Sparse Core Ops, SparseCore 0:
  139.6 264.7 all-reduce.2

commit v2 on v1

v2 whole, which is shorter than its diff:
```python
import math

import jax
import jax.numpy as jnp
from jax import lax
from jax.sharding import PartitionSpec as P


def split_dot(left, right):
    high = left.astype(jnp.bfloat16)
    low = (left - high.astype(jnp.float32)).astype(jnp.bfloat16)
    dims = (((0,), (0,)), ((), ()))
    return lax.dot_general(high, right, dims, preferred_element_type=jnp.float32) + lax.dot_general(
        low, right, dims, preferred_element_type=jnp.float32
    )


def local(queries, passage_hidden, out_weight, neg_owner, neg_local):
    dp_count = lax.axis_size("dp")
    group_pos = lax.axis_index("group")
    query_rows, width = queries.shape
    neg_count = neg_local.shape[1]
    ref_count = query_rows * neg_count
    capacity = 2 * ref_count // dp_count
    out_rows = out_weight.shape[0] // dp_count
    score_scale = 1.5 / math.sqrt(width)
    all_queries = lax.all_gather(queries, ("dp", "group"), axis=0, tiled=True)
    owners = neg_owner.reshape(ref_count)
    local_ids = neg_local.reshape(ref_count)
    one_hot = (owners[:, None] == jnp.arange(dp_count, dtype=jnp.int32)[None, :]).astype(jnp.int32)
    slot_rank = jnp.sum((jnp.cumsum(one_hot, axis=0) - one_hot) * one_hot, axis=1)
    position = owners * capacity + slot_rank
    requests = (
        jnp.zeros((dp_count * capacity,), jnp.int32)
        .at[position]
        .set(local_ids)
        .reshape(dp_count, capacity)
    )
    id_block = lax.all_to_all(requests, "dp", split_axis=0, concat_axis=0, tiled=True)
    hidden_block = jnp.take(passage_hidden, id_block, axis=0)
    returned_hidden = lax.all_to_all(hidden_block, "dp", split_axis=0, concat_axis=0, tiled=True)
    neg_hidden = jnp.take(returned_hidden.reshape(dp_count * capacity, width), position, axis=0)
    pos_hidden = lax.dynamic_slice_in_dim(passage_hidden, group_pos * query_rows, query_rows, 0)
    neg_keys = jnp.dot(neg_hidden, out_weight, preferred_element_type=jnp.float32).astype(
        jnp.bfloat16
    ).reshape(query_rows, neg_count, width)
    pos_keys = jnp.dot(pos_hidden, out_weight, preferred_element_type=jnp.float32).astype(
        jnp.bfloat16
    )
    pos_logit = (
        jnp.einsum("qd,qd->q", queries, pos_keys, preferred_element_type=jnp.float32) * score_scale
    )
    neg_logit = (
        jnp.einsum("qd,qjd->qj", queries, neg_keys, preferred_element_type=jnp.float32)
        * score_scale
    )
    logits = jnp.concatenate([pos_logit[:, None], neg_logit], axis=1)
    log_total = jnp.log(jnp.sum(jnp.exp(logits), axis=1))
    query_loss = log_total - pos_logit
    soft_prob = jnp.exp(logits - log_total[:, None])
    neg_coef = soft_prob[:, 1:] * score_scale
    pos_coef = (soft_prob[:, 0] - 1.0) * score_scale
    mixed = jnp.sum(
        neg_coef[:, :, None] * neg_hidden.reshape(query_rows, neg_count, width).astype(jnp.float32),
        axis=1,
    ) + pos_coef[:, None] * pos_hidden.astype(jnp.float32)
    mixed_cols = mixed.reshape(query_rows, dp_count, out_rows).transpose(1, 0, 2)
    mixed_cols = lax.all_to_all(mixed_cols, "dp", split_axis=0, concat_axis=0, tiled=True)
    mixed_cols = lax.all_gather(mixed_cols, "group", axis=0)
    mixed_cols = mixed_cols.transpose(1, 0, 2, 3).reshape(-1, out_rows)
    weight_grad = split_dot(mixed_cols, all_queries)
    return (weight_grad, query_loss)


def solution(mesh):
    placed = (
        P(("dp", "group"), None),
        P("dp", None),
        P(),
        P(("dp", "group"), None),
        P(("dp", "group"), None),
    )
    return jax.shard_map(
        local,
        mesh=mesh,
        in_specs=placed,
        out_specs=(P("dp", None), P(("dp", "group"))),
        check_vma=False,
    )
```

time: 418 us -> 146 us (0.35)
  waiting for transfers between devices: 326 us -> 31.1 us
  blocking collectives: 3.72 us -> 61.8 us
  starting transfers between devices: 32.3 us -> 7.35 us
  other arithmetic: 13.6 us -> 6.06 us
    unnamed x2 -> x1, waiting for transfers between devices: 265 us -> 0.68 us
    all_to_all x0 -> x2, blocking collectives: none -> 54.6 us  [the longest x1 27.7 us: local(): lax.all_to_all(mixed_cols, 'dp', split_axis=0, concat_axis=0, tiled=True)]
    all_to_all x3 -> x1, waiting for transfers between devices: 61 us -> 26.7 us  [local(): lax.all_to_all(hidden_block, 'dp', split_axis=0, concat_axis=0, tiled=True)]
    all_to_all x3 -> x1, starting transfers between devices: 32.3 us -> 7.32 us  [local(): lax.all_to_all(hidden_block, 'dp', split_axis=0, concat_axis=0, tiled=True)]
    scatter-add x1 -> x0, other arithmetic: 5.95 us -> none  [local(): embed_grad.at[id_block.reshape(-1)]]
  transfers between devices with their start and end apart: 4 -> 2, of which waited for: 4 -> 2; matrix products, arithmetic and copies ran while one was open for 1% -> 18% of each run, Pallas kernels for 0% -> 0%
where the time goes in v2:
time: 146 us; the launch traced here: 145 us
  blocking collectives  61.8 us (42%)
  waiting for transfers between devices  31.1 us (21%)
  local copies, waits for them, and re-layouts  18.9 us (13%)
  between operations  14.2 us (10%)
  starting transfers between devices  7.35 us (5%)
  other arithmetic  6.06 us (4%)
  matrix products  5.75 us (4%)
    all_to_all x1, blocking collectives, local(): lax.all_to_all(mixed_cols, 'dp', split_axis=0, concat_axis=0, tiled=True)  27.7 us
    all_to_all x1, blocking collectives, local(): lax.all_to_all(requests, 'dp', split_axis=0, concat_axis=0, tiled=True)  26.9 us
    all_to_all x1, waiting for transfers between devices, local(): lax.all_to_all(hidden_block, 'dp', split_axis=0, concat_axis=0, tiled=True)  26.7 us
    all_to_all x1, starting transfers between devices, local(): lax.all_to_all(hidden_block, 'dp', split_axis=0, concat_axis=0, tiled=True)  7.32 us
    all_gather x1, blocking collectives, local(): mixed_cols = lax.all_gather(mixed_cols, 'group', axis=0)  7.24 us
    gather x2, local copies, waits for them, and re-layouts, local(): hidden_block = jnp.take(passage_hidden, id_block, axis=0)  5.07 us
    all_gather x1, waiting for transfers between devices, local(): all_queries = lax.all_gather(queries, ('dp', 'group'), axis=0, tiled=True)  3.73 us
    dot_general x1, matrix products, split_dot(): lax.dot_general(high, right, dims, preferred_element_type=jnp.float32)  2.99 us
  transfers between devices with their start and end apart: 2, of which 2 were waited for; matrix products, arithmetic and copies ran while one was open for 18% of the time, Pallas kernels for 0%

profile of v2, /device:TPU:1, one launch (start us, length us, event | category | flops | bytes accessed | tf_op | source)
XLA Modules:
  0.0 145.2 jit_solution(2462665316846397747)
XLA Ops:
  7.2 0.0 copy-start
  7.2 0.0 copy-start.1
  7.2 0.0 all-gather.3.cloned.1.call-start
  7.2 0.7 all-gather.3.cloned.1.call-update
  7.9 0.8 copy.25
  8.7 0.2 fusion.6
  9.0 0.8 reshape.117
  9.8 0.9 fusion.8
  10.7 0.7 and_reduce_fusion
  11.4 1.4 scatter_custom_fusion
  12.8 0.1 all_to_all.16
  12.9 26.9 %all_to_all.25 = s32[128,1,4]{2,1,0:T(1,128)S(1)} all-to-all(s32[128,1,4]{2,1,0:T(1,128)S(1)} %bitcast.47), channel_id=1, replica_groups=mesh['dp'=128,'group'=2] {'dp'}, dimensions={0} | all-to-all | bytes 4096 | tf_op jit(solution)/shard_map/all_to_all | solution.py:39
  39.8 0.1 reshape.99
  39.9 0.0 copy-done.1
  39.9 2.8 %gather_fusion = bf16[512,1024]{1,0:T(8,128)(2,1)} fusion(bf16[256,1024]{1,0:T(8,128)(2,1)S(1)} %copy-done.1, s32[1024]{0:T(1024)S(1)} %pad_clamp_fusion.1), kind=kCustom, calls=%fused_computation | custom fusion | bytes 2099200 | tf_op jit(solution)/shard_map/jit(_take)/gather | solution.py:40
  42.7 0.0 copy-start.3
  42.7 2.3 %reshape.98 = bf16[128,4,1024]{2,1,0:T(4,128)(2,1)} reshape(bf16[512,1024]{1,0:T(8,128)(2,1)} %gather_fusion) | data formatting | bytes 2097152 | tf_op jit(solution)/shard_map/jit(_take)/gather | solution.py:40
  45.0 2.8 %broadcast_select_fusion = bf16[128,4,1024]{2,1,0:T(4,128)(2,1)} fusion(bf16[128,4,1024]{2,1,0:T(4,128)(2,1)} %reshape.98, pred[128,4]{1,0:T(8,128)(4,1)S(1)} %compare_and_fusion), kind=kLoop, calls=%fused_computation.10 | loop fusion | flops 524288 | bytes 2097664 | tf_op jit(solution)/shard_map/jit(_take)/select_n | solution.py:40
  47.8 7.3 %all-to-all-start.1 = ((bf16[128,4,1024]{2,1,0:T(4,128)(2,1)}), bf16[128,4,1024]{2,1,0:T(4,128)(2,1)}, u32[]{:S(2)}, u32[]{:S(2)}) async-start(bf16[128,4,1024]{2,1,0:T(4,128)(2,1)} %broadcast_select_fusion), calls=%async_computation.1 | async-start | bytes 2097152 | tf_op jit(solution)/shard_map/all_to_all | solution.py:41
  55.2 0.0 copy-done
  55.2 0.0 copy-done.3
  55.2 0.5 fusion.2
  55.7 0.1 copy.28
  55.8 0.1 broadcast_in_dim.43
  55.9 26.7 %all-to-all-done.1 = bf16[128,4,1024]{2,1,0:T(4,128)(2,1)} async-done(((bf16[128,4,1024]{2,1,0:T(4,128)(2,1)}), bf16[128,4,1024]{2,1,0:T(4,128)(2,1)}, u32[]{:S(2)}, u32[]{:S(2)}) %all-to-all-start.1) | async-done | bytes 1048608 | tf_op jit(solution)/shard_map/all_to_all | solution.py:41
  82.6 2.2 %reshape.93 = bf16[512,1024]{1,0:T(8,128)(2,1)} reshape(bf16[128,4,1024]{2,1,0:T(4,128)(2,1)} %all-to-all-done.1) | data formatting | bytes 2097152 | tf_op jit(solution)/shard_map/reshape | solution.py:42
  84.8 2.9 %gather_fusion.1 = bf16[256,1024]{1,0:T(8,128)(2,1)S(1)} fusion(bf16[512,1024]{1,0:T(8,128)(2,1)} %reshape.93, s32[1024]{0:T(1024)S(1)} %pad_clamp_fusion), kind=kCustom, calls=%fused_computation.1 | custom fusion | bytes 1049600 | tf_op jit(solution)/shard_map/jit(_take)/gather | solution.py:42
  87.7 0.8 convolution_convert_fusion
  88.5 0.2 fusion.11
  88.7 0.2 exponential_reduce_fusion
  88.9 0.5 multiply_subtract_fusion
  89.5 0.1 subtract_exponential_fusion
  89.5 0.1 multiply_reduce_fusion.1
  89.7 0.1 slice_multiply_fusion
  89.7 0.3 multiply_reduce_fusion
  90.0 0.1 multiply_add_fusion
  90.1 0.3 reshape.95
  90.4 0.3 copy.29
  90.7 27.7 %all_to_all.26 = f32[128,8,8]{2,1,0:T(8,128)S(1)} all-to-all(f32[128,8,8]{2,1,0:T(8,128)S(1)} %copy.29), channel_id=1, replica_groups=mesh['dp'=128,'group'=2] {'dp'}, dimensions={0} | all-to-all | bytes 65536 | tf_op jit(solution)/shard_map/all_to_all | solution.py:68
  118.4 0.2 copy.30
  118.6 7.2 %all-gather = f32[256,8,8]{0,2,1:T(8,128)S(1)} all-gather(f32[128,8,8]{0,2,1:T(8,128)S(1)} %copy.30), channel_id=2, replica_groups=mesh['dp'=128,'group'=2] {'group'}, dimensions={0}, use_global_device_ids=true | all-gather | bytes 98304 | tf_op jit(solution)/shard_map/all_gather | solution.py:69
  125.9 1.3 copy.31
  127.2 2.7 %reshape.96 = f32[2048,8]{0,1:T(8,128)S(1)} reshape(f32[128,2,8,8]{2,1,0,3:T(2,128)} %bitcast.40) | data formatting | bytes 131072 | tf_op jit(solution)/shard_map/reshape | solution.py:70
  129.9 3.7 %all-gather.3.cloned.1.call-done = bf16[2048,1024]{1,0:T(8,128)(2,1)} async-done(((bf16[8,1024]{1,0:T(8,128)(2,1)}), bf16[2048,1024]{1,0:T(8,128)(2,1)}) %all-gather.3.cloned.1.call-update) | async-done | bytes 4194320 | tf_op jit(solution)/shard_map/all_gather | solution.py:27
  133.6 0.0 copy-start.2
  133.6 3.0 %fusion.14 = f32[8,1024]{1,0:T(8,128)S(1)} fusion(bf16[2048,1024]{1,0:T(8,128)(2,1)} %all-gather.3.cloned.1.call-done, f32[2048,8]{0,1:T(8,128)S(1)} %reshape.96), kind=kOutput, calls=%fused_computation.31 | convolution fusion | flops 33570816 | bytes 4292608 | tf_op jit(solution)/shard_map/dot_general | solution.py:13
  136.6 0.5 copy-done.2
  137.1 1.3 convolution_add_fusion
  (12 shorter events, 0.1 us)
Async XLA Ops:
  7.2 48.0 %copy-start = (bf16[1024,1024]{1,0:T(8,128)(2,1)S(1)}, bf16[1024,1024]{1,0:T(8,128)(2,1)}, u32[]{:S(2)}) copy-start(bf16[1024,1024]{1,0:T(8,128)(2,1)} %param.7) | copy-start | bytes 6291460
  7.2 32.7 %copy-start.1 = (bf16[256,1024]{1,0:T(8,128)(2,1)S(1)}, bf16[256,1024]{1,0:T(8,128)(2,1)}, u32[]{:S(2)}) copy-start(bf16[256,1024]{1,0:T(8,128)(2,1)} %param.6) | copy-start | bytes 1572868
  7.2 126.5 %all-gather.3.cloned.1.call-start = ((), (), s32[]{:S(2)}) async-start(), calls=%async_computation.3 | async-start | bytes 4210688 | tf_op jit(solution)/shard_map/all_gather | solution.py:27
  42.7 12.5 %copy-start.3 = (bf16[8,1024]{1,0:T(8,128)(2,1)S(1)}, bf16[8,1024]{1,0:T(8,128)(2,1)}, u32[]{:S(2)}) copy-start(bf16[8,1024]{1,0:T(8,128)(2,1)} %param.5) | copy-start | bytes 49156
  47.8 34.8 %all-to-all-start.1 = ((bf16[128,4,1024]{2,1,0:T(4,128)(2,1)}), bf16[128,4,1024]{2,1,0:T(4,128)(2,1)}, u32[]{:S(2)}, u32[]{:S(2)}) async-start(bf16[128,4,1024]{2,1,0:T(4,128)(2,1)} %broadcast_select_fusion), calls=%async_computation.1 | async-start | bytes 2097152 | tf_op jit(solution)/shard_map/all_to_all | solution.py:41
  133.6 3.4 %copy-start.2 = (bf16[2048,1024]{1,0:T(8,128)(2,1)S(1)}, bf16[2048,1024]{1,0:T(8,128)(2,1)}, u32[]{:S(2)}) copy-start(bf16[2048,1024]{1,0:T(8,128)(2,1)} %all-gather.3.cloned.1.call-done) | copy-start | bytes 12582916
Sparse Core Ops, SparseCore 0:
  11.7 121.8 all-gather.2

commit v3 on v2

--- a/solution.py
+++ b/solution.py
@@ -24,7 +24,10 @@
     capacity = 2 * ref_count // dp_count
     out_rows = out_weight.shape[0] // dp_count
     score_scale = 1.5 / math.sqrt(width)
-    all_queries = lax.all_gather(queries, ("dp", "group"), axis=0, tiled=True)
+    col_half = width // 2
+    pair_queries = lax.all_gather(queries, "group", axis=0, tiled=True)
+    own_half = lax.dynamic_slice_in_dim(pair_queries, group_pos * col_half, col_half, 1)
+    all_queries = lax.all_gather(own_half, "dp", axis=0, tiled=True)
     owners = neg_owner.reshape(ref_count)
     local_ids = neg_local.reshape(ref_count)
     one_hot = (owners[:, None] == jnp.arange(dp_count, dtype=jnp.int32)[None, :]).astype(jnp.int32)
@@ -68,7 +71,8 @@
     mixed_cols = lax.all_to_all(mixed_cols, "dp", split_axis=0, concat_axis=0, tiled=True)
     mixed_cols = lax.all_gather(mixed_cols, "group", axis=0)
     mixed_cols = mixed_cols.transpose(1, 0, 2, 3).reshape(-1, out_rows)
-    weight_grad = split_dot(mixed_cols, all_queries)
+    weight_half = split_dot(mixed_cols, all_queries)
+    weight_grad = lax.all_gather(weight_half, "group", axis=1, tiled=True)
     return (weight_grad, query_loss)
 
 

time: 146 us -> 165 us (1.13)
  waiting for transfers between devices: 31.1 us -> 55 us
  blocking collectives: 61.8 us -> 40.9 us
  starting transfers between devices: 7.35 us -> 23.7 us
  matrix products: 5.75 us -> 3.98 us
    all_to_all x1 -> x0, blocking collectives: 26.9 us -> none  [local(): lax.all_to_all(requests, 'dp', split_axis=0, concat_axis=0, tiled=True)]
    all_gather x1, waiting for transfers between devices: 3.73 us -> 21.1 us  [local(): all_queries = lax.all_gather(own_half, 'dp', axis=0, tiled=True)]
    all_to_all x0 -> x1, starting transfers between devices: none -> 16.3 us  [local(): lax.all_to_all(requests, 'dp', split_axis=0, concat_axis=0, tiled=True)]
    all_gather x0 -> x2, blocking collectives: none -> 9.23 us  [the longest x1 6.57 us: local(): weight_grad = lax.all_gather(weight_half, 'group', axis=1, tiled=True)]
    all_to_all x0 -> x1, waiting for transfers between devices: none -> 7.38 us  [local(): lax.all_to_all(requests, 'dp', split_axis=0, concat_axis=0, tiled=True)]
    all_gather x1, blocking collectives: 7.24 us -> 5.49 us  [local(): mixed_cols = lax.all_gather(mixed_cols, 'group', axis=0)]
  transfers between devices with their start and end apart: 2 -> 3, of which waited for: 2 -> 3; matrix products, arithmetic and copies ran while one was open for 18% -> 13% of each run, Pallas kernels for 0% -> 0%
where the time goes in v3:
time: 165 us; the launch traced here: 164 us
  waiting for transfers between devices  55 us (33%)
  blocking collectives  40.9 us (25%)
  starting transfers between devices  23.7 us (14%)
  local copies, waits for them, and re-layouts  20.4 us (12%)
  between operations  14.2 us (9%)
  other arithmetic  6.03 us (4%)
  matrix products  3.98 us (2%)
    all_to_all x1, waiting for transfers between devices, local(): lax.all_to_all(hidden_block, 'dp', split_axis=0, concat_axis=0, tiled=True)  26.6 us
    all_to_all x1, blocking collectives, local(): lax.all_to_all(mixed_cols, 'dp', split_axis=0, concat_axis=0, tiled=True)  26.1 us
    all_gather x1, waiting for transfers between devices, local(): all_queries = lax.all_gather(own_half, 'dp', axis=0, tiled=True)  21.1 us
    all_to_all x1, starting transfers between devices, local(): lax.all_to_all(requests, 'dp', split_axis=0, concat_axis=0, tiled=True)  16.3 us
    all_to_all x1, waiting for transfers between devices, local(): lax.all_to_all(requests, 'dp', split_axis=0, concat_axis=0, tiled=True)  7.38 us
    all_to_all x1, starting transfers between devices, local(): lax.all_to_all(hidden_block, 'dp', split_axis=0, concat_axis=0, tiled=True)  7.32 us
    all_gather x1, blocking collectives, local(): weight_grad = lax.all_gather(weight_half, 'group', axis=1, tiled=True)  6.57 us
    all_gather x1, blocking collectives, local(): mixed_cols = lax.all_gather(mixed_cols, 'group', axis=0)  5.49 us
  transfers between devices with their start and end apart: 3, of which 3 were waited for; matrix products, arithmetic and copies ran while one was open for 13% of the time, Pallas kernels for 0%

profile of v3, /device:TPU:1, one launch (start us, length us, event | category | flops | bytes accessed | tf_op | source)
XLA Modules:
  0.0 164.2 jit_solution(13169053438907306087)
XLA Ops:
  7.2 0.0 copy-start
  7.2 0.9 copy.25
  8.1 0.2 fusion.6
  8.4 0.9 fusion.8
  9.3 0.7 and_reduce_fusion
  10.0 0.8 reshape.117
  10.8 1.4 scatter_custom_fusion
  12.2 0.7 all_to_all.16
  12.9 16.3 %all-to-all-start = ((s32[128,1,4]{2,1,0:T(1,128)}), s32[128,1,4]{2,1,0:T(1,128)S(1)}, u32[]{:S(2)}, u32[]{:S(2)}) async-start(s32[128,1,4]{2,1,0:T(1,128)} %bitcast.8), calls=%async_computation | async-start | bytes 131072 | tf_op jit(solution)/shard_map/all_to_all | solution.py:42
  29.2 0.0 all-gather.3.cloned.1.call-start
  29.3 2.7 %all_gather.17 = bf16[16,1024]{1,0:T(8,128)(2,1)S(1)} all-gather(bf16[8,1024]{1,0:T(8,128)(2,1)} %param.5), channel_id=1, replica_groups=mesh['dp'=128,'group'=2] {'group'}, dimensions={0}, use_global_device_ids=true | all-gather | bytes 49152 | tf_op jit(solution)/shard_map/all_gather | solution.py:28
  32.0 0.6 constant_dynamic-slice_fusion
  32.6 0.0 all-gather.3.cloned.1.call-update
  32.6 7.4 %all-to-all-done = s32[128,1,4]{2,1,0:T(1,128)S(1)} async-done(((s32[128,1,4]{2,1,0:T(1,128)}), s32[128,1,4]{2,1,0:T(1,128)S(1)}, u32[]{:S(2)}, u32[]{:S(2)}) %all-to-all-start) | async-done | bytes 2080 | tf_op jit(solution)/shard_map/all_to_all | solution.py:42
  40.0 0.1 reshape.99
  40.1 2.8 %gather_fusion = bf16[512,1024]{1,0:T(8,128)(2,1)} fusion(bf16[256,1024]{1,0:T(8,128)(2,1)S(1)} %copy-done.1, s32[1024]{0:T(1024)S(1)} %pad_clamp_fusion.1), kind=kCustom, calls=%fused_computation | custom fusion | bytes 2099200 | tf_op jit(solution)/shard_map/jit(_take)/gather | solution.py:43
  42.9 2.3 %reshape.98 = bf16[128,4,1024]{2,1,0:T(4,128)(2,1)} reshape(bf16[512,1024]{1,0:T(8,128)(2,1)} %gather_fusion) | data formatting | bytes 2097152 | tf_op jit(solution)/shard_map/jit(_take)/gather | solution.py:43
  45.2 0.0 copy-start.3
  45.2 2.8 %broadcast_select_fusion = bf16[128,4,1024]{2,1,0:T(4,128)(2,1)} fusion(bf16[128,4,1024]{2,1,0:T(4,128)(2,1)} %reshape.98, pred[128,4]{1,0:T(8,128)(4,1)S(1)} %compare_and_fusion), kind=kLoop, calls=%fused_computation.10 | loop fusion | flops 524288 | bytes 2097664 | tf_op jit(solution)/shard_map/jit(_take)/select_n | solution.py:43
  48.0 7.3 %all-to-all-start.1 = ((bf16[128,4,1024]{2,1,0:T(4,128)(2,1)}), bf16[128,4,1024]{2,1,0:T(4,128)(2,1)}, u32[]{:S(2)}, u32[]{:S(2)}) async-start(bf16[128,4,1024]{2,1,0:T(4,128)(2,1)} %broadcast_select_fusion), calls=%async_computation.1 | async-start | bytes 2097152 | tf_op jit(solution)/shard_map/all_to_all | solution.py:44
  55.3 0.5 fusion.2
  55.8 0.1 copy.28
  55.9 0.1 broadcast_in_dim.43
  56.0 26.6 %all-to-all-done.1 = bf16[128,4,1024]{2,1,0:T(4,128)(2,1)} async-done(((bf16[128,4,1024]{2,1,0:T(4,128)(2,1)}), bf16[128,4,1024]{2,1,0:T(4,128)(2,1)}, u32[]{:S(2)}, u32[]{:S(2)}) %all-to-all-start.1) | async-done | bytes 1048608 | tf_op jit(solution)/shard_map/all_to_all | solution.py:44
  82.6 2.1 %reshape.93 = bf16[512,1024]{1,0:T(8,128)(2,1)} reshape(bf16[128,4,1024]{2,1,0:T(4,128)(2,1)} %all-to-all-done.1) | data formatting | bytes 2097152 | tf_op jit(solution)/shard_map/reshape | solution.py:45
  84.7 2.9 %gather_fusion.1 = bf16[256,1024]{1,0:T(8,128)(2,1)S(1)} fusion(bf16[512,1024]{1,0:T(8,128)(2,1)} %reshape.93, s32[1024]{0:T(1024)S(1)} %pad_clamp_fusion), kind=kCustom, calls=%fused_computation.1 | custom fusion | bytes 1049600 | tf_op jit(solution)/shard_map/jit(_take)/gather | solution.py:45
  87.7 0.8 convolution_convert_fusion
  88.4 0.2 fusion.11
  88.7 0.2 exponential_reduce_fusion
  88.9 0.5 multiply_subtract_fusion
  89.4 0.1 subtract_exponential_fusion
  89.5 0.1 multiply_reduce_fusion.1
  89.6 0.1 slice_multiply_fusion
  89.7 0.3 multiply_reduce_fusion
  90.0 0.1 multiply_add_fusion
  90.0 0.3 reshape.95
  90.4 0.3 copy.29
  90.7 26.1 %all_to_all.25 = f32[128,8,8]{2,1,0:T(8,128)S(1)} all-to-all(f32[128,8,8]{2,1,0:T(8,128)S(1)} %copy.29), channel_id=1, replica_groups=mesh['dp'=128,'group'=2] {'dp'}, dimensions={0} | all-to-all | bytes 65536 | tf_op jit(solution)/shard_map/all_to_all | solution.py:71
  116.8 0.2 copy.30
  117.0 5.5 %all-gather = f32[256,8,8]{0,2,1:T(8,128)S(1)} all-gather(f32[128,8,8]{0,2,1:T(8,128)S(1)} %copy.30), channel_id=2, replica_groups=mesh['dp'=128,'group'=2] {'group'}, dimensions={0}, use_global_device_ids=true | all-gather | bytes 98304 | tf_op jit(solution)/shard_map/all_gather | solution.py:72
  122.5 1.3 copy.31
  123.8 2.7 %reshape.96 = f32[2048,8]{0,1:T(8,128)S(1)} reshape(f32[128,2,8,8]{2,1,0,3:T(2,128)} %bitcast.40) | data formatting | bytes 131072 | tf_op jit(solution)/shard_map/reshape | solution.py:73
  126.5 21.1 %all-gather.3.cloned.1.call-done = bf16[2048,512]{1,0:T(8,128)(2,1)} async-done(((bf16[16,512]{1,0:T(8,128)(2,1)}), bf16[2048,512]{1,0:T(8,128)(2,1)}) %all-gather.3.cloned.1.call-update) | async-done | bytes 2097168 | tf_op jit(solution)/shard_map/all_gather | solution.py:30
  147.6 2.1 %fusion.14 = f32[8,512]{1,0:T(8,128)S(1)} fusion(bf16[2048,512]{1,0:T(8,128)(2,1)} %all-gather.3.cloned.1.call-done, f32[2048,8]{0,1:T(8,128)S(1)} %reshape.96), kind=kOutput, calls=%fused_computation.31 | convolution fusion | flops 16793600 | bytes 2179072 | tf_op jit(solution)/shard_map/dot_general | solution.py:13
  149.7 0.1 copy-done.2
  149.8 0.4 convolution_add_fusion
  150.2 6.6 %all_gather.19 = f32[8,1024]{1,0:T(8,128)S(1)} all-gather(f32[8,512]{1,0:T(8,128)S(1)} %convolution_add_fusion), channel_id=1, replica_groups=mesh['dp'=128,'group'=2] {'group'}, dimensions={1}, use_global_device_ids=true | all-gather | bytes 49152 | tf_op jit(solution)/shard_map/all_gather | solution.py:75
  156.8 0.6 copy.42
  (17 shorter events, 0.1 us)
Async XLA Ops:
  7.2 48.1 %copy-start = (bf16[1024,1024]{1,0:T(8,128)(2,1)S(1)}, bf16[1024,1024]{1,0:T(8,128)(2,1)}, u32[]{:S(2)}) copy-start(bf16[1024,1024]{1,0:T(8,128)(2,1)} %param.7) | copy-start | bytes 6291460
  7.2 32.9 %copy-start.1 = (bf16[256,1024]{1,0:T(8,128)(2,1)S(1)}, bf16[256,1024]{1,0:T(8,128)(2,1)}, u32[]{:S(2)}) copy-start(bf16[256,1024]{1,0:T(8,128)(2,1)} %param.6) | copy-start | bytes 1572868
  12.9 27.1 %all-to-all-start = ((s32[128,1,4]{2,1,0:T(1,128)}), s32[128,1,4]{2,1,0:T(1,128)S(1)}, u32[]{:S(2)}, u32[]{:S(2)}) async-start(s32[128,1,4]{2,1,0:T(1,128)} %bitcast.8), calls=%async_computation | async-start | bytes 131072 | tf_op jit(solution)/shard_map/all_to_all | solution.py:42
  29.2 118.4 %all-gather.3.cloned.1.call-start = ((), (), s32[]{:S(2)}) async-start(), calls=%async_computation.3 | async-start | bytes 2113536 | tf_op jit(solution)/shard_map/all_gather | solution.py:30
  45.2 10.1 %copy-start.3 = (bf16[8,1024]{1,0:T(8,128)(2,1)S(1)}, bf16[8,1024]{1,0:T(8,128)(2,1)}, u32[]{:S(2)}) copy-start(bf16[8,1024]{1,0:T(8,128)(2,1)} %param.5) | copy-start | bytes 49156
  48.0 34.6 %all-to-all-start.1 = ((bf16[128,4,1024]{2,1,0:T(4,128)(2,1)}), bf16[128,4,1024]{2,1,0:T(4,128)(2,1)}, u32[]{:S(2)}, u32[]{:S(2)}) async-start(bf16[128,4,1024]{2,1,0:T(4,128)(2,1)} %broadcast_select_fusion), calls=%async_computation.1 | async-start | bytes 2097152 | tf_op jit(solution)/shard_map/all_to_all | solution.py:44
  147.6 2.2 %copy-start.2 = (bf16[2048,512]{1,0:T(8,128)(2,1)S(1)}, bf16[2048,512]{1,0:T(8,128)(2,1)}, u32[]{:S(2)}) copy-start(bf16[2048,512]{1,0:T(8,128)(2,1)} %all-gather.3.cloned.1.call-done) | copy-start | bytes 6291460
Sparse Core Ops, SparseCore 0:
  34.1 113.4 all-gather.2

commit v4 on v2

--- a/solution.py
+++ b/solution.py
@@ -24,7 +24,6 @@
     capacity = 2 * ref_count // dp_count
     out_rows = out_weight.shape[0] // dp_count
     score_scale = 1.5 / math.sqrt(width)
-    all_queries = lax.all_gather(queries, ("dp", "group"), axis=0, tiled=True)
     owners = neg_owner.reshape(ref_count)
     local_ids = neg_local.reshape(ref_count)
     one_hot = (owners[:, None] == jnp.arange(dp_count, dtype=jnp.int32)[None, :]).astype(jnp.int32)
@@ -37,9 +36,11 @@
         .reshape(dp_count, capacity)
     )
     id_block = lax.all_to_all(requests, "dp", split_axis=0, concat_axis=0, tiled=True)
-    hidden_block = jnp.take(passage_hidden, id_block, axis=0)
+    hidden_block = jnp.take(passage_hidden, id_block, axis=0, mode="clip")
     returned_hidden = lax.all_to_all(hidden_block, "dp", split_axis=0, concat_axis=0, tiled=True)
-    neg_hidden = jnp.take(returned_hidden.reshape(dp_count * capacity, width), position, axis=0)
+    neg_hidden = jnp.take(
+        returned_hidden.reshape(dp_count * capacity, width), position, axis=0, mode="clip"
+    )
     pos_hidden = lax.dynamic_slice_in_dim(passage_hidden, group_pos * query_rows, query_rows, 0)
     neg_keys = jnp.dot(neg_hidden, out_weight, preferred_element_type=jnp.float32).astype(
         jnp.bfloat16
@@ -64,11 +65,14 @@
         neg_coef[:, :, None] * neg_hidden.reshape(query_rows, neg_count, width).astype(jnp.float32),
         axis=1,
     ) + pos_coef[:, None] * pos_hidden.astype(jnp.float32)
-    mixed_cols = mixed.reshape(query_rows, dp_count, out_rows).transpose(1, 0, 2)
-    mixed_cols = lax.all_to_all(mixed_cols, "dp", split_axis=0, concat_axis=0, tiled=True)
-    mixed_cols = lax.all_gather(mixed_cols, "group", axis=0)
-    mixed_cols = mixed_cols.transpose(1, 0, 2, 3).reshape(-1, out_rows)
-    weight_grad = split_dot(mixed_cols, all_queries)
+    col_half = width // 2
+    chip_mixed = lax.all_gather(mixed, "group", axis=0, tiled=True)
+    chip_queries = lax.all_gather(queries, "group", axis=0, tiled=True)
+    half_queries = lax.dynamic_slice_in_dim(chip_queries, group_pos * col_half, col_half, 1)
+    partial = split_dot(chip_mixed, half_queries).reshape(dp_count, out_rows, col_half)
+    partial = lax.all_to_all(partial, "dp", split_axis=0, concat_axis=0, tiled=True)
+    weight_half = jnp.sum(partial, axis=0)
+    weight_grad = lax.all_gather(weight_half, "group", axis=1, tiled=True)
     return (weight_grad, query_loss)
 
 

time: 146 us -> 152 us (1.041)
  blocking collectives: 61.8 us -> 98.1 us
  between operations: 14.2 us -> 0.79 us
  waiting for transfers between devices: 31.1 us -> 22.8 us
  local copies, waits for them, and re-layouts: 18.9 us -> 14.8 us
  matrix products: 5.75 us -> 2.35 us
    all_to_all x1, blocking collectives: 27.7 us -> 56.5 us  [local(): lax.all_to_all(partial, 'dp', split_axis=0, concat_axis=0, tiled=True)]
    all_gather x1 -> x3, blocking collectives: 7.24 us -> 14.8 us  [the longest x1 6.27 us: local(): chip_mixed = lax.all_gather(mixed, 'group', axis=0, tiled=True)]
    all_to_all x1, waiting for transfers between devices: 26.7 us -> 22.8 us  [local(): lax.all_to_all(hidden_block, 'dp', split_axis=0, concat_axis=0, tiled=True)]
    all_gather x1 -> x0, waiting for transfers between devices: 3.73 us -> none  [local(): all_queries = lax.all_gather(queries, ('dp', 'group'), axis=0, tiled=True)]
    reshape x2 -> x0, local copies, waits for them, and re-layouts: 3.04 us -> none  [the longest x1 2.73 us: local(): mixed_cols = mixed_cols.transpose(1, 0, 2, 3).reshape(-1, out_rows)]
    dot_general x1, matrix products: 2.99 us -> 0.45 us  [split_dot(): lax.dot_general(high, right, dims, preferred_element_type=jnp.float32)]
    select_n x2 -> x1, other arithmetic: 2.83 us -> 0.69 us  [local(): requests = jnp.zeros((dp_count * capacity,), jnp.int32).at[position].set(...]
    reduce_sum x0 -> x1, other arithmetic: none -> 1.78 us  [local(): weight_half = jnp.sum(partial, axis=0)]
  transfers between devices with their start and end apart: 2 -> 1, of which waited for: 2 -> 1; matrix products, arithmetic and copies ran while one was open for 18% -> 0% of each run, Pallas kernels for 0% -> 0%
where the time goes in v4:
time: 152 us
  blocking collectives  98.1 us (65%)
  waiting for transfers between devices  22.8 us (15%)
  local copies, waits for them, and re-layouts  14.8 us (10%)
  starting transfers between devices  7.32 us (5%)
  other arithmetic  5.76 us (4%)
  matrix products  2.35 us (2%)
    all_to_all x1, blocking collectives, local(): lax.all_to_all(partial, 'dp', split_axis=0, concat_axis=0, tiled=True)  56.5 us
    all_to_all x1, blocking collectives, local(): lax.all_to_all(requests, 'dp', split_axis=0, concat_axis=0, tiled=True)  26.9 us
    all_to_all x1, waiting for transfers between devices, local(): lax.all_to_all(hidden_block, 'dp', split_axis=0, concat_axis=0, tiled=True)  22.8 us
    all_to_all x1, starting transfers between devices, local(): lax.all_to_all(hidden_block, 'dp', split_axis=0, concat_axis=0, tiled=True)  7.32 us
    all_gather x1, blocking collectives, local(): chip_mixed = lax.all_gather(mixed, 'group', axis=0, tiled=True)  6.27 us
    gather x2, local copies, waits for them, and re-layouts, local(): hidden_block = jnp.take(passage_hidden, id_block, axis=0, mode='clip')  5.08 us
    all_gather x1, blocking collectives, local(): weight_grad = lax.all_gather(weight_half, 'group', axis=1, tiled=True)  4.89 us
    all_gather x1, blocking collectives, local(): chip_queries = lax.all_gather(queries, 'group', axis=0, tiled=True)  3.59 us
  transfers between devices with their start and end apart: 1, of which 1 were waited for; matrix products, arithmetic and copies ran while one was open for 0% of the time, Pallas kernels for 0%

profile of v4, /device:TPU:1, one launch (start us, length us, event | category | flops | bytes accessed | tf_op | source)
XLA Modules:
  0.0 151.9 jit_solution(12315932850322448813)
XLA Ops:
  0.6 0.0 copy-start
  0.6 0.0 copy-start.1
  0.7 0.9 reshape.73
  1.6 0.8 copy.16
  2.4 0.2 fusion.4
  2.7 0.9 fusion.6
  3.5 0.7 compare_select_fusion
  4.2 1.4 scatter_custom_fusion
  5.6 0.1 all_to_all.12
  5.7 26.9 %all_to_all.19 = s32[128,1,4]{2,1,0:T(1,128)S(1)} all-to-all(s32[128,1,4]{2,1,0:T(1,128)S(1)} %bitcast.37), channel_id=1, replica_groups=mesh['dp'=128,'group'=2] {'dp'}, dimensions={0} | all-to-all | bytes 4096 | tf_op jit(solution)/shard_map/all_to_all | solution.py:38
  32.6 0.5 broadcast.60
  33.1 0.8 reduce.7
  33.9 0.1 reshape.55
  34.1 0.0 copy-done.1
  34.1 2.8 %gather_fusion = bf16[512,1024]{1,0:T(8,128)(2,1)} fusion(bf16[256,1024]{1,0:T(8,128)(2,1)S(1)} %copy-done.1, s32[1024]{0:T(1024)S(1)} %pad_clamp_fusion.1), kind=kCustom, calls=%fused_computation | custom fusion | bytes 2099200 | tf_op jit(solution)/shard_map/jit(_take)/gather | solution.py:39
  36.9 0.0 copy-start.2
  36.9 2.3 %reshape.54 = bf16[128,4,1024]{2,1,0:T(4,128)(2,1)} reshape(bf16[512,1024]{1,0:T(8,128)(2,1)} %gather_fusion) | data formatting | bytes 2097152 | tf_op jit(solution)/shard_map/jit(_take)/gather | solution.py:39
  39.1 7.3 %all-to-all-start.1 = ((bf16[128,4,1024]{2,1,0:T(4,128)(2,1)}), bf16[128,4,1024]{2,1,0:T(4,128)(2,1)}, u32[]{:S(2)}, u32[]{:S(2)}) async-start(bf16[128,4,1024]{2,1,0:T(4,128)(2,1)} %reshape.54), calls=%async_computation.1 | async-start | bytes 2097152 | tf_op jit(solution)/shard_map/all_to_all | solution.py:40
  46.5 0.0 copy-done
  46.5 0.0 copy-done.2
  46.5 0.5 fusion.2
  47.0 0.1 copy.19
  47.1 3.6 %all_gather.10 = bf16[16,1024]{1,0:T(8,128)(2,1)S(1)} all-gather(bf16[8,1024]{1,0:T(8,128)(2,1)S(1)} %copy-done.2), channel_id=1, replica_groups=mesh['dp'=128,'group'=2] {'group'}, dimensions={0}, use_global_device_ids=true | all-gather | bytes 49152 | tf_op jit(solution)/shard_map/all_gather | solution.py:70
  50.7 22.8 %all-to-all-done.1 = bf16[128,4,1024]{2,1,0:T(4,128)(2,1)} async-done(((bf16[128,4,1024]{2,1,0:T(4,128)(2,1)}), bf16[128,4,1024]{2,1,0:T(4,128)(2,1)}, u32[]{:S(2)}, u32[]{:S(2)}) %all-to-all-start.1) | async-done | bytes 1048608 | tf_op jit(solution)/shard_map/all_to_all | solution.py:40
  73.4 2.2 %reshape.49 = bf16[512,1024]{1,0:T(8,128)(2,1)} reshape(bf16[128,4,1024]{2,1,0:T(4,128)(2,1)} %all-to-all-done.1) | data formatting | bytes 2097152 | tf_op jit(solution)/shard_map/reshape | solution.py:42
  75.6 2.9 %gather_fusion.1 = bf16[256,1024]{1,0:T(8,128)(2,1)S(1)} fusion(bf16[512,1024]{1,0:T(8,128)(2,1)} %reshape.49, s32[1024]{0:T(1024)S(1)} %pad_clamp_fusion), kind=kCustom, calls=%fused_computation.1 | custom fusion | bytes 1049600 | tf_op jit(solution)/shard_map/jit(_take)/gather | solution.py:41
  78.6 0.7 convolution_convert_fusion
  79.3 0.2 fusion.9
  79.5 0.2 exponential_reduce_fusion
  79.7 0.5 multiply_subtract_fusion
  80.3 0.1 subtract_exponential_fusion
  80.3 0.1 multiply_reduce_fusion
  80.5 0.1 slice_multiply_fusion
  80.5 0.3 fusion.3
  80.8 0.1 multiply_add_fusion
  80.9 6.3 %all_gather.9 = f32[16,1024]{1,0:T(8,128)S(1)} all-gather(f32[8,1024]{1,0:T(8,128)S(1)} %multiply_add_fusion), channel_id=1, replica_groups=mesh['dp'=128,'group'=2] {'group'}, dimensions={0}, use_global_device_ids=true | all-gather | bytes 98304 | tf_op jit(solution)/shard_map/all_gather | solution.py:69
  87.2 0.4 fusion.12
  87.6 0.5 add_bitcast_fusion
  88.1 56.5 %all_to_all.20 = f32[128,8,512]{2,1,0:T(8,128)} all-to-all(f32[128,8,512]{2,1,0:T(8,128)S(1)} %add_bitcast_fusion), channel_id=1, replica_groups=mesh['dp'=128,'group'=2] {'dp'}, dimensions={0} | all-to-all | bytes 4194304 | tf_op jit(solution)/shard_map/all_to_all | solution.py:73
  144.6 1.8 %reduce_sum.42 = f32[8,512]{1,0:T(8,128)S(1)} reduce(f32[128,8,512]{2,1,0:T(8,128)} %all_to_all.20, f32[]{:T(128)} %constant.6.clone.1), dimensions={0}, to_apply=%region_6.7 | reduce | flops 520192 | bytes 2113540 | tf_op jit(solution)/shard_map/reduce_sum | solution.py:74
  146.3 4.9 %all_gather.11 = f32[8,1024]{1,0:T(8,128)S(1)} all-gather(f32[8,512]{1,0:T(8,128)S(1)} %reduce_sum.42), channel_id=1, replica_groups=mesh['dp'=128,'group'=2] {'group'}, dimensions={1}, use_global_device_ids=true | all-gather | bytes 49152 | tf_op jit(solution)/shard_map/all_gather | solution.py:75
  151.2 0.6 copy.30
  (10 shorter events, 0.1 us)
Async XLA Ops:
  0.6 45.8 %copy-start = (bf16[1024,1024]{1,0:T(8,128)(2,1)S(1)}, bf16[1024,1024]{1,0:T(8,128)(2,1)}, u32[]{:S(2)}) copy-start(bf16[1024,1024]{1,0:T(8,128)(2,1)} %param.7) | copy-start | bytes 6291460
  0.6 33.4 %copy-start.1 = (bf16[256,1024]{1,0:T(8,128)(2,1)S(1)}, bf16[256,1024]{1,0:T(8,128)(2,1)}, u32[]{:S(2)}) copy-start(bf16[256,1024]{1,0:T(8,128)(2,1)} %param.6) | copy-start | bytes 1572868
  36.9 9.6 %copy-start.2 = (bf16[8,1024]{1,0:T(8,128)(2,1)S(1)}, bf16[8,1024]{1,0:T(8,128)(2,1)}, u32[]{:S(2)}) copy-start(bf16[8,1024]{1,0:T(8,128)(2,1)} %param.5) | copy-start | bytes 49156
  39.1 34.3 %all-to-all-start.1 = ((bf16[128,4,1024]{2,1,0:T(4,128)(2,1)}), bf16[128,4,1024]{2,1,0:T(4,128)(2,1)}, u32[]{:S(2)}, u32[]{:S(2)}) async-start(bf16[128,4,1024]{2,1,0:T(4,128)(2,1)} %reshape.54), calls=%async_computation.1 | async-start | bytes 2097152 | tf_op jit(solution)/shard_map/all_to_all | solution.py:40

commit v5 on v4

--- a/solution.py
+++ b/solution.py
@@ -69,9 +69,10 @@
     chip_mixed = lax.all_gather(mixed, "group", axis=0, tiled=True)
     chip_queries = lax.all_gather(queries, "group", axis=0, tiled=True)
     half_queries = lax.dynamic_slice_in_dim(chip_queries, group_pos * col_half, col_half, 1)
-    partial = split_dot(chip_mixed, half_queries).reshape(dp_count, out_rows, col_half)
+    partial = split_dot(chip_mixed, half_queries).astype(jnp.bfloat16)
+    partial = partial.reshape(dp_count, out_rows, col_half)
     partial = lax.all_to_all(partial, "dp", split_axis=0, concat_axis=0, tiled=True)
-    weight_half = jnp.sum(partial, axis=0)
+    weight_half = jnp.sum(partial.astype(jnp.float32), axis=0)
     weight_grad = lax.all_gather(weight_half, "group", axis=1, tiled=True)
     return (weight_grad, query_loss)
 

time: 152 us -> 129 us (0.85)
  blocking collectives: 98.1 us -> 76 us
  other arithmetic: 5.76 us -> 4.18 us
    all_to_all x1, blocking collectives: 56.5 us -> 34.7 us  [local(): lax.all_to_all(partial, 'dp', split_axis=0, concat_axis=0, tiled=True)]
    reduce_sum x1, other arithmetic: 1.78 us -> 0.19 us  [local(): weight_half = jnp.sum(partial.astype(jnp.float32), axis=0)]
where the time goes in v5:
time: 129 us; the launch traced here: 128 us
  blocking collectives  76 us (59%)
  waiting for transfers between devices  22.8 us (18%)
  local copies, waits for them, and re-layouts  14.7 us (11%)
  starting transfers between devices  7.32 us (6%)
  other arithmetic  4.18 us (3%)
  matrix products  2.35 us (2%)
    all_to_all x1, blocking collectives, local(): lax.all_to_all(partial, 'dp', split_axis=0, concat_axis=0, tiled=True)  34.7 us
    all_to_all x1, blocking collectives, local(): lax.all_to_all(requests, 'dp', split_axis=0, concat_axis=0, tiled=True)  26.9 us
    all_to_all x1, waiting for transfers between devices, local(): lax.all_to_all(hidden_block, 'dp', split_axis=0, concat_axis=0, tiled=True)  22.8 us
    all_to_all x1, starting transfers between devices, local(): lax.all_to_all(hidden_block, 'dp', split_axis=0, concat_axis=0, tiled=True)  7.32 us
    all_gather x1, blocking collectives, local(): chip_mixed = lax.all_gather(mixed, 'group', axis=0, tiled=True)  6.27 us
    gather x2, local copies, waits for them, and re-layouts, local(): hidden_block = jnp.take(passage_hidden, id_block, axis=0, mode='clip')  5.08 us
    all_gather x1, blocking collectives, local(): weight_grad = lax.all_gather(weight_half, 'group', axis=1, tiled=True)  4.56 us
    all_gather x1, blocking collectives, local(): chip_queries = lax.all_gather(queries, 'group', axis=0, tiled=True)  3.59 us
  transfers between devices with their start and end apart: 1, of which 1 were waited for; matrix products, arithmetic and copies ran while one was open for 0% of the time, Pallas kernels for 0%

profile of v5, /device:TPU:1, one launch (start us, length us, event | category | flops | bytes accessed | tf_op | source)
XLA Modules:
  0.0 128.1 jit_solution(2554820275864923331)
XLA Ops:
  0.6 0.0 copy-start
  0.6 0.0 copy-start.1
  0.7 0.9 reshape.73
  1.6 0.8 copy.16
  2.4 0.2 fusion.5
  2.7 0.9 fusion.7
  3.5 0.7 compare_select_fusion
  4.2 1.4 %scatter_custom_fusion = s32[512]{0:T(512)S(1)} fusion(s32[256]{0:T(256)S(1)} %bitcast.45, s32[256]{0:T(256)S(1)} %reshape.73, s32[]{:T(128)} %constant.12.clone.1), kind=kCustom, calls=%fused_computation.43 | custom fusion | bytes 2052 | tf_op jit(solution)/shard_map/scatter | solution.py:35
  5.6 0.1 all_to_all.12
  5.7 26.9 %all_to_all.19 = s32[128,1,4]{2,1,0:T(1,128)S(1)} all-to-all(s32[128,1,4]{2,1,0:T(1,128)S(1)} %bitcast.37), channel_id=1, replica_groups=mesh['dp'=128,'group'=2] {'dp'}, dimensions={0} | all-to-all | bytes 4096 | tf_op jit(solution)/shard_map/all_to_all | solution.py:38
  32.6 0.5 broadcast.60
  33.1 0.8 reduce.7
  33.9 0.1 reshape.55
  34.1 0.0 copy-done.1
  34.1 2.8 %gather_fusion = bf16[512,1024]{1,0:T(8,128)(2,1)} fusion(bf16[256,1024]{1,0:T(8,128)(2,1)S(1)} %copy-done.1, s32[1024]{0:T(1024)S(1)} %pad_clamp_fusion.1), kind=kCustom, calls=%fused_computation | custom fusion | bytes 2099200 | tf_op jit(solution)/shard_map/jit(_take)/gather | solution.py:39
  36.9 0.0 copy-start.2
  36.9 2.3 %reshape.54 = bf16[128,4,1024]{2,1,0:T(4,128)(2,1)} reshape(bf16[512,1024]{1,0:T(8,128)(2,1)} %gather_fusion) | data formatting | bytes 2097152 | tf_op jit(solution)/shard_map/jit(_take)/gather | solution.py:39
  39.1 7.3 %all-to-all-start.1 = ((bf16[128,4,1024]{2,1,0:T(4,128)(2,1)}), bf16[128,4,1024]{2,1,0:T(4,128)(2,1)}, u32[]{:S(2)}, u32[]{:S(2)}) async-start(bf16[128,4,1024]{2,1,0:T(4,128)(2,1)} %reshape.54), calls=%async_computation.1 | async-start | bytes 2097152 | tf_op jit(solution)/shard_map/all_to_all | solution.py:40
  46.5 0.0 copy-done
  46.5 0.0 copy-done.2
  46.5 0.5 fusion.3
  47.0 0.1 copy.19
  47.1 3.6 %all_gather.10 = bf16[16,1024]{1,0:T(8,128)(2,1)S(1)} all-gather(bf16[8,1024]{1,0:T(8,128)(2,1)S(1)} %copy-done.2), channel_id=1, replica_groups=mesh['dp'=128,'group'=2] {'group'}, dimensions={0}, use_global_device_ids=true | all-gather | bytes 49152 | tf_op jit(solution)/shard_map/all_gather | solution.py:70
  50.7 22.8 %all-to-all-done.1 = bf16[128,4,1024]{2,1,0:T(4,128)(2,1)} async-done(((bf16[128,4,1024]{2,1,0:T(4,128)(2,1)}), bf16[128,4,1024]{2,1,0:T(4,128)(2,1)}, u32[]{:S(2)}, u32[]{:S(2)}) %all-to-all-start.1) | async-done | bytes 1048608 | tf_op jit(solution)/shard_map/all_to_all | solution.py:40
  73.4 2.2 %reshape.49 = bf16[512,1024]{1,0:T(8,128)(2,1)} reshape(bf16[128,4,1024]{2,1,0:T(4,128)(2,1)} %all-to-all-done.1) | data formatting | bytes 2097152 | tf_op jit(solution)/shard_map/reshape | solution.py:42
  75.6 2.9 %gather_fusion.1 = bf16[256,1024]{1,0:T(8,128)(2,1)S(1)} fusion(bf16[512,1024]{1,0:T(8,128)(2,1)} %reshape.49, s32[1024]{0:T(1024)S(1)} %pad_clamp_fusion), kind=kCustom, calls=%fused_computation.1 | custom fusion | bytes 1049600 | tf_op jit(solution)/shard_map/jit(_take)/gather | solution.py:41
  78.6 0.7 convolution_convert_fusion
  79.3 0.2 fusion.10
  79.5 0.2 exponential_reduce_fusion
  79.7 0.5 multiply_subtract_fusion
  80.3 0.1 subtract_exponential_fusion
  80.3 0.1 multiply_reduce_fusion
  80.5 0.1 slice_multiply_fusion
  80.5 0.3 fusion.4
  80.8 0.1 multiply_add_fusion
  80.9 6.3 %all_gather.9 = f32[16,1024]{1,0:T(8,128)S(1)} all-gather(f32[8,1024]{1,0:T(8,128)S(1)} %multiply_add_fusion), channel_id=1, replica_groups=mesh['dp'=128,'group'=2] {'group'}, dimensions={0}, use_global_device_ids=true | all-gather | bytes 98304 | tf_op jit(solution)/shard_map/all_gather | solution.py:69
  87.2 0.4 fusion.13
  87.6 0.5 fusion
  88.1 34.7 %all_to_all.20 = bf16[128,8,512]{2,1,0:T(8,128)(2,1)S(1)} all-to-all(bf16[128,8,512]{2,1,0:T(8,128)(2,1)S(1)} %fusion), channel_id=1, replica_groups=mesh['dp'=128,'group'=2] {'dp'}, dimensions={0} | all-to-all | bytes 2097152 | tf_op jit(solution)/shard_map/all_to_all | solution.py:74
  122.7 0.2 convert_reduce_fusion
  122.9 4.6 %all_gather.11 = f32[8,1024]{1,0:T(8,128)S(1)} all-gather(f32[8,512]{1,0:T(8,128)S(1)} %convert_reduce_fusion), channel_id=1, replica_groups=mesh['dp'=128,'group'=2] {'group'}, dimensions={1}, use_global_device_ids=true | all-gather | bytes 49152 | tf_op jit(solution)/shard_map/all_gather | solution.py:76
  127.5 0.6 copy.30
  (10 shorter events, 0.1 us)
Async XLA Ops:
  0.6 45.8 %copy-start = (bf16[1024,1024]{1,0:T(8,128)(2,1)S(1)}, bf16[1024,1024]{1,0:T(8,128)(2,1)}, u32[]{:S(2)}) copy-start(bf16[1024,1024]{1,0:T(8,128)(2,1)} %param.7) | copy-start | bytes 6291460
  0.6 33.4 %copy-start.1 = (bf16[256,1024]{1,0:T(8,128)(2,1)S(1)}, bf16[256,1024]{1,0:T(8,128)(2,1)}, u32[]{:S(2)}) copy-start(bf16[256,1024]{1,0:T(8,128)(2,1)} %param.6) | copy-start | bytes 1572868
  36.9 9.6 %copy-start.2 = (bf16[8,1024]{1,0:T(8,128)(2,1)S(1)}, bf16[8,1024]{1,0:T(8,128)(2,1)}, u32[]{:S(2)}) copy-start(bf16[8,1024]{1,0:T(8,128)(2,1)} %param.5) | copy-start | bytes 49156
  39.1 34.3 %all-to-all-start.1 = ((bf16[128,4,1024]{2,1,0:T(4,128)(2,1)}), bf16[128,4,1024]{2,1,0:T(4,128)(2,1)}, u32[]{:S(2)}, u32[]{:S(2)}) async-start(bf16[128,4,1024]{2,1,0:T(4,128)(2,1)} %reshape.54), calls=%async_computation.1 | async-start | bytes 2097152 | tf_op jit(solution)/shard_map/all_to_all | solution.py:40

commit v6 on v5

--- a/solution.py
+++ b/solution.py
@@ -19,6 +19,7 @@
     dp_count = lax.axis_size("dp")
     group_pos = lax.axis_index("group")
     query_rows, width = queries.shape
+    passage_rows = passage_hidden.shape[0]
     neg_count = neg_local.shape[1]
     ref_count = query_rows * neg_count
     capacity = 2 * ref_count // dp_count
@@ -36,11 +37,20 @@
         .reshape(dp_count, capacity)
     )
     id_block = lax.all_to_all(requests, "dp", split_axis=0, concat_axis=0, tiled=True)
-    hidden_block = jnp.take(passage_hidden, id_block, axis=0, mode="clip")
+    pick_send = (
+        id_block[:, :, None] == jnp.arange(passage_rows, dtype=jnp.int32)[None, None, :]
+    ).astype(jnp.bfloat16)
+    hidden_block = jnp.einsum(
+        "kcp,pd->kcd", pick_send, passage_hidden, preferred_element_type=jnp.float32
+    ).astype(jnp.bfloat16)
     returned_hidden = lax.all_to_all(hidden_block, "dp", split_axis=0, concat_axis=0, tiled=True)
-    neg_hidden = jnp.take(
-        returned_hidden.reshape(dp_count * capacity, width), position, axis=0, mode="clip"
-    )
+    pick_back = (
+        position[:, None, None]
+        == (jnp.arange(dp_count * capacity, dtype=jnp.int32).reshape(1, dp_count, capacity))
+    ).astype(jnp.bfloat16)
+    neg_hidden = jnp.einsum(
+        "rkc,kcd->rd", pick_back, returned_hidden, preferred_element_type=jnp.float32
+    ).astype(jnp.bfloat16)
     pos_hidden = lax.dynamic_slice_in_dim(passage_hidden, group_pos * query_rows, query_rows, 0)
     neg_keys = jnp.dot(neg_hidden, out_weight, preferred_element_type=jnp.float32).astype(
         jnp.bfloat16

time: 129 us -> 121 us (0.938)
  local copies, waits for them, and re-layouts: 14.7 us -> 5.79 us
  matrix products: 2.35 us -> 5.5 us
    gather x3 -> x0, local copies, waits for them, and re-layouts: 7.99 us -> none  [the longest x2 5.08 us: local(): hidden_block = jnp.take(passage_hidden, id_block, axis=0, mode='clip')]
    dot_general x0 -> x2, matrix products: none -> 2.42 us  [the longest x1 1.55 us: local(): jnp.einsum('kcp,pd->kcd', pick_send, passage_hidden, preferred_element_ty...]
    reshape x1 -> x0, local copies, waits for them, and re-layouts: 2.2 us -> none  [local(): returned_hidden.reshape(dp_count * capacity, width)]
    convert_element_type x0 -> x1, local copies, waits for them, and re-layouts: none -> 1.8 us  [local(): hidden_block = jnp.einsum('kcp,pd->kcd', pick_send, passage_hidden, prefe...]
  transfers between devices with their start and end apart: 1 -> 1, of which waited for: 1 -> 1; matrix products, arithmetic and copies ran while one was open for 0% -> 1% of each run, Pallas kernels for 0% -> 0%
where the time goes in v6:
time: 121 us
  blocking collectives  76 us (63%)
  waiting for transfers between devices  22.5 us (19%)
  starting transfers between devices  6.32 us (5%)
  local copies, waits for them, and re-layouts  5.79 us (5%)
  matrix products  5.5 us (5%)
  other arithmetic  4.09 us (3%)
    all_to_all x1, blocking collectives, local(): lax.all_to_all(partial, 'dp', split_axis=0, concat_axis=0, tiled=True)  34.7 us
    all_to_all x1, blocking collectives, local(): lax.all_to_all(requests, 'dp', split_axis=0, concat_axis=0, tiled=True)  26.9 us
    all_to_all x1, waiting for transfers between devices, local(): lax.all_to_all(hidden_block, 'dp', split_axis=0, concat_axis=0, tiled=True)  22.5 us
    all_to_all x1, starting transfers between devices, local(): lax.all_to_all(hidden_block, 'dp', split_axis=0, concat_axis=0, tiled=True)  6.32 us
    all_gather x1, blocking collectives, local(): chip_mixed = lax.all_gather(mixed, 'group', axis=0, tiled=True)  6.27 us
    all_gather x1, blocking collectives, local(): weight_grad = lax.all_gather(weight_half, 'group', axis=1, tiled=True)  4.54 us
    all_gather x1, blocking collectives, local(): chip_queries = lax.all_gather(queries, 'group', axis=0, tiled=True)  3.59 us
  transfers between devices with their start and end apart: 1, of which 1 were waited for; matrix products, arithmetic and copies ran while one was open for 1% of the time, Pallas kernels for 0%

profile of v6, /device:TPU:1, one launch (start us, length us, event | category | flops | bytes accessed | tf_op | source)
XLA Modules:
  0.0 120.9 jit_solution(1378757857400612301)
XLA Ops:
  0.6 0.0 copy-start
  0.6 0.9 reshape.84
  1.6 0.8 copy.19
  2.3 0.2 fusion.12
  2.6 0.9 fusion.14
  3.5 0.7 compare_select_fusion
  4.2 1.4 %scatter_custom_fusion = s32[512]{0:T(512)S(1)} fusion(s32[256]{0:T(256)S(1)} %bitcast.53, s32[256]{0:T(256)S(1)} %reshape.84, s32[]{:T(128)} %constant.12.clone.1), kind=kCustom, calls=%fused_computation.49 | custom fusion | bytes 2052 | tf_op jit(solution)/shard_map/scatter | solution.py:36
  5.6 0.1 all_to_all.12
  5.7 26.9 %all_to_all.19 = s32[128,1,4]{2,1,0:T(1,128)S(1)} all-to-all(s32[128,1,4]{2,1,0:T(1,128)S(1)} %bitcast.44), channel_id=1, replica_groups=mesh['dp'=128,'group'=2] {'dp'}, dimensions={0} | all-to-all | bytes 4096 | tf_op jit(solution)/shard_map/all_to_all | solution.py:39
  32.6 0.1 copy.22
  32.7 1.5 %convolution_convert_fusion = bf16[128,4,1024]{2,0,1:T(8,128)(2,1)S(1)} fusion(bf16[256,1024]{1,0:T(8,128)(2,1)} %param.6, s32[128,4]{0,1:T(4,128)S(1)} %copy.22), kind=kOutput, calls=%fused_computation.3 | convolution fusion | flops 269090816 | bytes 1574912 | tf_op jit(solution)/shard_map/kcp,pd->kcd/dot_general | solution.py:43
  34.2 0.0 copy-start.1
  34.2 1.8 %copy.23 = bf16[128,4,1024]{2,1,0:T(4,128)(2,1)} copy(bf16[128,4,1024]{2,0,1:T(8,128)(2,1)S(1)} %convolution_convert_fusion) | data formatting | bytes 2097152 | tf_op jit(solution)/shard_map/convert_element_type | solution.py:45
  36.0 0.0 copy-start.2
  36.0 6.3 %all-to-all-start.1 = ((bf16[128,4,1024]{2,1,0:T(4,128)(2,1)}), bf16[128,4,1024]{2,1,0:T(4,128)(2,1)S(1)}, u32[]{:S(2)}, u32[]{:S(2)}) async-start(bf16[128,4,1024]{2,1,0:T(4,128)(2,1)} %copy.23), calls=%async_computation.1 | async-start | bytes 2097152 | tf_op jit(solution)/shard_map/all_to_all | solution.py:46
  42.4 0.0 copy-done
  42.4 0.0 copy-done.1
  42.4 1.2 %fusion.4 = f32[8]{0:T(128)S(1)} fusion(bf16[1024,1024]{1,0:T(8,128)(2,1)S(1)} %copy-done, bf16[8,1024]{1,0:T(8,128)(2,1)S(1)} %copy-done.1, bf16[256,1024]{1,0:T(8,128)(2,1)} %param.6, s32[]{:T(128)S(6)} %select_n.10), kind=kOutput, calls=%fused_computation.11 | convolution fusion | flops 16818168 | bytes 2129956 | tf_op jit(solution)/shard_map/dot_general | solution.py:58
  43.6 0.1 copy.25
  43.7 3.6 %all_gather.10 = bf16[16,1024]{1,0:T(8,128)(2,1)S(1)} all-gather(bf16[8,1024]{1,0:T(8,128)(2,1)S(1)} %copy-done.1), channel_id=1, replica_groups=mesh['dp'=128,'group'=2] {'group'}, dimensions={0}, use_global_device_ids=true | all-gather | bytes 49152 | tf_op jit(solution)/shard_map/all_gather | solution.py:80
  47.3 0.0 copy-done.2
  47.3 22.5 %all-to-all-done.1 = bf16[128,4,1024]{2,1,0:T(4,128)(2,1)S(1)} async-done(((bf16[128,4,1024]{2,1,0:T(4,128)(2,1)}), bf16[128,4,1024]{2,1,0:T(4,128)(2,1)S(1)}, u32[]{:S(2)}, u32[]{:S(2)}) %all-to-all-start.1) | async-done | bytes 1048608 | tf_op jit(solution)/shard_map/all_to_all | solution.py:46
  69.7 0.9 fusion.1
  70.6 0.7 convolution_convert_fusion.1
  71.3 0.2 fusion.17
  71.6 0.2 exponential_reduce_fusion
  71.8 0.5 multiply_subtract_fusion
  72.3 0.1 subtract_exponential_fusion
  72.4 0.1 multiply_reduce_fusion
  72.5 0.1 slice_multiply_fusion
  72.6 0.3 fusion.5
  72.9 0.8 multiply_add_fusion
  73.7 6.3 %all_gather.9 = f32[16,1024]{1,0:T(8,128)S(1)} all-gather(f32[8,1024]{1,0:T(8,128)S(1)} %multiply_add_fusion), channel_id=1, replica_groups=mesh['dp'=128,'group'=2] {'group'}, dimensions={0}, use_global_device_ids=true | all-gather | bytes 98304 | tf_op jit(solution)/shard_map/all_gather | solution.py:79
  79.9 0.5 fusion.20
  80.4 0.5 fusion
  80.9 34.7 %all_to_all.20 = bf16[128,8,512]{2,1,0:T(8,128)(2,1)S(1)} all-to-all(bf16[128,8,512]{2,1,0:T(8,128)(2,1)S(1)} %fusion), channel_id=1, replica_groups=mesh['dp'=128,'group'=2] {'dp'}, dimensions={0} | all-to-all | bytes 2097152 | tf_op jit(solution)/shard_map/all_to_all | solution.py:84
  115.6 0.2 convert_reduce_fusion
  115.8 4.5 %all_gather.11 = f32[8,1024]{1,0:T(8,128)S(1)} all-gather(f32[8,512]{1,0:T(8,128)S(1)} %convert_reduce_fusion), channel_id=1, replica_groups=mesh['dp'=128,'group'=2] {'group'}, dimensions={1}, use_global_device_ids=true | all-gather | bytes 49152 | tf_op jit(solution)/shard_map/all_gather | solution.py:86
  120.3 0.6 copy.38
  (10 shorter events, 0.1 us)
Async XLA Ops:
  0.6 41.7 %copy-start = (bf16[1024,1024]{1,0:T(8,128)(2,1)S(1)}, bf16[1024,1024]{1,0:T(8,128)(2,1)}, u32[]{:S(2)}) copy-start(bf16[1024,1024]{1,0:T(8,128)(2,1)} %param.7) | copy-start | bytes 6291460
  34.2 8.2 %copy-start.1 = (bf16[8,1024]{1,0:T(8,128)(2,1)S(1)}, bf16[8,1024]{1,0:T(8,128)(2,1)}, u32[]{:S(2)}) copy-start(bf16[8,1024]{1,0:T(8,128)(2,1)} %param.5) | copy-start | bytes 49156
  36.0 11.3 %copy-start.2 = (s32[256,1]{0,1:T(1,128)S(1)}, s32[256,1]{0,1:T(1,128)}, u32[]{:S(2)}) copy-start(s32[256,1]{0,1:T(1,128)} %param.8) | copy-start | bytes 3076
  36.0 33.7 %all-to-all-start.1 = ((bf16[128,4,1024]{2,1,0:T(4,128)(2,1)}), bf16[128,4,1024]{2,1,0:T(4,128)(2,1)S(1)}, u32[]{:S(2)}, u32[]{:S(2)}) async-start(bf16[128,4,1024]{2,1,0:T(4,128)(2,1)} %copy.23), calls=%async_computation.1 | async-start | bytes 2097152 | tf_op jit(solution)/shard_map/all_to_all | solution.py:46

commit v7 on v6

--- a/solution.py
+++ b/solution.py
@@ -27,13 +27,16 @@
     score_scale = 1.5 / math.sqrt(width)
     owners = neg_owner.reshape(ref_count)
     local_ids = neg_local.reshape(ref_count)
-    one_hot = (owners[:, None] == jnp.arange(dp_count, dtype=jnp.int32)[None, :]).astype(jnp.int32)
-    slot_rank = jnp.sum((jnp.cumsum(one_hot, axis=0) - one_hot) * one_hot, axis=1)
+    ref_index = jnp.arange(ref_count, dtype=jnp.int32)
+    same_owner = (owners[:, None] == owners[None, :]) & (ref_index[:, None] > ref_index[None, :])
+    slot_rank = jnp.sum(same_owner.astype(jnp.int32), axis=1)
     position = owners * capacity + slot_rank
+    place = (
+        position[:, None] == jnp.arange(dp_count * capacity, dtype=jnp.int32)[None, :]
+    ).astype(jnp.bfloat16)
     requests = (
-        jnp.zeros((dp_count * capacity,), jnp.int32)
-        .at[position]
-        .set(local_ids)
+        jnp.dot(local_ids.astype(jnp.bfloat16), place, preferred_element_type=jnp.float32)
+        .astype(jnp.int32)
         .reshape(dp_count, capacity)
     )
     id_block = lax.all_to_all(requests, "dp", split_axis=0, concat_axis=0, tiled=True)

time: 121 us -> 119 us (0.983)
  local copies, waits for them, and re-layouts: 5.79 us -> 2.77 us
    scatter x1 -> x0, local copies, waits for them, and re-layouts: 1.39 us -> none  [local(): requests = jnp.zeros((dp_count * capacity,), jnp.int32).at[position].set(...]
where the time goes in v7:
time: 119 us
  blocking collectives  76 us (64%)
  waiting for transfers between devices  22.5 us (19%)
  starting transfers between devices  6.32 us (5%)
  matrix products  5.74 us (5%)
  other arithmetic  4.69 us (4%)
  local copies, waits for them, and re-layouts  2.77 us (2%)
    all_to_all x1, blocking collectives, local(): lax.all_to_all(partial, 'dp', split_axis=0, concat_axis=0, tiled=True)  34.7 us
    all_to_all x1, blocking collectives, local(): lax.all_to_all(requests, 'dp', split_axis=0, concat_axis=0, tiled=True)  26.9 us
    all_to_all x1, waiting for transfers between devices, local(): lax.all_to_all(hidden_block, 'dp', split_axis=0, concat_axis=0, tiled=True)  22.5 us
    all_to_all x1, starting transfers between devices, local(): lax.all_to_all(hidden_block, 'dp', split_axis=0, concat_axis=0, tiled=True)  6.32 us
    all_gather x1, blocking collectives, local(): chip_mixed = lax.all_gather(mixed, 'group', axis=0, tiled=True)  6.27 us
    all_gather x1, blocking collectives, local(): weight_grad = lax.all_gather(weight_half, 'group', axis=1, tiled=True)  4.56 us
    all_gather x1, blocking collectives, local(): chip_queries = lax.all_gather(queries, 'group', axis=0, tiled=True)  3.59 us
  transfers between devices with their start and end apart: 1, of which 1 were waited for; matrix products, arithmetic and copies ran while one was open for 1% of the time, Pallas kernels for 0%

profile of v7, /device:TPU:1, one launch (start us, length us, event | category | flops | bytes accessed | tf_op | source)
XLA Modules:
  0.0 118.7 jit_solution(9900280204001929719)
XLA Ops:
  0.6 0.0 copy-start
  0.6 1.0 convert_reduce_fusion.1
  1.7 0.7 multiply_add_fusion.2
  2.4 0.7 convert_element_type.53
  3.0 0.1 reshape.65
  3.1 0.3 fusion.9
  3.4 0.1 all_to_all.12
  3.5 26.9 %all_to_all.19 = s32[128,1,4]{2,1,0:T(1,128)S(1)} all-to-all(s32[128,1,4]{2,1,0:T(1,128)S(1)} %bitcast.29), channel_id=1, replica_groups=mesh['dp'=128,'group'=2] {'dp'}, dimensions={0} | all-to-all | bytes 4096 | tf_op jit(solution)/shard_map/all_to_all | solution.py:42
  30.4 0.1 copy.20
  30.5 1.5 %convolution_convert_fusion = bf16[128,4,1024]{2,0,1:T(8,128)(2,1)S(1)} fusion(bf16[256,1024]{1,0:T(8,128)(2,1)} %param.6, s32[128,4]{0,1:T(4,128)S(1)} %copy.20), kind=kOutput, calls=%fused_computation.2 | convolution fusion | flops 269090816 | bytes 1574912 | tf_op jit(solution)/shard_map/kcp,pd->kcd/dot_general | solution.py:46
  32.0 0.0 copy-start.1
  32.0 1.8 %copy.21 = bf16[128,4,1024]{2,1,0:T(4,128)(2,1)} copy(bf16[128,4,1024]{2,0,1:T(8,128)(2,1)S(1)} %convolution_convert_fusion) | data formatting | bytes 2097152 | tf_op jit(solution)/shard_map/convert_element_type | solution.py:48
  33.8 0.0 copy-start.2
  33.8 6.3 %all-to-all-start.1 = ((bf16[128,4,1024]{2,1,0:T(4,128)(2,1)}), bf16[128,4,1024]{2,1,0:T(4,128)(2,1)S(1)}, u32[]{:S(2)}, u32[]{:S(2)}) async-start(bf16[128,4,1024]{2,1,0:T(4,128)(2,1)} %copy.21), calls=%async_computation.1 | async-start | bytes 2097152 | tf_op jit(solution)/shard_map/all_to_all | solution.py:49
  40.2 0.0 copy-done
  40.2 0.0 copy-done.1
  40.2 1.2 %fusion.4 = f32[8]{0:T(128)S(1)} fusion(bf16[1024,1024]{1,0:T(8,128)(2,1)S(1)} %copy-done, bf16[8,1024]{1,0:T(8,128)(2,1)S(1)} %copy-done.1, bf16[256,1024]{1,0:T(8,128)(2,1)} %param.6, s32[]{:T(128)S(6)} %select_n.6), kind=kOutput, calls=%fused_computation.10 | convolution fusion | flops 16818168 | bytes 2129956 | tf_op jit(solution)/shard_map/dot_general | solution.py:61
  41.4 0.1 copy.23
  41.5 3.6 %all_gather.10 = bf16[16,1024]{1,0:T(8,128)(2,1)S(1)} all-gather(bf16[8,1024]{1,0:T(8,128)(2,1)S(1)} %copy-done.1), channel_id=1, replica_groups=mesh['dp'=128,'group'=2] {'group'}, dimensions={0}, use_global_device_ids=true | all-gather | bytes 49152 | tf_op jit(solution)/shard_map/all_gather | solution.py:83
  45.1 0.0 copy-done.2
  45.1 22.5 %all-to-all-done.1 = bf16[128,4,1024]{2,1,0:T(4,128)(2,1)S(1)} async-done(((bf16[128,4,1024]{2,1,0:T(4,128)(2,1)}), bf16[128,4,1024]{2,1,0:T(4,128)(2,1)S(1)}, u32[]{:S(2)}, u32[]{:S(2)}) %all-to-all-start.1) | async-done | bytes 1048608 | tf_op jit(solution)/shard_map/all_to_all | solution.py:49
  67.6 0.9 fusion.1
  68.4 0.7 convolution_convert_fusion.1
  69.2 0.2 fusion.15
  69.4 0.2 exponential_reduce_fusion
  69.6 0.5 multiply_subtract_fusion
  70.1 0.1 subtract_exponential_fusion
  70.2 0.1 multiply_reduce_fusion
  70.3 0.1 slice_multiply_fusion
  70.4 0.3 fusion.5
  70.7 0.8 multiply_add_fusion
  71.5 6.3 %all_gather.9 = f32[16,1024]{1,0:T(8,128)S(1)} all-gather(f32[8,1024]{1,0:T(8,128)S(1)} %multiply_add_fusion), channel_id=1, replica_groups=mesh['dp'=128,'group'=2] {'group'}, dimensions={0}, use_global_device_ids=true | all-gather | bytes 98304 | tf_op jit(solution)/shard_map/all_gather | solution.py:82
  77.8 0.4 fusion.18
  78.2 0.5 fusion
  78.7 34.7 %all_to_all.20 = bf16[128,8,512]{2,1,0:T(8,128)(2,1)S(1)} all-to-all(bf16[128,8,512]{2,1,0:T(8,128)(2,1)S(1)} %fusion), channel_id=1, replica_groups=mesh['dp'=128,'group'=2] {'dp'}, dimensions={0} | all-to-all | bytes 2097152 | tf_op jit(solution)/shard_map/all_to_all | solution.py:87
  113.3 0.2 convert_reduce_fusion
  113.5 4.6 %all_gather.11 = f32[8,1024]{1,0:T(8,128)S(1)} all-gather(f32[8,512]{1,0:T(8,128)S(1)} %convert_reduce_fusion), channel_id=1, replica_groups=mesh['dp'=128,'group'=2] {'group'}, dimensions={1}, use_global_device_ids=true | all-gather | bytes 49152 | tf_op jit(solution)/shard_map/all_gather | solution.py:89
  118.1 0.6 copy.36
  (5 shorter events, 0.0 us)
Async XLA Ops:
  0.6 39.5 %copy-start = (bf16[1024,1024]{1,0:T(8,128)(2,1)S(1)}, bf16[1024,1024]{1,0:T(8,128)(2,1)}, u32[]{:S(2)}) copy-start(bf16[1024,1024]{1,0:T(8,128)(2,1)} %param.7) | copy-start | bytes 6291460
  32.0 8.2 %copy-start.1 = (bf16[8,1024]{1,0:T(8,128)(2,1)S(1)}, bf16[8,1024]{1,0:T(8,128)(2,1)}, u32[]{:S(2)}) copy-start(bf16[8,1024]{1,0:T(8,128)(2,1)} %param.5) | copy-start | bytes 49156
  33.8 11.3 %copy-start.2 = (s32[256,1]{0,1:T(1,128)S(1)}, s32[256,1]{0,1:T(1,128)}, u32[]{:S(2)}) copy-start(s32[256,1]{0,1:T(1,128)} %param.8) | copy-start | bytes 3076
  33.8 33.7 %all-to-all-start.1 = ((bf16[128,4,1024]{2,1,0:T(4,128)(2,1)}), bf16[128,4,1024]{2,1,0:T(4,128)(2,1)S(1)}, u32[]{:S(2)}, u32[]{:S(2)}) async-start(bf16[128,4,1024]{2,1,0:T(4,128)(2,1)} %copy.21), calls=%async_computation.1 | async-start | bytes 2097152 | tf_op jit(solution)/shard_map/all_to_all | solution.py:49

commit v8 on v7

--- a/solution.py
+++ b/solution.py
@@ -83,9 +83,9 @@
     chip_queries = lax.all_gather(queries, "group", axis=0, tiled=True)
     half_queries = lax.dynamic_slice_in_dim(chip_queries, group_pos * col_half, col_half, 1)
     partial = split_dot(chip_mixed, half_queries).astype(jnp.bfloat16)
-    partial = partial.reshape(dp_count, out_rows, col_half)
+    partial = partial.reshape(dp_count, 2 * out_rows, col_half // 2)
     partial = lax.all_to_all(partial, "dp", split_axis=0, concat_axis=0, tiled=True)
-    weight_half = jnp.sum(partial.astype(jnp.float32), axis=0)
+    weight_half = jnp.sum(partial.astype(jnp.float32), axis=0).reshape(out_rows, col_half)
     weight_grad = lax.all_gather(weight_half, "group", axis=1, tiled=True)
     return (weight_grad, query_loss)
 

time: 119 us -> 121 us (1.017)
    all_to_all x1, blocking collectives: 34.7 us -> 36 us  [local(): lax.all_to_all(partial, 'dp', split_axis=0, concat_axis=0, tiled=True)]
where the time goes in v8:
time: 121 us
  blocking collectives  76.9 us (64%)
  waiting for transfers between devices  22.5 us (19%)
  starting transfers between devices  6.32 us (5%)
  matrix products  5.74 us (5%)
  other arithmetic  4.69 us (4%)
  local copies, waits for them, and re-layouts  3.97 us (3%)
    all_to_all x1, blocking collectives, local(): lax.all_to_all(partial, 'dp', split_axis=0, concat_axis=0, tiled=True)  36 us
    all_to_all x1, blocking collectives, local(): lax.all_to_all(requests, 'dp', split_axis=0, concat_axis=0, tiled=True)  26.9 us
    all_to_all x1, waiting for transfers between devices, local(): lax.all_to_all(hidden_block, 'dp', split_axis=0, concat_axis=0, tiled=True)  22.5 us
    all_to_all x1, starting transfers between devices, local(): lax.all_to_all(hidden_block, 'dp', split_axis=0, concat_axis=0, tiled=True)  6.32 us
    all_gather x1, blocking collectives, local(): chip_mixed = lax.all_gather(mixed, 'group', axis=0, tiled=True)  6.27 us
    all_gather x1, blocking collectives, local(): weight_grad = lax.all_gather(weight_half, 'group', axis=1, tiled=True)  4.15 us
    all_gather x1, blocking collectives, local(): chip_queries = lax.all_gather(queries, 'group', axis=0, tiled=True)  3.59 us
  transfers between devices with their start and end apart: 1, of which 1 were waited for; matrix products, arithmetic and copies ran while one was open for 1% of the time, Pallas kernels for 0%

profile of v8, /device:TPU:1, one launch (start us, length us, event | category | flops | bytes accessed | tf_op | source)
XLA Modules:
  0.0 120.8 jit_solution(3568646290488869005)
XLA Ops:
  0.6 0.0 copy-start
  0.6 1.0 convert_reduce_fusion.1
  1.7 0.7 multiply_add_fusion.2
  2.4 0.7 convert_element_type.53
  3.0 0.1 reshape.69
  3.1 0.3 fusion.8
  3.4 0.1 all_to_all.12
  3.5 26.9 %all_to_all.19 = s32[128,1,4]{2,1,0:T(1,128)S(1)} all-to-all(s32[128,1,4]{2,1,0:T(1,128)S(1)} %bitcast.27), channel_id=1, replica_groups=mesh['dp'=128,'group'=2] {'dp'}, dimensions={0} | all-to-all | bytes 4096 | tf_op jit(solution)/shard_map/all_to_all | solution.py:42
  30.4 0.1 copy.20
  30.5 1.5 %convolution_convert_fusion = bf16[128,4,1024]{2,0,1:T(8,128)(2,1)S(1)} fusion(bf16[256,1024]{1,0:T(8,128)(2,1)} %param.6, s32[128,4]{0,1:T(4,128)S(1)} %copy.20), kind=kOutput, calls=%fused_computation.2 | convolution fusion | flops 269090816 | bytes 1574912 | tf_op jit(solution)/shard_map/kcp,pd->kcd/dot_general | solution.py:46
  32.0 0.0 copy-start.1
  32.0 1.8 %copy.21 = bf16[128,4,1024]{2,1,0:T(4,128)(2,1)} copy(bf16[128,4,1024]{2,0,1:T(8,128)(2,1)S(1)} %convolution_convert_fusion) | data formatting | bytes 2097152 | tf_op jit(solution)/shard_map/convert_element_type | solution.py:48
  33.8 0.0 copy-start.2
  33.8 6.3 %all-to-all-start.1 = ((bf16[128,4,1024]{2,1,0:T(4,128)(2,1)}), bf16[128,4,1024]{2,1,0:T(4,128)(2,1)S(1)}, u32[]{:S(2)}, u32[]{:S(2)}) async-start(bf16[128,4,1024]{2,1,0:T(4,128)(2,1)} %copy.21), calls=%async_computation.1 | async-start | bytes 2097152 | tf_op jit(solution)/shard_map/all_to_all | solution.py:49
  40.2 0.0 copy-done
  40.2 0.0 copy-done.1
  40.2 1.2 %fusion.3 = f32[8]{0:T(128)S(1)} fusion(bf16[1024,1024]{1,0:T(8,128)(2,1)S(1)} %copy-done, bf16[8,1024]{1,0:T(8,128)(2,1)S(1)} %copy-done.1, bf16[256,1024]{1,0:T(8,128)(2,1)} %param.6, s32[]{:T(128)S(6)} %select_n.6), kind=kOutput, calls=%fused_computation.9 | convolution fusion | flops 16818168 | bytes 2129956 | tf_op jit(solution)/shard_map/dot_general | solution.py:61
  41.4 0.1 copy.23
  41.5 3.6 %all_gather.10 = bf16[16,1024]{1,0:T(8,128)(2,1)S(1)} all-gather(bf16[8,1024]{1,0:T(8,128)(2,1)S(1)} %copy-done.1), channel_id=1, replica_groups=mesh['dp'=128,'group'=2] {'group'}, dimensions={0}, use_global_device_ids=true | all-gather | bytes 49152 | tf_op jit(solution)/shard_map/all_gather | solution.py:83
  45.1 0.0 copy-done.2
  45.1 22.5 %all-to-all-done.1 = bf16[128,4,1024]{2,1,0:T(4,128)(2,1)S(1)} async-done(((bf16[128,4,1024]{2,1,0:T(4,128)(2,1)}), bf16[128,4,1024]{2,1,0:T(4,128)(2,1)S(1)}, u32[]{:S(2)}, u32[]{:S(2)}) %all-to-all-start.1) | async-done | bytes 1048608 | tf_op jit(solution)/shard_map/all_to_all | solution.py:49
  67.6 0.9 fusion
  68.4 0.7 convolution_convert_fusion.1
  69.2 0.2 fusion.14
  69.4 0.2 exponential_reduce_fusion
  69.6 0.5 multiply_subtract_fusion
  70.1 0.1 subtract_exponential_fusion
  70.2 0.1 multiply_reduce_fusion
  70.3 0.1 slice_multiply_fusion
  70.4 0.3 fusion.4
  70.7 0.8 multiply_add_fusion
  71.5 6.3 %all_gather.9 = f32[16,1024]{1,0:T(8,128)S(1)} all-gather(f32[8,1024]{1,0:T(8,128)S(1)} %multiply_add_fusion), channel_id=1, replica_groups=mesh['dp'=128,'group'=2] {'group'}, dimensions={0}, use_global_device_ids=true | all-gather | bytes 98304 | tf_op jit(solution)/shard_map/all_gather | solution.py:82
  77.8 0.4 fusion.17
  78.2 0.5 add_convert_fusion
  78.7 1.2 reshape.63
  79.9 36.0 %all_to_all.20 = bf16[128,16,256]{2,1,0:T(8,128)(2,1)S(1)} all-to-all(bf16[128,16,256]{2,1,0:T(8,128)(2,1)} %reshape.63), channel_id=1, replica_groups=mesh['dp'=128,'group'=2] {'dp'}, dimensions={0} | all-to-all | bytes 2097152 | tf_op jit(solution)/shard_map/all_to_all | solution.py:87
  115.9 0.2 convert_reduce_fusion
  116.1 4.1 %all_gather.11 = f32[8,1024]{1,0:T(8,128)S(1)} all-gather(f32[8,512]{1,0:T(8,128)S(1)} %reshape.64), channel_id=1, replica_groups=mesh['dp'=128,'group'=2] {'group'}, dimensions={1}, use_global_device_ids=true | all-gather | bytes 49152 | tf_op jit(solution)/shard_map/all_gather | solution.py:89
  120.2 0.6 copy.36
  (6 shorter events, 0.0 us)
Async XLA Ops:
  0.6 39.5 %copy-start = (bf16[1024,1024]{1,0:T(8,128)(2,1)S(1)}, bf16[1024,1024]{1,0:T(8,128)(2,1)}, u32[]{:S(2)}) copy-start(bf16[1024,1024]{1,0:T(8,128)(2,1)} %param.7) | copy-start | bytes 6291460
  32.0 8.2 %copy-start.1 = (bf16[8,1024]{1,0:T(8,128)(2,1)S(1)}, bf16[8,1024]{1,0:T(8,128)(2,1)}, u32[]{:S(2)}) copy-start(bf16[8,1024]{1,0:T(8,128)(2,1)} %param.5) | copy-start | bytes 49156
  33.8 11.3 %copy-start.2 = (s32[256,1]{0,1:T(1,128)S(1)}, s32[256,1]{0,1:T(1,128)}, u32[]{:S(2)}) copy-start(s32[256,1]{0,1:T(1,128)} %param.8) | copy-start | bytes 3076
  33.8 33.7 %all-to-all-start.1 = ((bf16[128,4,1024]{2,1,0:T(4,128)(2,1)}), bf16[128,4,1024]{2,1,0:T(4,128)(2,1)S(1)}, u32[]{:S(2)}, u32[]{:S(2)}) async-start(bf16[128,4,1024]{2,1,0:T(4,128)(2,1)} %copy.21), calls=%async_computation.1 | async-start | bytes 2097152 | tf_op jit(solution)/shard_map/all_to_all | solution.py:49

commit v9 on v7

--- a/solution.py
+++ b/solution.py
@@ -31,14 +31,10 @@
     same_owner = (owners[:, None] == owners[None, :]) & (ref_index[:, None] > ref_index[None, :])
     slot_rank = jnp.sum(same_owner.astype(jnp.int32), axis=1)
     position = owners * capacity + slot_rank
-    place = (
-        position[:, None] == jnp.arange(dp_count * capacity, dtype=jnp.int32)[None, :]
-    ).astype(jnp.bfloat16)
-    requests = (
-        jnp.dot(local_ids.astype(jnp.bfloat16), place, preferred_element_type=jnp.float32)
-        .astype(jnp.int32)
-        .reshape(dp_count, capacity)
-    )
+    slots = jnp.arange(dp_count * capacity, dtype=jnp.int32)
+    requests = jnp.sum(
+        jnp.where(position[:, None] == slots[None, :], local_ids[:, None], 0), axis=0
+    ).reshape(dp_count, capacity)
     id_block = lax.all_to_all(requests, "dp", split_axis=0, concat_axis=0, tiled=True)
     pick_send = (
         id_block[:, :, None] == jnp.arange(passage_rows, dtype=jnp.int32)[None, None, :]
@@ -79,14 +75,21 @@
         axis=1,
     ) + pos_coef[:, None] * pos_hidden.astype(jnp.float32)
     col_half = width // 2
-    chip_mixed = lax.all_gather(mixed, "group", axis=0, tiled=True)
-    chip_queries = lax.all_gather(queries, "group", axis=0, tiled=True)
-    half_queries = lax.dynamic_slice_in_dim(chip_queries, group_pos * col_half, col_half, 1)
-    partial = split_dot(chip_mixed, half_queries).astype(jnp.bfloat16)
-    partial = partial.reshape(dp_count, out_rows, col_half)
+    swap = [(0, 1), (1, 0)]
+    other_mixed = lax.ppermute(mixed, "group", swap)
+    other_queries = lax.ppermute(queries, "group", swap)
+    own_cols = lax.dynamic_slice_in_dim(queries, group_pos * col_half, col_half, 1)
+    other_cols = lax.dynamic_slice_in_dim(other_queries, group_pos * col_half, col_half, 1)
+    partial = split_dot(mixed, own_cols) + split_dot(other_mixed, other_cols)
+    partial = partial.astype(jnp.bfloat16).reshape(dp_count, out_rows, col_half)
     partial = lax.all_to_all(partial, "dp", split_axis=0, concat_axis=0, tiled=True)
     weight_half = jnp.sum(partial.astype(jnp.float32), axis=0)
-    weight_grad = lax.all_gather(weight_half, "group", axis=1, tiled=True)
+    other_half = lax.ppermute(weight_half, "group", swap)
+    weight_grad = jnp.where(
+        group_pos == 0,
+        jnp.concatenate([weight_half, other_half], axis=1),
+        jnp.concatenate([other_half, weight_half], axis=1),
+    )
     return (weight_grad, query_loss)
 
 

time: 119 us -> 118 us (level)
  blocking collectives: 76 us -> 61.8 us
  starting transfers between devices: 6.32 us -> 16.3 us
  waiting for transfers between devices: 22.5 us -> 24.7 us
    all_gather x3 -> x0, blocking collectives: 14.4 us -> none  [the longest x1 6.27 us: local(): chip_mixed = lax.all_gather(mixed, 'group', axis=0, tiled=True)]
    ppermute x0 -> x3, starting transfers between devices: none -> 9.97 us  [the longest x1 4.78 us: local(): other_mixed = lax.ppermute(mixed, 'group', swap)]
    all_to_all x1, waiting for transfers between devices: 22.5 us -> 23.9 us  [local(): lax.all_to_all(hidden_block, 'dp', split_axis=0, concat_axis=0, tiled=True)]
  transfers between devices with their start and end apart: 1 -> 4, of which waited for: 1 -> 2; matrix products, arithmetic and copies ran while one was open for 1% -> 5% of each run, Pallas kernels for 0% -> 0%
where the time goes in v9:
time: 118 us
  blocking collectives  61.8 us (52%)
  waiting for transfers between devices  24.7 us (21%)
  starting transfers between devices  16.3 us (14%)
  matrix products  6.47 us (5%)
  other arithmetic  4.76 us (4%)
  local copies, waits for them, and re-layouts  2.83 us (2%)
    all_to_all x1, blocking collectives, local(): lax.all_to_all(partial, 'dp', split_axis=0, concat_axis=0, tiled=True)  34.9 us
    all_to_all x1, blocking collectives, local(): lax.all_to_all(requests, 'dp', split_axis=0, concat_axis=0, tiled=True)  26.9 us
    all_to_all x1, waiting for transfers between devices, local(): lax.all_to_all(hidden_block, 'dp', split_axis=0, concat_axis=0, tiled=True)  23.9 us
    all_to_all x1, starting transfers between devices, local(): lax.all_to_all(hidden_block, 'dp', split_axis=0, concat_axis=0, tiled=True)  6.32 us
    ppermute x1, starting transfers between devices, local(): other_mixed = lax.ppermute(mixed, 'group', swap)  4.78 us
    ppermute x1, starting transfers between devices, local(): other_half = lax.ppermute(weight_half, 'group', swap)  3 us
  transfers between devices with their start and end apart: 4, of which 2 were waited for; matrix products, arithmetic and copies ran while one was open for 5% of the time, Pallas kernels for 0%

profile of v9, /device:TPU:1, one launch (start us, length us, event | category | flops | bytes accessed | tf_op | source)
XLA Modules:
  0.0 117.7 jit_solution(5433493123827704311)
XLA Ops:
  0.6 0.0 copy-start
  0.6 1.0 convert_reduce_fusion.1
  1.7 0.7 multiply_add_fusion.2
  2.4 0.8 broadcast_in_dim.17
  3.1 0.1 select_reduce_fusion
  3.3 0.1 all_to_all.12
  3.4 26.9 %all_to_all.19 = s32[128,1,4]{2,1,0:T(1,128)S(1)} all-to-all(s32[128,1,4]{2,1,0:T(1,128)S(1)} %bitcast.27), channel_id=1, replica_groups=mesh['dp'=128,'group'=2] {'dp'}, dimensions={0} | all-to-all | bytes 4096 | tf_op jit(solution)/shard_map/all_to_all | solution.py:38
  30.3 0.1 copy.20
  30.3 1.5 %convolution_convert_fusion = bf16[128,4,1024]{2,0,1:T(8,128)(2,1)S(1)} fusion(bf16[256,1024]{1,0:T(8,128)(2,1)} %param.6, s32[128,4]{0,1:T(4,128)S(1)} %copy.20), kind=kOutput, calls=%fused_computation.2 | convolution fusion | flops 269090816 | bytes 1574912 | tf_op jit(solution)/shard_map/kcp,pd->kcd/dot_general | solution.py:42
  31.9 0.0 copy-start.1
  31.9 1.8 %copy.21 = bf16[128,4,1024]{2,1,0:T(4,128)(2,1)} copy(bf16[128,4,1024]{2,0,1:T(8,128)(2,1)S(1)} %convolution_convert_fusion) | data formatting | bytes 2097152 | tf_op jit(solution)/shard_map/convert_element_type | solution.py:44
  33.7 0.0 copy-start.2
  33.7 6.3 %all-to-all-start.1 = ((bf16[128,4,1024]{2,1,0:T(4,128)(2,1)}), bf16[128,4,1024]{2,1,0:T(4,128)(2,1)S(1)}, u32[]{:S(2)}, u32[]{:S(2)}) async-start(bf16[128,4,1024]{2,1,0:T(4,128)(2,1)} %copy.21), calls=%async_computation.1 | async-start | bytes 2097152 | tf_op jit(solution)/shard_map/all_to_all | solution.py:45
  40.0 0.0 copy-done.1
  40.0 2.2 %collective-permute-start.1 = (bf16[8,1024]{1,0:T(8,128)(2,1)S(1)}, bf16[8,1024]{1,0:T(8,128)(2,1)S(1)}, u32[]{:S(2)}, u32[]{:S(2)}) collective-permute-start(bf16[8,1024]{1,0:T(8,128)(2,1)S(1)} %copy-done.1), channel_id=1, source_target_pairs={{0,1},{1,0},{2,3},{3,2},{4,5},{5,4},{6,7},{7,6},{8,9},{9,8},{10,11... | collective-permute-start | bytes 49160 | tf_op jit(solution)/shard_map/ppermute | solution.py:80
  42.2 0.0 copy-done
  42.2 1.2 %fusion.4 = f32[8]{0:T(128)S(1)} fusion(bf16[1024,1024]{1,0:T(8,128)(2,1)S(1)} %copy-done, bf16[8,1024]{1,0:T(8,128)(2,1)S(1)} %copy-done.1, bf16[256,1024]{1,0:T(8,128)(2,1)} %param.6, s32[]{:T(128)S(6)} %select_n.20), kind=kOutput, calls=%fused_computation.10 | convolution fusion | flops 16818168 | bytes 2129956 | tf_op jit(solution)/shard_map/dot_general | solution.py:57
  43.4 0.1 copy.23
  43.5 0.0 copy-done.2
  43.5 23.9 %all-to-all-done.1 = bf16[128,4,1024]{2,1,0:T(4,128)(2,1)S(1)} async-done(((bf16[128,4,1024]{2,1,0:T(4,128)(2,1)}), bf16[128,4,1024]{2,1,0:T(4,128)(2,1)S(1)}, u32[]{:S(2)}, u32[]{:S(2)}) %all-to-all-start.1) | async-done | bytes 1048608 | tf_op jit(solution)/shard_map/all_to_all | solution.py:45
  67.4 0.9 fusion.1
  68.3 0.7 convolution_convert_fusion.1
  69.0 0.2 fusion.13
  69.3 0.2 exponential_reduce_fusion
  69.5 0.5 multiply_subtract_fusion
  70.0 0.1 subtract_exponential_fusion
  70.1 0.1 multiply_reduce_fusion
  70.2 0.1 slice_multiply_fusion
  70.3 0.3 fusion.5
  70.6 0.8 multiply_add_fusion
  71.4 4.8 %collective-permute-start = (f32[8,1024]{1,0:T(8,128)S(1)}, f32[8,1024]{1,0:T(8,128)S(1)}, u32[]{:S(2)}, u32[]{:S(2)}) collective-permute-start(f32[8,1024]{1,0:T(8,128)S(1)} %multiply_add_fusion), channel_id=1, source_target_pairs={{0,1},{1,0},{2,3},{3,2},{4,5},{5,4},{6,7},{7,6},{8,9},{9,8},{10,11... | collective-permute-start | bytes 98312 | tf_op jit(solution)/shard_map/ppermute | solution.py:79
  76.1 0.5 fusion.15
  76.6 0.5 fusion.21
  77.1 0.0 collective-permute-done.1
  77.1 0.0 collective-permute-done
  77.1 0.5 fusion.16
  77.6 0.5 fusion
  78.1 34.9 %all_to_all.20 = bf16[128,8,512]{2,1,0:T(8,128)(2,1)S(1)} all-to-all(bf16[128,8,512]{2,1,0:T(8,128)(2,1)S(1)} %fusion), channel_id=1, replica_groups=mesh['dp'=128,'group'=2] {'dp'}, dimensions={0} | all-to-all | bytes 2097152 | tf_op jit(solution)/shard_map/all_to_all | solution.py:85
  113.0 0.2 convert_reduce_fusion
  113.2 3.0 %collective-permute-start.2 = (f32[8,512]{1,0:T(8,128)S(1)}, f32[8,512]{1,0:T(8,128)S(1)}, u32[]{:S(2)}, u32[]{:S(2)}) collective-permute-start(f32[8,512]{1,0:T(8,128)S(1)} %convert_reduce_fusion), channel_id=1, source_target_pairs={{0,1},{1,0},{2,3},{3,2},{4,5},{5,4},{6,7},{7,6},{8,9},{9,8},{10,11... | collective-permute-start | bytes 49160 | tf_op jit(solution)/shard_map/ppermute | solution.py:87
  116.2 0.8 collective-permute-done.2
  117.1 0.6 maximum_select_fusion
  (4 shorter events, 0.0 us)
Async XLA Ops:
  0.6 41.6 %copy-start = (bf16[1024,1024]{1,0:T(8,128)(2,1)S(1)}, bf16[1024,1024]{1,0:T(8,128)(2,1)}, u32[]{:S(2)}) copy-start(bf16[1024,1024]{1,0:T(8,128)(2,1)} %param.7) | copy-start | bytes 6291460
  31.9 8.1 %copy-start.1 = (bf16[8,1024]{1,0:T(8,128)(2,1)S(1)}, bf16[8,1024]{1,0:T(8,128)(2,1)}, u32[]{:S(2)}) copy-start(bf16[8,1024]{1,0:T(8,128)(2,1)} %param.5) | copy-start | bytes 49156
  33.7 9.8 %copy-start.2 = (s32[256,1]{0,1:T(1,128)S(1)}, s32[256,1]{0,1:T(1,128)}, u32[]{:S(2)}) copy-start(s32[256,1]{0,1:T(1,128)} %param.8) | copy-start | bytes 3076
  33.7 33.7 %all-to-all-start.1 = ((bf16[128,4,1024]{2,1,0:T(4,128)(2,1)}), bf16[128,4,1024]{2,1,0:T(4,128)(2,1)S(1)}, u32[]{:S(2)}, u32[]{:S(2)}) async-start(bf16[128,4,1024]{2,1,0:T(4,128)(2,1)} %copy.21), calls=%async_computation.1 | async-start | bytes 2097152 | tf_op jit(solution)/shard_map/all_to_all | solution.py:45
  40.0 37.1 %collective-permute-start.1 = (bf16[8,1024]{1,0:T(8,128)(2,1)S(1)}, bf16[8,1024]{1,0:T(8,128)(2,1)S(1)}, u32[]{:S(2)}, u32[]{:S(2)}) collective-permute-start(bf16[8,1024]{1,0:T(8,128)(2,1)S(1)} %copy-done.1), channel_id=1, source_target_pairs={{0,1},{1,0},{2,3},{3,2},{4,5},{5,4},{6,7},{7,6},{8,9},{9,8},{10,11... | collective-permute-start | bytes 49160 | tf_op jit(solution)/shard_map/ppermute | solution.py:80
  71.4 5.8 %collective-permute-start = (f32[8,1024]{1,0:T(8,128)S(1)}, f32[8,1024]{1,0:T(8,128)S(1)}, u32[]{:S(2)}, u32[]{:S(2)}) collective-permute-start(f32[8,1024]{1,0:T(8,128)S(1)} %multiply_add_fusion), channel_id=1, source_target_pairs={{0,1},{1,0},{2,3},{3,2},{4,5},{5,4},{6,7},{7,6},{8,9},{9,8},{10,11... | collective-permute-start | bytes 98312 | tf_op jit(solution)/shard_map/ppermute | solution.py:79
  113.2 3.8 %collective-permute-start.2 = (f32[8,512]{1,0:T(8,128)S(1)}, f32[8,512]{1,0:T(8,128)S(1)}, u32[]{:S(2)}, u32[]{:S(2)}) collective-permute-start(f32[8,512]{1,0:T(8,128)S(1)} %convert_reduce_fusion), channel_id=1, source_target_pairs={{0,1},{1,0},{2,3},{3,2},{4,5},{5,4},{6,7},{7,6},{8,9},{9,8},{10,11... | collective-permute-start | bytes 49160 | tf_op jit(solution)/shard_map/ppermute | solution.py:87

commit v10 on v9

--- a/solution.py
+++ b/solution.py
@@ -3,6 +3,7 @@
 import jax
 import jax.numpy as jnp
 from jax import lax
+from jax.experimental import pallas as pl
 from jax.sharding import PartitionSpec as P
 
 
@@ -13,6 +14,17 @@
     return lax.dot_general(high, right, dims, preferred_element_type=jnp.float32) + lax.dot_general(
         low, right, dims, preferred_element_type=jnp.float32
     )
+
+
+def send_kernel(ids_ref, hidden_ref, out_ref):
+    hidden = hidden_ref[...]
+    owners, capacity, _ = out_ref.shape
+    rows = lax.broadcasted_iota(jnp.int32, (owners, hidden.shape[0]), 1)
+    for slot in range(capacity):
+        pick = (ids_ref[:, slot : slot + 1] == rows).astype(jnp.bfloat16)
+        out_ref[:, slot, :] = jnp.dot(pick, hidden, preferred_element_type=jnp.float32).astype(
+            jnp.bfloat16
+        )
 
 
 def local(queries, passage_hidden, out_weight, neg_owner, neg_local):
@@ -36,12 +48,10 @@
         jnp.where(position[:, None] == slots[None, :], local_ids[:, None], 0), axis=0
     ).reshape(dp_count, capacity)
     id_block = lax.all_to_all(requests, "dp", split_axis=0, concat_axis=0, tiled=True)
-    pick_send = (
-        id_block[:, :, None] == jnp.arange(passage_rows, dtype=jnp.int32)[None, None, :]
-    ).astype(jnp.bfloat16)
-    hidden_block = jnp.einsum(
-        "kcp,pd->kcd", pick_send, passage_hidden, preferred_element_type=jnp.float32
-    ).astype(jnp.bfloat16)
+    hidden_block = pl.pallas_call(
+        send_kernel,
+        out_shape=jax.ShapeDtypeStruct((dp_count, capacity, width), jnp.bfloat16),
+    )(id_block, passage_hidden)
     returned_hidden = lax.all_to_all(hidden_block, "dp", split_axis=0, concat_axis=0, tiled=True)
     pick_back = (
         position[:, None, None]

time: 118 us -> 118 us (level)
  Pallas kernels: 0 us -> 2.98 us
  local copies, waits for them, and re-layouts: 2.83 us -> 0.97 us
  matrix products: 6.47 us -> 4.93 us
    pallas_call x0 -> x1, Pallas kernels: none -> 2.98 us  [local(): pl.pallas_call(send_kernel, out_shape=jax.ShapeDtypeStruct((dp_count, cap...]
    convert_element_type x1 -> x0, local copies, waits for them, and re-layouts: 1.8 us -> none  [local(): hidden_block = jnp.einsum('kcp,pd->kcd', pick_send, passage_hidden, prefe...]
    dot_general x1 -> x0, matrix products: 1.55 us -> none  [local(): jnp.einsum('kcp,pd->kcd', pick_send, passage_hidden, preferred_element_ty...]
where the time goes in v10:
time: 118 us
  blocking collectives  62.1 us (53%)
  waiting for transfers between devices  24.5 us (21%)
  starting transfers between devices  16.5 us (14%)
  matrix products  4.93 us (4%)
  other arithmetic  4.77 us (4%)
  Pallas kernels  2.98 us (3%)
    all_to_all x1, blocking collectives, local(): lax.all_to_all(partial, 'dp', split_axis=0, concat_axis=0, tiled=True)  34.9 us
    all_to_all x1, blocking collectives, local(): lax.all_to_all(requests, 'dp', split_axis=0, concat_axis=0, tiled=True)  27.2 us
    all_to_all x1, waiting for transfers between devices, local(): lax.all_to_all(hidden_block, 'dp', split_axis=0, concat_axis=0, tiled=True)  23.6 us
    all_to_all x1, starting transfers between devices, local(): lax.all_to_all(hidden_block, 'dp', split_axis=0, concat_axis=0, tiled=True)  6.32 us
    ppermute x1, starting transfers between devices, local(): other_mixed = lax.ppermute(mixed, 'group', swap)  4.87 us
    ppermute x1, starting transfers between devices, local(): other_half = lax.ppermute(weight_half, 'group', swap)  3 us
    pallas_call x1, Pallas kernels, local(): pl.pallas_call(send_kernel, out_shape=jax.ShapeDtypeStruct((dp_count, cap...  2.98 us
  transfers between devices with their start and end apart: 4, of which 2 were waited for; matrix products, arithmetic and copies ran while one was open for 5% of the time, Pallas kernels for 0%

profile of v10, /device:TPU:1, one launch (start us, length us, event | category | flops | bytes accessed | tf_op | source)
XLA Modules:
  0.0 117.6 jit_solution(9236257303757066432)
XLA Ops:
  0.6 0.0 copy-start
  0.6 0.0 copy-start.1
  0.7 1.0 convert_reduce_fusion.1
  1.7 0.7 multiply_add_fusion.2
  2.4 0.8 broadcast_in_dim.26
  3.1 0.1 select_reduce_fusion
  3.3 0.1 all_to_all.13
  3.4 27.2 %all_to_all.21 = s32[128,1,4]{2,1,0:T(1,128)} all-to-all(s32[128,1,4]{2,1,0:T(1,128)S(1)} %bitcast.25), channel_id=1, replica_groups=mesh['dp'=128,'group'=2] {'dp'}, dimensions={0} | all-to-all | bytes 4096 | tf_op jit(solution)/shard_map/all_to_all | solution.py:50
  30.6 3.0 %shard_map.68 = bf16[128,4,1024]{2,1,0:T(4,128)(2,1)} custom-call(s32[128,4]{1,0:T(8,128)} %bitcast.24, bf16[256,1024]{1,0:T(8,128)(2,1)} %hidden_ref.1), custom_call_target="tpu_custom_call" | custom-call | tf_op jit(solution)/shard_map/pallas_call | solution.py:51
  33.6 0.0 copy-start.2
  33.6 6.3 %all-to-all-start.1 = ((bf16[128,4,1024]{2,1,0:T(4,128)(2,1)}), bf16[128,4,1024]{2,1,0:T(4,128)(2,1)S(1)}, u32[]{:S(2)}, u32[]{:S(2)}) async-start(bf16[128,4,1024]{2,1,0:T(4,128)(2,1)} %shard_map.68), calls=%async_computation.1 | async-start | bytes 2097152 | tf_op jit(solution)/shard_map/all_to_all | solution.py:55
  39.9 0.0 copy-done.1
  39.9 2.3 %collective-permute-start.1 = (bf16[8,1024]{1,0:T(8,128)(2,1)S(1)}, bf16[8,1024]{1,0:T(8,128)(2,1)S(1)}, u32[]{:S(2)}, u32[]{:S(2)}) collective-permute-start(bf16[8,1024]{1,0:T(8,128)(2,1)S(1)} %copy-done.1), channel_id=1, source_target_pairs={{0,1},{1,0},{2,3},{3,2},{4,5},{5,4},{6,7},{7,6},{8,9},{9,8},{10,11... | collective-permute-start | bytes 49160 | tf_op jit(solution)/shard_map/ppermute | solution.py:90
  42.3 0.0 copy-done
  42.3 1.2 %fusion.4 = f32[8]{0:T(128)S(1)} fusion(bf16[1024,1024]{1,0:T(8,128)(2,1)S(1)} %copy-done, bf16[8,1024]{1,0:T(8,128)(2,1)S(1)} %copy-done.1, bf16[256,1024]{1,0:T(8,128)(2,1)} %hidden_ref.1, s32[]{:T(128)S(6)} %select_n.20), kind=kOutput, calls=%fused_computation.9 | convolution fusion | flops 16818168 | bytes 2129956 | tf_op jit(solution)/shard_map/dot_general | solution.py:67
  43.5 0.1 copy.19
  43.6 0.0 copy-done.2
  43.6 23.6 %all-to-all-done.1 = bf16[128,4,1024]{2,1,0:T(4,128)(2,1)S(1)} async-done(((bf16[128,4,1024]{2,1,0:T(4,128)(2,1)}), bf16[128,4,1024]{2,1,0:T(4,128)(2,1)S(1)}, u32[]{:S(2)}, u32[]{:S(2)}) %all-to-all-start.1) | async-done | bytes 1048608 | tf_op jit(solution)/shard_map/all_to_all | solution.py:55
  67.2 0.9 fusion.1
  68.1 0.7 convolution_convert_fusion
  68.8 0.2 fusion.11
  69.1 0.2 exponential_reduce_fusion
  69.3 0.5 multiply_subtract_fusion
  69.8 0.1 subtract_exponential_fusion
  69.9 0.1 multiply_reduce_fusion
  70.0 0.1 slice_multiply_fusion
  70.1 0.3 fusion.5
  70.3 0.8 multiply_add_fusion
  71.1 4.9 %collective-permute-start = (f32[8,1024]{1,0:T(8,128)S(1)}, f32[8,1024]{1,0:T(8,128)S(1)}, u32[]{:S(2)}, u32[]{:S(2)}) collective-permute-start(f32[8,1024]{1,0:T(8,128)S(1)} %multiply_add_fusion), channel_id=1, source_target_pairs={{0,1},{1,0},{2,3},{3,2},{4,5},{5,4},{6,7},{7,6},{8,9},{9,8},{10,11... | collective-permute-start | bytes 98312 | tf_op jit(solution)/shard_map/ppermute | solution.py:89
  76.0 0.5 fusion.13
  76.5 0.5 fusion.19
  77.0 0.0 collective-permute-done.1
  77.0 0.0 collective-permute-done
  77.0 0.5 fusion.14
  77.5 0.5 fusion
  78.0 34.9 %all_to_all.22 = bf16[128,8,512]{2,1,0:T(8,128)(2,1)S(1)} all-to-all(bf16[128,8,512]{2,1,0:T(8,128)(2,1)S(1)} %fusion), channel_id=1, replica_groups=mesh['dp'=128,'group'=2] {'dp'}, dimensions={0} | all-to-all | bytes 2097152 | tf_op jit(solution)/shard_map/all_to_all | solution.py:95
  112.9 0.2 convert_reduce_fusion
  113.1 3.0 %collective-permute-start.2 = (f32[8,512]{1,0:T(8,128)S(1)}, f32[8,512]{1,0:T(8,128)S(1)}, u32[]{:S(2)}, u32[]{:S(2)}) collective-permute-start(f32[8,512]{1,0:T(8,128)S(1)} %convert_reduce_fusion), channel_id=1, source_target_pairs={{0,1},{1,0},{2,3},{3,2},{4,5},{5,4},{6,7},{7,6},{8,9},{9,8},{10,11... | collective-permute-start | bytes 49160 | tf_op jit(solution)/shard_map/ppermute | solution.py:97
  116.1 0.8 collective-permute-done.2
  116.9 0.6 maximum_select_fusion
  (4 shorter events, 0.0 us)
Async XLA Ops:
  0.6 41.6 %copy-start = (bf16[1024,1024]{1,0:T(8,128)(2,1)S(1)}, bf16[1024,1024]{1,0:T(8,128)(2,1)}, u32[]{:S(2)}) copy-start(bf16[1024,1024]{1,0:T(8,128)(2,1)} %param.7) | copy-start | bytes 6291460
  0.6 39.3 %copy-start.1 = (bf16[8,1024]{1,0:T(8,128)(2,1)S(1)}, bf16[8,1024]{1,0:T(8,128)(2,1)}, u32[]{:S(2)}) copy-start(bf16[8,1024]{1,0:T(8,128)(2,1)} %param.5) | copy-start | bytes 49156
  33.6 10.0 %copy-start.2 = (s32[256,1]{0,1:T(1,128)S(1)}, s32[256,1]{0,1:T(1,128)}, u32[]{:S(2)}) copy-start(s32[256,1]{0,1:T(1,128)} %param.8) | copy-start | bytes 3076
  33.6 33.6 %all-to-all-start.1 = ((bf16[128,4,1024]{2,1,0:T(4,128)(2,1)}), bf16[128,4,1024]{2,1,0:T(4,128)(2,1)S(1)}, u32[]{:S(2)}, u32[]{:S(2)}) async-start(bf16[128,4,1024]{2,1,0:T(4,128)(2,1)} %shard_map.68), calls=%async_computation.1 | async-start | bytes 2097152 | tf_op jit(solution)/shard_map/all_to_all | solution.py:55
  39.9 37.1 %collective-permute-start.1 = (bf16[8,1024]{1,0:T(8,128)(2,1)S(1)}, bf16[8,1024]{1,0:T(8,128)(2,1)S(1)}, u32[]{:S(2)}, u32[]{:S(2)}) collective-permute-start(bf16[8,1024]{1,0:T(8,128)(2,1)S(1)} %copy-done.1), channel_id=1, source_target_pairs={{0,1},{1,0},{2,3},{3,2},{4,5},{5,4},{6,7},{7,6},{8,9},{9,8},{10,11... | collective-permute-start | bytes 49160 | tf_op jit(solution)/shard_map/ppermute | solution.py:90
  71.1 5.8 %collective-permute-start = (f32[8,1024]{1,0:T(8,128)S(1)}, f32[8,1024]{1,0:T(8,128)S(1)}, u32[]{:S(2)}, u32[]{:S(2)}) collective-permute-start(f32[8,1024]{1,0:T(8,128)S(1)} %multiply_add_fusion), channel_id=1, source_target_pairs={{0,1},{1,0},{2,3},{3,2},{4,5},{5,4},{6,7},{7,6},{8,9},{9,8},{10,11... | collective-permute-start | bytes 98312 | tf_op jit(solution)/shard_map/ppermute | solution.py:89
  113.1 3.8 %collective-permute-start.2 = (f32[8,512]{1,0:T(8,128)S(1)}, f32[8,512]{1,0:T(8,128)S(1)}, u32[]{:S(2)}, u32[]{:S(2)}) collective-permute-start(f32[8,512]{1,0:T(8,128)S(1)} %convert_reduce_fusion), channel_id=1, source_target_pairs={{0,1},{1,0},{2,3},{3,2},{4,5},{5,4},{6,7},{7,6},{8,9},{9,8},{10,11... | collective-permute-start | bytes 49160 | tf_op jit(solution)/shard_map/ppermute | solution.py:97

commit v11 on v10

--- a/solution.py
+++ b/solution.py
@@ -25,6 +25,39 @@
         out_ref[:, slot, :] = jnp.dot(pick, hidden, preferred_element_type=jnp.float32).astype(
             jnp.bfloat16
         )
+
+
+def score_kernel(neg_ref, pos_ref, q_ref, w_ref, mixed_ref, loss_ref):
+    f32 = jnp.float32
+    queries, width = q_ref.shape
+    neg_count = neg_ref.shape[0] // queries
+    scale = 1.5 / math.sqrt(width)
+    w = w_ref[...]
+    neg = neg_ref[...]
+    keys = jnp.dot(neg, w, preferred_element_type=f32).astype(jnp.bfloat16).astype(f32)
+    pos = pos_ref[...]
+    pos_keys = jnp.dot(pos, w, preferred_element_type=f32).astype(jnp.bfloat16).astype(f32)
+    q = q_ref[...].astype(f32)
+    q3 = q.reshape(queries, 1, width)
+    neg_logit = jnp.sum(keys.reshape(queries, neg_count, width) * q3, axis=2, keepdims=True) * scale
+    pos_logit = jnp.sum((pos_keys * q).reshape(queries, 1, width), axis=2, keepdims=True) * scale
+    total = jnp.exp(pos_logit) + jnp.sum(jnp.exp(neg_logit), axis=1, keepdims=True)
+    log_total = jnp.log(total)
+    neg_coef = jnp.exp(neg_logit - log_total) * scale
+    pos_coef = (jnp.exp(pos_logit - log_total) - 1.0) * scale
+    mixed = jnp.sum(neg.astype(f32).reshape(queries, neg_count, width) * neg_coef, axis=1, keepdims=True)
+    mixed = mixed + pos_coef * pos.astype(f32).reshape(queries, 1, width)
+    mixed_ref[...] = mixed.reshape(queries, width)
+    loss_ref[...] = jnp.broadcast_to((log_total - pos_logit).reshape(queries, 1), loss_ref.shape)
+
+def score(neg, pos, q, w):
+    return pl.pallas_call(
+        score_kernel,
+        out_shape=(
+            jax.ShapeDtypeStruct(q.shape, jnp.float32),
+            jax.ShapeDtypeStruct((q.shape[0], 128), jnp.float32),
+        ),
+    )(neg, pos, q, w)
 
 
 def local(queries, passage_hidden, out_weight, neg_owner, neg_local):
@@ -61,29 +94,8 @@
         "rkc,kcd->rd", pick_back, returned_hidden, preferred_element_type=jnp.float32
     ).astype(jnp.bfloat16)
     pos_hidden = lax.dynamic_slice_in_dim(passage_hidden, group_pos * query_rows, query_rows, 0)
-    neg_keys = jnp.dot(neg_hidden, out_weight, preferred_element_type=jnp.float32).astype(
-        jnp.bfloat16
-    ).reshape(query_rows, neg_count, width)
-    pos_keys = jnp.dot(pos_hidden, out_weight, preferred_element_type=jnp.float32).astype(
-        jnp.bfloat16
-    )
-    pos_logit = (
-        jnp.einsum("qd,qd->q", queries, pos_keys, preferred_element_type=jnp.float32) * score_scale
-    )
-    neg_logit = (
-        jnp.einsum("qd,qjd->qj", queries, neg_keys, preferred_element_type=jnp.float32)
-        * score_scale
-    )
-    logits = jnp.concatenate([pos_logit[:, None], neg_logit], axis=1)
-    log_total = jnp.log(jnp.sum(jnp.exp(logits), axis=1))
-    query_loss = log_total - pos_logit
-    soft_prob = jnp.exp(logits - log_total[:, None])
-    neg_coef = soft_prob[:, 1:] * score_scale
-    pos_coef = (soft_prob[:, 0] - 1.0) * score_scale
-    mixed = jnp.sum(
-        neg_coef[:, :, None] * neg_hidden.reshape(query_rows, neg_count, width).astype(jnp.float32),
-        axis=1,
-    ) + pos_coef[:, None] * pos_hidden.astype(jnp.float32)
+    mixed, loss_rows = score(neg_hidden, pos_hidden, queries, out_weight)
+    query_loss = loss_rows[:, 0]
     col_half = width // 2
     swap = [(0, 1), (1, 0)]
     other_mixed = lax.ppermute(mixed, "group", swap)

time: 118 us -> 123 us (1.042)
  blocking collectives: 62.1 us -> 27.2 us
  waiting for transfers between devices: 24.5 us -> 53.8 us
  starting transfers between devices: 16.5 us -> 22.2 us
  Pallas kernels: 2.98 us -> 6.7 us
  other arithmetic: 4.77 us -> 2.62 us
  local copies, waits for them, and re-layouts: 0.97 us -> 2.83 us
    all_to_all x1 -> x0, blocking collectives: 34.9 us -> none  [local(): lax.all_to_all(partial, 'dp', split_axis=0, concat_axis=0, tiled=True)]
    all_to_all x0 -> x1, waiting for transfers between devices: none -> 29.9 us  [local(): lax.all_to_all(partial, 'dp', split_axis=0, concat_axis=0, tiled=True)]
    all_to_all x0 -> x1, starting transfers between devices: none -> 6.32 us  [local(): lax.all_to_all(partial, 'dp', split_axis=0, concat_axis=0, tiled=True)]
    pallas_call x0 -> x1, Pallas kernels: none -> 3.73 us  [score(): pl.pallas_call(score_kernel, out_shape=(jax.ShapeDtypeStruct(q.shape, jnp...]
    dot_general x3 -> x0, matrix products: 2.16 us -> none  [the longest x1 1.21 us: local(): jnp.dot(pos_hidden, out_weight, preferred_element_type=jnp.float32)]
    dot_general x2, matrix products: 0.95 us -> 2.65 us  [split_dot(): lax.dot_general(high, right, dims, preferred_element_type=jnp.float32)]
    dynamic_slice x0 -> x1, local copies, waits for them, and re-layouts: none -> 1.32 us  [local(): lax.dynamic_slice_in_dim(passage_hidden, group_pos * query_rows, query_ro...]
  transfers between devices with their start and end apart: 4 -> 5, of which waited for: 2 -> 3; matrix products, arithmetic and copies ran while one was open for 5% -> 5% of each run, Pallas kernels for 0% -> 3%
where the time goes in v11:
time: 123 us; the launch traced here: 122 us
  waiting for transfers between devices  53.8 us (44%)
  blocking collectives  27.2 us (22%)
  starting transfers between devices  22.2 us (18%)
  Pallas kernels  6.7 us (5%)
  matrix products  6.09 us (5%)
  local copies, waits for them, and re-layouts  2.83 us (2%)
  other arithmetic  2.62 us (2%)
    all_to_all x1, waiting for transfers between devices, local(): lax.all_to_all(partial, 'dp', split_axis=0, concat_axis=0, tiled=True)  29.9 us
    all_to_all x1, blocking collectives, local(): lax.all_to_all(requests, 'dp', split_axis=0, concat_axis=0, tiled=True)  27.2 us
    all_to_all x1, waiting for transfers between devices, local(): lax.all_to_all(hidden_block, 'dp', split_axis=0, concat_axis=0, tiled=True)  23.6 us
    all_to_all x1, starting transfers between devices, local(): lax.all_to_all(partial, 'dp', split_axis=0, concat_axis=0, tiled=True)  6.32 us
    all_to_all x1, starting transfers between devices, local(): lax.all_to_all(hidden_block, 'dp', split_axis=0, concat_axis=0, tiled=True)  6.19 us
    ppermute x1, starting transfers between devices, local(): other_mixed = lax.ppermute(mixed, 'group', swap)  4.87 us
    pallas_call x1, Pallas kernels, score(): pl.pallas_call(score_kernel, out_shape=(jax.ShapeDtypeStruct(q.shape, jnp...  3.73 us
    pallas_call x1, Pallas kernels, local(): pl.pallas_call(send_kernel, out_shape=jax.ShapeDtypeStruct((dp_count, cap...  2.97 us
  transfers between devices with their start and end apart: 5, of which 3 were waited for; matrix products, arithmetic and copies ran while one was open for 5% of the time, Pallas kernels for 3%

profile of v11, /device:TPU:1, one launch (start us, length us, event | category | flops | bytes accessed | tf_op | source)
XLA Modules:
  0.0 122.2 jit_solution(8318621525116365356)
XLA Ops:
  0.6 0.0 copy-start.1
  0.6 1.0 convert_reduce_fusion.1
  1.6 0.7 multiply_add_fusion.1
  2.3 0.8 broadcast_in_dim.19
  3.0 0.1 select_reduce_fusion
  3.2 0.1 all_to_all.13
  3.3 27.2 %all_to_all.21 = s32[128,1,4]{2,1,0:T(1,128)} all-to-all(s32[128,1,4]{2,1,0:T(1,128)S(1)} %bitcast.12), channel_id=1, replica_groups=mesh['dp'=128,'group'=2] {'dp'}, dimensions={0} | all-to-all | bytes 4096 | tf_op jit(solution)/shard_map/all_to_all | solution.py:83
  30.5 3.0 %shard_map.68 = bf16[128,4,1024]{2,1,0:T(4,128)(2,1)} custom-call(s32[128,4]{1,0:T(8,128)} %bitcast.11, bf16[256,1024]{1,0:T(8,128)(2,1)} %hidden_ref.1), custom_call_target="tpu_custom_call" | custom-call | tf_op jit(solution)/shard_map/pallas_call | solution.py:84
  33.5 6.2 %all-to-all-start.1 = ((bf16[128,4,1024]{2,1,0:T(4,128)(2,1)}), bf16[128,4,1024]{2,1,0:T(4,128)(2,1)S(1)}, u32[]{:S(2)}, u32[]{:S(2)}) async-start(bf16[128,4,1024]{2,1,0:T(4,128)(2,1)} %shard_map.68), calls=%async_computation.1 | async-start | bytes 2097152 | tf_op jit(solution)/shard_map/all_to_all | solution.py:88
  39.7 2.3 %collective-permute-start.1 = (bf16[8,1024]{1,0:T(8,128)(2,1)}, bf16[8,1024]{1,0:T(8,128)(2,1)S(1)}, u32[]{:S(2)}, u32[]{:S(2)}) collective-permute-start(bf16[8,1024]{1,0:T(8,128)(2,1)} %q_ref.1), channel_id=1, source_target_pairs={{0,1},{1,0},{2,3},{3,2},{4,5},{5,4},{6,7},{7,6},{8,9},{9,8},{10,11... | collective-permute-start | bytes 49160 | tf_op jit(solution)/shard_map/ppermute | solution.py:102
  42.0 1.3 %constant_dynamic-slice_fusion.pos_ref = bf16[8,1024]{1,0:T(8,128)(2,1)} fusion(bf16[256,1024]{1,0:T(8,128)(2,1)} %hidden_ref.1, s32[]{:T(128)S(6)} %select_n.21), kind=kLoop, calls=%fused_computation.35 | loop fusion | bytes 32772 | tf_op jit(solution)/shard_map/dynamic_slice | solution.py:96
  43.4 0.0 copy-done.1
  43.4 23.6 %all-to-all-done.1 = bf16[128,4,1024]{2,1,0:T(4,128)(2,1)S(1)} async-done(((bf16[128,4,1024]{2,1,0:T(4,128)(2,1)}), bf16[128,4,1024]{2,1,0:T(4,128)(2,1)S(1)}, u32[]{:S(2)}, u32[]{:S(2)}) %all-to-all-start.1) | async-done | bytes 1048608 | tf_op jit(solution)/shard_map/all_to_all | solution.py:88
  67.0 1.7 %fusion.1.neg_ref = bf16[256,1024]{1,0:T(8,128)(2,1)} fusion(bf16[128,4,1024]{2,1,0:T(4,128)(2,1)S(1)} %all-to-all-done.1, s32[128,4]{0,1:T(4,128)S(1)} %multiply_add_fusion, s32[256]{0:T(256)S(1)} %multiply_add_fusion.2), kind=kOutput, calls=%fused_computation.4 | convolution fusion | flops 268828672 | bytes 1575936 | tf_op jit(solution)/shard_map/rkc,kcd->rd/dot_general | solution.py:93
  68.7 3.7 %shard_map.69 = (f32[8,1024]{1,0:T(8,128)}, f32[8,128]{1,0:T(8,128)}) custom-call(bf16[256,1024]{1,0:T(8,128)(2,1)} %fusion.1.neg_ref, bf16[8,1024]{1,0:T(8,128)(2,1)} %constant_dynamic-slice_fusion.pos_ref, bf16[8,1024]{1,0:T(8,128)(2,1)} %q_ref.1, bf16[1024,1024]{1,0:T(8,128)(2,1)} %w_ref.1), custom_call_target="tpu_custom_call" | custom-call | tf_op jit(solution)/shard_map/pallas_call | solution.py:54
  72.4 0.0 copy-start
  72.4 4.9 %collective-permute-start = (f32[8,1024]{1,0:T(8,128)}, f32[8,1024]{1,0:T(8,128)S(1)}, u32[]{:S(2)}, u32[]{:S(2)}) collective-permute-start(f32[8,1024]{1,0:T(8,128)} %get-tuple-element.4), channel_id=1, source_target_pairs={{0,1},{1,0},{2,3},{3,2},{4,5},{5,4},{6,7},{7,6},{8,9},{9,8},{10,11... | collective-permute-start | bytes 98312 | tf_op jit(solution)/shard_map/ppermute | solution.py:101
  77.3 1.3 %fusion.7 = f32[1024,512]{1,0:T(8,128)S(1)} fusion(f32[8,1024]{1,0:T(8,128)} %get-tuple-element.4, bf16[8,1024]{1,0:T(8,128)(2,1)} %q_ref.1, s32[]{:T(128)S(6)} %select_n.22), kind=kOutput, calls=%fused_computation.17 | convolution fusion | flops 8421376 | bytes 2138116 | tf_op jit(solution)/shard_map/dot_general | solution.py:14
  78.6 0.0 copy-done
  78.6 1.2 fusion.12
  79.8 0.0 collective-permute-done.1
  79.8 0.0 collective-permute-done
  79.8 0.5 fusion.8
  80.3 1.5 %fusion = bf16[128,8,512]{2,1,0:T(8,128)(2,1)} fusion(f32[1024,512]{1,0:T(8,128)S(1)} %fusion.8, f32[1024,512]{1,0:T(8,128)S(1)} %fusion.12, f32[1024,512]{1,0:T(8,128)S(1)} %fusion.7, f32[8,1024]{1,0:T(8,128)S(1)} %collective-permute-done, bf16[8,1024]{1,0:T(8,128)(2,1)S(1)} %collective-permute-done.1, s32[]{:T(128)S(6)} %select_n.22), kind=kOutput, calls=%fused_computation.2 | convolution fusion | flops 10493952 | bytes 7380996 | tf_op jit(solution)/shard_map/dot_general | solution.py:14
  81.7 0.0 copy-start.2
  81.7 6.3 %all-to-all-start.2 = ((bf16[128,8,512]{2,1,0:T(8,128)(2,1)}), bf16[128,8,512]{2,1,0:T(8,128)(2,1)S(1)}, u32[]{:S(2)}, u32[]{:S(2)}) async-start(bf16[128,8,512]{2,1,0:T(8,128)(2,1)} %fusion), calls=%async_computation.2 | async-start | bytes 2097152 | tf_op jit(solution)/shard_map/all_to_all | solution.py:107
  88.1 29.9 %all-to-all-done.2 = bf16[128,8,512]{2,1,0:T(8,128)(2,1)S(1)} async-done(((bf16[128,8,512]{2,1,0:T(8,128)(2,1)}), bf16[128,8,512]{2,1,0:T(8,128)(2,1)S(1)}, u32[]{:S(2)}, u32[]{:S(2)}) %all-to-all-start.2) | async-done | bytes 1048608 | tf_op jit(solution)/shard_map/all_to_all | solution.py:107
  118.0 0.2 convert_reduce_fusion
  118.2 2.5 %collective-permute-start.2 = (f32[8,512]{1,0:T(8,128)S(1)}, f32[8,512]{1,0:T(8,128)S(1)}, u32[]{:S(2)}, u32[]{:S(2)}) collective-permute-start(f32[8,512]{1,0:T(8,128)S(1)} %convert_reduce_fusion), channel_id=1, source_target_pairs={{0,1},{1,0},{2,3},{3,2},{4,5},{5,4},{6,7},{7,6},{8,9},{9,8},{10,11... | collective-permute-start | bytes 49160 | tf_op jit(solution)/shard_map/ppermute | solution.py:109
  120.7 0.0 copy-done.2
  120.7 0.6 slice_reduce_fusion
  121.3 0.2 collective-permute-done.2
  121.5 0.6 maximum_select_fusion
  (2 shorter events, 0.0 us)
Async XLA Ops:
  0.6 42.7 %copy-start.1 = (s32[256,1]{0,1:T(1,128)S(1)}, s32[256,1]{0,1:T(1,128)}, u32[]{:S(2)}) copy-start(s32[256,1]{0,1:T(1,128)} %param.8) | copy-start | bytes 3076
  33.5 33.5 %all-to-all-start.1 = ((bf16[128,4,1024]{2,1,0:T(4,128)(2,1)}), bf16[128,4,1024]{2,1,0:T(4,128)(2,1)S(1)}, u32[]{:S(2)}, u32[]{:S(2)}) async-start(bf16[128,4,1024]{2,1,0:T(4,128)(2,1)} %shard_map.68), calls=%async_computation.1 | async-start | bytes 2097152 | tf_op jit(solution)/shard_map/all_to_all | solution.py:88
  39.7 40.1 %collective-permute-start.1 = (bf16[8,1024]{1,0:T(8,128)(2,1)}, bf16[8,1024]{1,0:T(8,128)(2,1)S(1)}, u32[]{:S(2)}, u32[]{:S(2)}) collective-permute-start(bf16[8,1024]{1,0:T(8,128)(2,1)} %q_ref.1), channel_id=1, source_target_pairs={{0,1},{1,0},{2,3},{3,2},{4,5},{5,4},{6,7},{7,6},{8,9},{9,8},{10,11... | collective-permute-start | bytes 49160 | tf_op jit(solution)/shard_map/ppermute | solution.py:102
  72.4 6.2 %copy-start = (f32[8,1024]{1,0:T(8,128)S(1)}, f32[8,1024]{1,0:T(8,128)}, u32[]{:S(2)}) copy-start(f32[8,1024]{1,0:T(8,128)} %get-tuple-element.4) | copy-start | bytes 98308
  72.4 7.4 %collective-permute-start = (f32[8,1024]{1,0:T(8,128)}, f32[8,1024]{1,0:T(8,128)S(1)}, u32[]{:S(2)}, u32[]{:S(2)}) collective-permute-start(f32[8,1024]{1,0:T(8,128)} %get-tuple-element.4), channel_id=1, source_target_pairs={{0,1},{1,0},{2,3},{3,2},{4,5},{5,4},{6,7},{7,6},{8,9},{9,8},{10,11... | collective-permute-start | bytes 98312 | tf_op jit(solution)/shard_map/ppermute | solution.py:101
  81.7 39.0 %copy-start.2 = (f32[8,128]{1,0:T(8,128)S(1)}, f32[8,128]{1,0:T(8,128)}, u32[]{:S(2)}) copy-start(f32[8,128]{1,0:T(8,128)} %get-tuple-element.5) | copy-start | bytes 12292
  81.7 36.3 %all-to-all-start.2 = ((bf16[128,8,512]{2,1,0:T(8,128)(2,1)}), bf16[128,8,512]{2,1,0:T(8,128)(2,1)S(1)}, u32[]{:S(2)}, u32[]{:S(2)}) async-start(bf16[128,8,512]{2,1,0:T(8,128)(2,1)} %fusion), calls=%async_computation.2 | async-start | bytes 2097152 | tf_op jit(solution)/shard_map/all_to_all | solution.py:107
  118.2 3.3 %collective-permute-start.2 = (f32[8,512]{1,0:T(8,128)S(1)}, f32[8,512]{1,0:T(8,128)S(1)}, u32[]{:S(2)}, u32[]{:S(2)}) collective-permute-start(f32[8,512]{1,0:T(8,128)S(1)} %convert_reduce_fusion), channel_id=1, source_target_pairs={{0,1},{1,0},{2,3},{3,2},{4,5},{5,4},{6,7},{7,6},{8,9},{9,8},{10,11... | collective-permute-start | bytes 49160 | tf_op jit(solution)/shard_map/ppermute | solution.py:109

commit v12 on v10

--- a/solution.py
+++ b/solution.py
@@ -7,24 +7,15 @@
 from jax.sharding import PartitionSpec as P
 
 
-def split_dot(left, right):
-    high = left.astype(jnp.bfloat16)
-    low = (left - high.astype(jnp.float32)).astype(jnp.bfloat16)
-    dims = (((0,), (0,)), ((), ()))
-    return lax.dot_general(high, right, dims, preferred_element_type=jnp.float32) + lax.dot_general(
-        low, right, dims, preferred_element_type=jnp.float32
-    )
-
-
 def send_kernel(ids_ref, hidden_ref, out_ref):
     hidden = hidden_ref[...]
-    owners, capacity, _ = out_ref.shape
-    rows = lax.broadcasted_iota(jnp.int32, (owners, hidden.shape[0]), 1)
-    for slot in range(capacity):
-        pick = (ids_ref[:, slot : slot + 1] == rows).astype(jnp.bfloat16)
-        out_ref[:, slot, :] = jnp.dot(pick, hidden, preferred_element_type=jnp.float32).astype(
-            jnp.bfloat16
-        )
+    owners, capacity, width = out_ref.shape
+    rows = lax.broadcasted_iota(jnp.int32, (owners, capacity, hidden.shape[0]), 2)
+    pick = (ids_ref[...][:, :, None] == rows).astype(jnp.bfloat16)
+    picked = jnp.dot(
+        pick.reshape(owners * capacity, hidden.shape[0]), hidden, preferred_element_type=jnp.float32
+    )
+    out_ref[...] = picked.astype(jnp.bfloat16).reshape(owners, capacity, width)
 
 
 def local(queries, passage_hidden, out_weight, neg_owner, neg_local):
@@ -86,11 +77,20 @@
     ) + pos_coef[:, None] * pos_hidden.astype(jnp.float32)
     col_half = width // 2
     swap = [(0, 1), (1, 0)]
-    other_mixed = lax.ppermute(mixed, "group", swap)
+    mixed_high = mixed.astype(jnp.bfloat16)
+    mixed_parts = jnp.concatenate(
+        [mixed_high, (mixed - mixed_high.astype(jnp.float32)).astype(jnp.bfloat16)], axis=0
+    )
+    other_parts = lax.ppermute(mixed_parts, "group", swap)
     other_queries = lax.ppermute(queries, "group", swap)
     own_cols = lax.dynamic_slice_in_dim(queries, group_pos * col_half, col_half, 1)
     other_cols = lax.dynamic_slice_in_dim(other_queries, group_pos * col_half, col_half, 1)
-    partial = split_dot(mixed, own_cols) + split_dot(other_mixed, other_cols)
+    partial = lax.dot_general(
+        jnp.concatenate([mixed_parts, other_parts], axis=0),
+        jnp.concatenate([own_cols, own_cols, other_cols, other_cols], axis=0),
+        (((0,), (0,)), ((), ())),
+        preferred_element_type=jnp.float32,
+    )
     partial = partial.astype(jnp.bfloat16).reshape(dp_count, out_rows, col_half)
     partial = lax.all_to_all(partial, "dp", split_axis=0, concat_axis=0, tiled=True)
     weight_half = jnp.sum(partial.astype(jnp.float32), axis=0)

time: 118 us -> 117 us (level)
  matrix products: 4.93 us -> 3.48 us
    dot_general x4 -> x1, matrix products: 1.9 us -> 0.45 us  [local(): lax.dot_general(jnp.concatenate([mixed_parts, other_parts], axis=0), jnp....]
  transfers between devices with their start and end apart: 4 -> 4, of which waited for: 2 -> 3; matrix products, arithmetic and copies ran while one was open for 5% -> 4% of each run, Pallas kernels for 0% -> 0%
where the time goes in v12:
time: 117 us
  blocking collectives  61.9 us (53%)
  waiting for transfers between devices  25.3 us (22%)
  starting transfers between devices  16.8 us (14%)
  other arithmetic  4.68 us (4%)
  matrix products  3.48 us (3%)
  Pallas kernels  2.62 us (2%)
    all_to_all x1, blocking collectives, local(): lax.all_to_all(partial, 'dp', split_axis=0, concat_axis=0, tiled=True)  34.7 us
    all_to_all x1, blocking collectives, local(): lax.all_to_all(requests, 'dp', split_axis=0, concat_axis=0, tiled=True)  27.2 us
    all_to_all x1, waiting for transfers between devices, local(): lax.all_to_all(hidden_block, 'dp', split_axis=0, concat_axis=0, tiled=True)  23.6 us
    all_to_all x1, starting transfers between devices, local(): lax.all_to_all(hidden_block, 'dp', split_axis=0, concat_axis=0, tiled=True)  6.32 us
    ppermute x1, starting transfers between devices, local(): other_parts = lax.ppermute(mixed_parts, 'group', swap)  4.97 us
    ppermute x1, starting transfers between devices, local(): other_half = lax.ppermute(weight_half, 'group', swap)  3.17 us
    pallas_call x1, Pallas kernels, local(): pl.pallas_call(send_kernel, out_shape=jax.ShapeDtypeStruct((dp_count, cap...  2.62 us
    ppermute x1, starting transfers between devices, local(): other_queries = lax.ppermute(queries, 'group', swap)  2.35 us
  transfers between devices with their start and end apart: 4, of which 3 were waited for; matrix products, arithmetic and copies ran while one was open for 4% of the time, Pallas kernels for 0%

profile of v12, /device:TPU:1, one launch (start us, length us, event | category | flops | bytes accessed | tf_op | source)
XLA Modules:
  0.0 116.6 jit_solution(3617404696737480201)
XLA Ops:
  0.6 0.0 copy-start
  0.6 0.0 copy-start.1
  0.7 0.9 broadcast_in_dim.26
  1.6 0.9 convert_reduce_fusion.1
  2.5 0.7 multiply_add_fusion.2
  3.2 0.1 select_reduce_fusion
  3.3 0.1 all_to_all.13
  3.5 27.2 %all_to_all.21 = s32[128,1,4]{2,1,0:T(1,128)} all-to-all(s32[128,1,4]{2,1,0:T(1,128)S(1)} %bitcast.25), channel_id=1, replica_groups=mesh['dp'=128,'group'=2] {'dp'}, dimensions={0} | all-to-all | bytes 4096 | tf_op jit(solution)/shard_map/all_to_all | solution.py:41
  30.7 2.6 %shard_map.68 = bf16[128,4,1024]{2,1,0:T(4,128)(2,1)} custom-call(s32[128,4]{1,0:T(8,128)} %bitcast.24, bf16[256,1024]{1,0:T(8,128)(2,1)} %hidden_ref.1), custom_call_target="tpu_custom_call" | custom-call | tf_op jit(solution)/shard_map/pallas_call | solution.py:42
  33.3 0.0 copy-start.2
  33.3 6.3 %all-to-all-start.1 = ((bf16[128,4,1024]{2,1,0:T(4,128)(2,1)}), bf16[128,4,1024]{2,1,0:T(4,128)(2,1)S(1)}, u32[]{:S(2)}, u32[]{:S(2)}) async-start(bf16[128,4,1024]{2,1,0:T(4,128)(2,1)} %shard_map.68), calls=%async_computation.1 | async-start | bytes 2097152 | tf_op jit(solution)/shard_map/all_to_all | solution.py:46
  39.6 0.0 copy-done.1
  39.6 2.4 %collective-permute-start.1 = (bf16[8,1024]{1,0:T(8,128)(2,1)S(1)}, bf16[8,1024]{1,0:T(8,128)(2,1)S(1)}, u32[]{:S(2)}, u32[]{:S(2)}) collective-permute-start(bf16[8,1024]{1,0:T(8,128)(2,1)S(1)} %copy-done.1), channel_id=1, source_target_pairs={{0,1},{1,0},{2,3},{3,2},{4,5},{5,4},{6,7},{7,6},{8,9},{9,8},{10,11... | collective-permute-start | bytes 49160 | tf_op jit(solution)/shard_map/ppermute | solution.py:85
  42.0 0.0 copy-done
  42.0 1.2 %fusion.4 = f32[8]{0:T(128)S(1)} fusion(bf16[1024,1024]{1,0:T(8,128)(2,1)S(1)} %copy-done, bf16[8,1024]{1,0:T(8,128)(2,1)S(1)} %copy-done.1, bf16[256,1024]{1,0:T(8,128)(2,1)} %hidden_ref.1, s32[]{:T(128)S(6)} %select_n.20), kind=kOutput, calls=%fused_computation.9 | convolution fusion | flops 16818168 | bytes 2129956 | tf_op jit(solution)/shard_map/dot_general | solution.py:58
  43.2 0.1 copy.19
  43.3 0.0 copy-done.2
  43.3 23.6 %all-to-all-done.1 = bf16[128,4,1024]{2,1,0:T(4,128)(2,1)S(1)} async-done(((bf16[128,4,1024]{2,1,0:T(4,128)(2,1)}), bf16[128,4,1024]{2,1,0:T(4,128)(2,1)S(1)}, u32[]{:S(2)}, u32[]{:S(2)}) %all-to-all-start.1) | async-done | bytes 1048608 | tf_op jit(solution)/shard_map/all_to_all | solution.py:46
  66.9 0.9 fusion.1
  67.8 0.7 convolution_convert_fusion.1
  68.5 0.2 fusion.23
  68.8 0.2 exponential_reduce_fusion
  69.0 0.5 multiply_subtract_fusion
  69.5 0.1 subtract_exponential_fusion
  69.6 0.1 slice_multiply_fusion
  69.6 0.1 multiply_reduce_fusion
  69.8 0.3 fusion.5
  70.0 0.8 fusion.25
  70.8 5.0 %collective-permute-start = (bf16[16,1024]{1,0:T(8,128)(2,1)S(1)}, bf16[16,1024]{1,0:T(8,128)(2,1)S(1)}, u32[]{:S(2)}, u32[]{:S(2)}) collective-permute-start(bf16[16,1024]{1,0:T(8,128)(2,1)S(1)} %pad_maximum_fusion), channel_id=1, source_target_pairs={{0,1},{1,0},{2,3},{3,2},{4,5},{5,4},{6,7},{7,6},{8,9},{9,8},{10,11... | collective-permute-start | bytes 98312 | tf_op jit(solution)/shard_map/ppermute | solution.py:84
  75.8 0.0 collective-permute-done.1
  75.8 0.9 collective-permute-done
  76.7 0.5 fusion
  77.1 34.7 %all_to_all.22 = bf16[128,8,512]{2,1,0:T(8,128)(2,1)S(1)} all-to-all(bf16[128,8,512]{2,1,0:T(8,128)(2,1)S(1)} %fusion), channel_id=1, replica_groups=mesh['dp'=128,'group'=2] {'dp'}, dimensions={0} | all-to-all | bytes 2097152 | tf_op jit(solution)/shard_map/all_to_all | solution.py:95
  111.8 0.2 convert_reduce_fusion
  112.0 3.2 %collective-permute-start.2 = (f32[8,512]{1,0:T(8,128)S(1)}, f32[8,512]{1,0:T(8,128)S(1)}, u32[]{:S(2)}, u32[]{:S(2)}) collective-permute-start(f32[8,512]{1,0:T(8,128)S(1)} %convert_reduce_fusion), channel_id=1, source_target_pairs={{0,1},{1,0},{2,3},{3,2},{4,5},{5,4},{6,7},{7,6},{8,9},{9,8},{10,11... | collective-permute-start | bytes 49160 | tf_op jit(solution)/shard_map/ppermute | solution.py:97
  115.1 0.8 collective-permute-done.2
  116.0 0.6 maximum_select_fusion
  (7 shorter events, 0.0 us)
Async XLA Ops:
  0.6 41.3 %copy-start = (bf16[1024,1024]{1,0:T(8,128)(2,1)S(1)}, bf16[1024,1024]{1,0:T(8,128)(2,1)}, u32[]{:S(2)}) copy-start(bf16[1024,1024]{1,0:T(8,128)(2,1)} %param.7) | copy-start | bytes 6291460
  0.6 39.0 %copy-start.1 = (bf16[8,1024]{1,0:T(8,128)(2,1)S(1)}, bf16[8,1024]{1,0:T(8,128)(2,1)}, u32[]{:S(2)}) copy-start(bf16[8,1024]{1,0:T(8,128)(2,1)} %param.5) | copy-start | bytes 49156
  33.3 10.0 %copy-start.2 = (s32[256,1]{0,1:T(1,128)S(1)}, s32[256,1]{0,1:T(1,128)}, u32[]{:S(2)}) copy-start(s32[256,1]{0,1:T(1,128)} %param.8) | copy-start | bytes 3076
  33.3 33.6 %all-to-all-start.1 = ((bf16[128,4,1024]{2,1,0:T(4,128)(2,1)}), bf16[128,4,1024]{2,1,0:T(4,128)(2,1)S(1)}, u32[]{:S(2)}, u32[]{:S(2)}) async-start(bf16[128,4,1024]{2,1,0:T(4,128)(2,1)} %shard_map.68), calls=%async_computation.1 | async-start | bytes 2097152 | tf_op jit(solution)/shard_map/all_to_all | solution.py:46
  39.6 36.2 %collective-permute-start.1 = (bf16[8,1024]{1,0:T(8,128)(2,1)S(1)}, bf16[8,1024]{1,0:T(8,128)(2,1)S(1)}, u32[]{:S(2)}, u32[]{:S(2)}) collective-permute-start(bf16[8,1024]{1,0:T(8,128)(2,1)S(1)} %copy-done.1), channel_id=1, source_target_pairs={{0,1},{1,0},{2,3},{3,2},{4,5},{5,4},{6,7},{7,6},{8,9},{9,8},{10,11... | collective-permute-start | bytes 49160 | tf_op jit(solution)/shard_map/ppermute | solution.py:85
  70.8 5.8 %collective-permute-start = (bf16[16,1024]{1,0:T(8,128)(2,1)S(1)}, bf16[16,1024]{1,0:T(8,128)(2,1)S(1)}, u32[]{:S(2)}, u32[]{:S(2)}) collective-permute-start(bf16[16,1024]{1,0:T(8,128)(2,1)S(1)} %pad_maximum_fusion), channel_id=1, source_target_pairs={{0,1},{1,0},{2,3},{3,2},{4,5},{5,4},{6,7},{7,6},{8,9},{9,8},{10,11... | collective-permute-start | bytes 98312 | tf_op jit(solution)/shard_map/ppermute | solution.py:84
  112.0 4.0 %collective-permute-start.2 = (f32[8,512]{1,0:T(8,128)S(1)}, f32[8,512]{1,0:T(8,128)S(1)}, u32[]{:S(2)}, u32[]{:S(2)}) collective-permute-start(f32[8,512]{1,0:T(8,128)S(1)} %convert_reduce_fusion), channel_id=1, source_target_pairs={{0,1},{1,0},{2,3},{3,2},{4,5},{5,4},{6,7},{7,6},{8,9},{9,8},{10,11... | collective-permute-start | bytes 49160 | tf_op jit(solution)/shard_map/ppermute | solution.py:97

commit v13 on v12

--- a/solution.py
+++ b/solution.py
@@ -32,8 +32,8 @@
     local_ids = neg_local.reshape(ref_count)
     ref_index = jnp.arange(ref_count, dtype=jnp.int32)
     same_owner = (owners[:, None] == owners[None, :]) & (ref_index[:, None] > ref_index[None, :])
-    slot_rank = jnp.sum(same_owner.astype(jnp.int32), axis=1)
-    position = owners * capacity + slot_rank
+    own_term = jnp.where(ref_index[:, None] == ref_index[None, :], owners[:, None] * capacity, 0)
+    position = jnp.sum(same_owner.astype(jnp.int32) + own_term, axis=1)
     slots = jnp.arange(dp_count * capacity, dtype=jnp.int32)
     requests = jnp.sum(
         jnp.where(position[:, None] == slots[None, :], local_ids[:, None], 0), axis=0

time: 117 us -> 117 us (level)
  no operation moved by 1% of the time
where the time goes in v13:
time: 117 us
  blocking collectives  61.8 us (53%)
  waiting for transfers between devices  25.3 us (22%)
  starting transfers between devices  16.7 us (14%)
  other arithmetic  4.7 us (4%)
  matrix products  3.48 us (3%)
  Pallas kernels  2.62 us (2%)
    all_to_all x1, blocking collectives, local(): lax.all_to_all(partial, 'dp', split_axis=0, concat_axis=0, tiled=True)  34.6 us
    all_to_all x1, blocking collectives, local(): lax.all_to_all(requests, 'dp', split_axis=0, concat_axis=0, tiled=True)  27.2 us
    all_to_all x1, waiting for transfers between devices, local(): lax.all_to_all(hidden_block, 'dp', split_axis=0, concat_axis=0, tiled=True)  23.6 us
    all_to_all x1, starting transfers between devices, local(): lax.all_to_all(hidden_block, 'dp', split_axis=0, concat_axis=0, tiled=True)  6.19 us
    ppermute x1, starting transfers between devices, local(): other_parts = lax.ppermute(mixed_parts, 'group', swap)  4.97 us
    ppermute x1, starting transfers between devices, local(): other_half = lax.ppermute(weight_half, 'group', swap)  3.17 us
    pallas_call x1, Pallas kernels, local(): pl.pallas_call(send_kernel, out_shape=jax.ShapeDtypeStruct((dp_count, cap...  2.62 us
    ppermute x1, starting transfers between devices, local(): other_queries = lax.ppermute(queries, 'group', swap)  2.34 us
  transfers between devices with their start and end apart: 4, of which 3 were waited for; matrix products, arithmetic and copies ran while one was open for 4% of the time, Pallas kernels for 0%

profile of v13, /device:TPU:1, one launch (start us, length us, event | category | flops | bytes accessed | tf_op | source)
XLA Modules:
  0.0 116.5 jit_solution(16459984678503053843)
XLA Ops:
  0.6 0.0 copy-start
  0.6 0.0 copy-start.1
  0.7 0.9 broadcast_in_dim.45
  1.6 0.7 broadcast_multiply_fusion.1
  2.3 1.0 add_reduce_fusion
  3.2 0.2 select_reduce_fusion
  3.4 0.1 all_to_all.13
  3.5 27.2 %all_to_all.21 = s32[128,1,4]{2,1,0:T(1,128)} all-to-all(s32[128,1,4]{2,1,0:T(1,128)S(1)} %bitcast.24), channel_id=1, replica_groups=mesh['dp'=128,'group'=2] {'dp'}, dimensions={0} | all-to-all | bytes 4096 | tf_op jit(solution)/shard_map/all_to_all | solution.py:41
  30.7 2.6 %shard_map.68 = bf16[128,4,1024]{2,1,0:T(4,128)(2,1)} custom-call(s32[128,4]{1,0:T(8,128)} %bitcast.23, bf16[256,1024]{1,0:T(8,128)(2,1)} %hidden_ref.1), custom_call_target="tpu_custom_call" | custom-call | tf_op jit(solution)/shard_map/pallas_call | solution.py:42
  33.3 6.2 %all-to-all-start.1 = ((bf16[128,4,1024]{2,1,0:T(4,128)(2,1)}), bf16[128,4,1024]{2,1,0:T(4,128)(2,1)S(1)}, u32[]{:S(2)}, u32[]{:S(2)}) async-start(bf16[128,4,1024]{2,1,0:T(4,128)(2,1)} %shard_map.68), calls=%async_computation.1 | async-start | bytes 2097152 | tf_op jit(solution)/shard_map/all_to_all | solution.py:46
  39.5 0.0 copy-done.1
  39.5 2.3 %collective-permute-start.1 = (bf16[8,1024]{1,0:T(8,128)(2,1)S(1)}, bf16[8,1024]{1,0:T(8,128)(2,1)S(1)}, u32[]{:S(2)}, u32[]{:S(2)}) collective-permute-start(bf16[8,1024]{1,0:T(8,128)(2,1)S(1)} %copy-done.1), channel_id=1, source_target_pairs={{0,1},{1,0},{2,3},{3,2},{4,5},{5,4},{6,7},{7,6},{8,9},{9,8},{10,11... | collective-permute-start | bytes 49160 | tf_op jit(solution)/shard_map/ppermute | solution.py:85
  41.9 0.0 copy-done
  41.9 1.2 %fusion.4 = f32[8]{0:T(128)S(1)} fusion(bf16[1024,1024]{1,0:T(8,128)(2,1)S(1)} %copy-done, bf16[8,1024]{1,0:T(8,128)(2,1)S(1)} %copy-done.1, bf16[256,1024]{1,0:T(8,128)(2,1)} %hidden_ref.1, s32[]{:T(128)S(6)} %select_n.24), kind=kOutput, calls=%fused_computation.9 | convolution fusion | flops 16818168 | bytes 2129956 | tf_op jit(solution)/shard_map/dot_general | solution.py:58
  43.1 0.1 copy.19
  43.2 23.6 %all-to-all-done.1 = bf16[128,4,1024]{2,1,0:T(4,128)(2,1)S(1)} async-done(((bf16[128,4,1024]{2,1,0:T(4,128)(2,1)}), bf16[128,4,1024]{2,1,0:T(4,128)(2,1)S(1)}, u32[]{:S(2)}, u32[]{:S(2)}) %all-to-all-start.1) | async-done | bytes 1048608 | tf_op jit(solution)/shard_map/all_to_all | solution.py:46
  66.8 0.9 fusion.1
  67.7 0.7 convolution_convert_fusion.1
  68.4 0.2 fusion.23
  68.7 0.2 exponential_reduce_fusion
  68.9 0.5 multiply_subtract_fusion
  69.4 0.1 subtract_exponential_fusion
  69.5 0.1 slice_multiply_fusion
  69.5 0.1 multiply_reduce_fusion
  69.7 0.3 fusion.5
  69.9 0.8 fusion.25
  70.7 5.0 %collective-permute-start = (bf16[16,1024]{1,0:T(8,128)(2,1)S(1)}, bf16[16,1024]{1,0:T(8,128)(2,1)S(1)}, u32[]{:S(2)}, u32[]{:S(2)}) collective-permute-start(bf16[16,1024]{1,0:T(8,128)(2,1)S(1)} %pad_maximum_fusion), channel_id=1, source_target_pairs={{0,1},{1,0},{2,3},{3,2},{4,5},{5,4},{6,7},{7,6},{8,9},{9,8},{10,11... | collective-permute-start | bytes 98312 | tf_op jit(solution)/shard_map/ppermute | solution.py:84
  75.7 0.0 collective-permute-done.1
  75.7 0.9 collective-permute-done
  76.6 0.5 fusion
  77.0 34.6 %all_to_all.22 = bf16[128,8,512]{2,1,0:T(8,128)(2,1)S(1)} all-to-all(bf16[128,8,512]{2,1,0:T(8,128)(2,1)S(1)} %fusion), channel_id=1, replica_groups=mesh['dp'=128,'group'=2] {'dp'}, dimensions={0} | all-to-all | bytes 2097152 | tf_op jit(solution)/shard_map/all_to_all | solution.py:95
  111.7 0.2 convert_reduce_fusion
  111.9 3.2 %collective-permute-start.2 = (f32[8,512]{1,0:T(8,128)S(1)}, f32[8,512]{1,0:T(8,128)S(1)}, u32[]{:S(2)}, u32[]{:S(2)}) collective-permute-start(f32[8,512]{1,0:T(8,128)S(1)} %convert_reduce_fusion), channel_id=1, source_target_pairs={{0,1},{1,0},{2,3},{3,2},{4,5},{5,4},{6,7},{7,6},{8,9},{9,8},{10,11... | collective-permute-start | bytes 49160 | tf_op jit(solution)/shard_map/ppermute | solution.py:97
  115.0 0.8 collective-permute-done.2
  115.9 0.6 maximum_select_fusion
  (6 shorter events, 0.0 us)
Async XLA Ops:
  0.6 41.2 %copy-start = (bf16[1024,1024]{1,0:T(8,128)(2,1)S(1)}, bf16[1024,1024]{1,0:T(8,128)(2,1)}, u32[]{:S(2)}) copy-start(bf16[1024,1024]{1,0:T(8,128)(2,1)} %param.7) | copy-start | bytes 6291460
  0.6 38.9 %copy-start.1 = (bf16[8,1024]{1,0:T(8,128)(2,1)S(1)}, bf16[8,1024]{1,0:T(8,128)(2,1)}, u32[]{:S(2)}) copy-start(bf16[8,1024]{1,0:T(8,128)(2,1)} %param.5) | copy-start | bytes 49156
  33.3 33.5 %all-to-all-start.1 = ((bf16[128,4,1024]{2,1,0:T(4,128)(2,1)}), bf16[128,4,1024]{2,1,0:T(4,128)(2,1)S(1)}, u32[]{:S(2)}, u32[]{:S(2)}) async-start(bf16[128,4,1024]{2,1,0:T(4,128)(2,1)} %shard_map.68), calls=%async_computation.1 | async-start | bytes 2097152 | tf_op jit(solution)/shard_map/all_to_all | solution.py:46
  39.5 36.2 %collective-permute-start.1 = (bf16[8,1024]{1,0:T(8,128)(2,1)S(1)}, bf16[8,1024]{1,0:T(8,128)(2,1)S(1)}, u32[]{:S(2)}, u32[]{:S(2)}) collective-permute-start(bf16[8,1024]{1,0:T(8,128)(2,1)S(1)} %copy-done.1), channel_id=1, source_target_pairs={{0,1},{1,0},{2,3},{3,2},{4,5},{5,4},{6,7},{7,6},{8,9},{9,8},{10,11... | collective-permute-start | bytes 49160 | tf_op jit(solution)/shard_map/ppermute | solution.py:85
  70.7 5.8 %collective-permute-start = (bf16[16,1024]{1,0:T(8,128)(2,1)S(1)}, bf16[16,1024]{1,0:T(8,128)(2,1)S(1)}, u32[]{:S(2)}, u32[]{:S(2)}) collective-permute-start(bf16[16,1024]{1,0:T(8,128)(2,1)S(1)} %pad_maximum_fusion), channel_id=1, source_target_pairs={{0,1},{1,0},{2,3},{3,2},{4,5},{5,4},{6,7},{7,6},{8,9},{9,8},{10,11... | collective-permute-start | bytes 98312 | tf_op jit(solution)/shard_map/ppermute | solution.py:84
  111.9 4.0 %collective-permute-start.2 = (f32[8,512]{1,0:T(8,128)S(1)}, f32[8,512]{1,0:T(8,128)S(1)}, u32[]{:S(2)}, u32[]{:S(2)}) collective-permute-start(f32[8,512]{1,0:T(8,128)S(1)} %convert_reduce_fusion), channel_id=1, source_target_pairs={{0,1},{1,0},{2,3},{3,2},{4,5},{5,4},{6,7},{7,6},{8,9},{9,8},{10,11... | collective-permute-start | bytes 49160 | tf_op jit(solution)/shard_map/ppermute | solution.py:97

commit v14 on v12

--- a/solution.py
+++ b/solution.py
@@ -48,6 +48,7 @@
         position[:, None, None]
         == (jnp.arange(dp_count * capacity, dtype=jnp.int32).reshape(1, dp_count, capacity))
     ).astype(jnp.bfloat16)
+    pick_back = lax.optimization_barrier(pick_back)
     neg_hidden = jnp.einsum(
         "rkc,kcd->rd", pick_back, returned_hidden, preferred_element_type=jnp.float32
     ).astype(jnp.bfloat16)

time: 117 us -> 117 us (level)
  transfers between devices with their start and end apart: 4 -> 4, of which waited for: 3 -> 3; matrix products, arithmetic and copies ran while one was open for 4% -> 5% of each run, Pallas kernels for 0% -> 0%
where the time goes in v14:
time: 117 us; the launch traced here: 116 us
  blocking collectives  61.9 us (53%)
  waiting for transfers between devices  25.2 us (22%)
  starting transfers between devices  16.7 us (14%)
  other arithmetic  4.89 us (4%)
  matrix products  3.43 us (3%)
  Pallas kernels  2.62 us (2%)
    all_to_all x1, blocking collectives, local(): lax.all_to_all(partial, 'dp', split_axis=0, concat_axis=0, tiled=True)  34.7 us
    all_to_all x1, blocking collectives, local(): lax.all_to_all(requests, 'dp', split_axis=0, concat_axis=0, tiled=True)  27.2 us
    all_to_all x1, waiting for transfers between devices, local(): lax.all_to_all(hidden_block, 'dp', split_axis=0, concat_axis=0, tiled=True)  23.5 us
    all_to_all x1, starting transfers between devices, local(): lax.all_to_all(hidden_block, 'dp', split_axis=0, concat_axis=0, tiled=True)  6.19 us
    ppermute x1, starting transfers between devices, local(): other_parts = lax.ppermute(mixed_parts, 'group', swap)  4.96 us
    ppermute x1, starting transfers between devices, local(): other_half = lax.ppermute(weight_half, 'group', swap)  3.16 us
    pallas_call x1, Pallas kernels, local(): pl.pallas_call(send_kernel, out_shape=jax.ShapeDtypeStruct((dp_count, cap...  2.62 us
    ppermute x1, starting transfers between devices, local(): other_queries = lax.ppermute(queries, 'group', swap)  2.34 us
  transfers between devices with their start and end apart: 4, of which 3 were waited for; matrix products, arithmetic and copies ran while one was open for 5% of the time, Pallas kernels for 0%

profile of v14, /device:TPU:1, one launch (start us, length us, event | category | flops | bytes accessed | tf_op | source)
XLA Modules:
  0.0 116.4 jit_solution(5058094307710673658)
XLA Ops:
  0.6 0.0 copy-start
  0.6 0.0 copy-start.2
  0.7 0.0 copy-start.1
  0.7 1.0 convert_reduce_fusion.1
  1.7 0.8 broadcast_in_dim.26
  2.5 0.7 multiply_add_fusion.2
  3.2 0.1 select_reduce_fusion
  3.3 0.1 all_to_all.13
  3.4 27.2 %all_to_all.21 = s32[128,1,4]{2,1,0:T(1,128)} all-to-all(s32[128,1,4]{2,1,0:T(1,128)S(1)} %bitcast.26), channel_id=1, replica_groups=mesh['dp'=128,'group'=2] {'dp'}, dimensions={0} | all-to-all | bytes 4096 | tf_op jit(solution)/shard_map/all_to_all | solution.py:41
  30.6 2.6 %shard_map.68 = bf16[128,4,1024]{2,1,0:T(4,128)(2,1)} custom-call(s32[128,4]{1,0:T(8,128)} %bitcast.25, bf16[256,1024]{1,0:T(8,128)(2,1)} %hidden_ref.1), custom_call_target="tpu_custom_call" | custom-call | tf_op jit(solution)/shard_map/pallas_call | solution.py:42
  33.2 6.2 %all-to-all-start.1 = ((bf16[128,4,1024]{2,1,0:T(4,128)(2,1)}), bf16[128,4,1024]{2,1,0:T(4,128)(2,1)S(1)}, u32[]{:S(2)}, u32[]{:S(2)}) async-start(bf16[128,4,1024]{2,1,0:T(4,128)(2,1)} %shard_map.68), calls=%async_computation.1 | async-start | bytes 2097152 | tf_op jit(solution)/shard_map/all_to_all | solution.py:46
  39.4 0.0 copy-done.1
  39.4 2.3 %collective-permute-start.1 = (bf16[8,1024]{1,0:T(8,128)(2,1)S(1)}, bf16[8,1024]{1,0:T(8,128)(2,1)S(1)}, u32[]{:S(2)}, u32[]{:S(2)}) collective-permute-start(bf16[8,1024]{1,0:T(8,128)(2,1)S(1)} %copy-done.1), channel_id=1, source_target_pairs={{0,1},{1,0},{2,3},{3,2},{4,5},{5,4},{6,7},{7,6},{8,9},{9,8},{10,11... | collective-permute-start | bytes 49160 | tf_op jit(solution)/shard_map/ppermute | solution.py:86
  41.8 0.0 copy-done.2
  41.8 0.1 compare_convert_fusion
  41.9 0.0 copy-done
  41.9 1.2 %fusion.4 = f32[8]{0:T(128)S(1)} fusion(bf16[1024,1024]{1,0:T(8,128)(2,1)S(1)} %copy-done, bf16[8,1024]{1,0:T(8,128)(2,1)S(1)} %copy-done.1, bf16[256,1024]{1,0:T(8,128)(2,1)} %hidden_ref.1, s32[]{:T(128)S(6)} %select_n.20), kind=kOutput, calls=%fused_computation.9 | convolution fusion | flops 16818168 | bytes 2129956 | tf_op jit(solution)/shard_map/dot_general | solution.py:59
  43.2 0.1 copy.19
  43.3 23.5 %all-to-all-done.1 = bf16[128,4,1024]{2,1,0:T(4,128)(2,1)S(1)} async-done(((bf16[128,4,1024]{2,1,0:T(4,128)(2,1)}), bf16[128,4,1024]{2,1,0:T(4,128)(2,1)S(1)}, u32[]{:S(2)}, u32[]{:S(2)}) %all-to-all-start.1) | async-done | bytes 1048608 | tf_op jit(solution)/shard_map/all_to_all | solution.py:46
  66.7 0.8 fusion.1
  67.6 0.7 convolution_convert_fusion.1
  68.3 0.2 fusion.20
  68.5 0.2 exponential_reduce_fusion
  68.7 0.5 multiply_subtract_fusion
  69.3 0.1 subtract_exponential_fusion
  69.3 0.1 slice_multiply_fusion
  69.4 0.1 multiply_reduce_fusion
  69.5 0.3 fusion.5
  69.8 0.8 fusion.22
  70.6 5.0 %collective-permute-start = (bf16[16,1024]{1,0:T(8,128)(2,1)S(1)}, bf16[16,1024]{1,0:T(8,128)(2,1)S(1)}, u32[]{:S(2)}, u32[]{:S(2)}) collective-permute-start(bf16[16,1024]{1,0:T(8,128)(2,1)S(1)} %pad_maximum_fusion), channel_id=1, source_target_pairs={{0,1},{1,0},{2,3},{3,2},{4,5},{5,4},{6,7},{7,6},{8,9},{9,8},{10,11... | collective-permute-start | bytes 98312 | tf_op jit(solution)/shard_map/ppermute | solution.py:85
  75.6 0.0 collective-permute-done.1
  75.6 0.9 collective-permute-done
  76.4 0.5 fusion
  76.9 34.7 %all_to_all.22 = bf16[128,8,512]{2,1,0:T(8,128)(2,1)S(1)} all-to-all(bf16[128,8,512]{2,1,0:T(8,128)(2,1)S(1)} %fusion), channel_id=1, replica_groups=mesh['dp'=128,'group'=2] {'dp'}, dimensions={0} | all-to-all | bytes 2097152 | tf_op jit(solution)/shard_map/all_to_all | solution.py:96
  111.6 0.2 convert_reduce_fusion
  111.8 3.2 %collective-permute-start.2 = (f32[8,512]{1,0:T(8,128)S(1)}, f32[8,512]{1,0:T(8,128)S(1)}, u32[]{:S(2)}, u32[]{:S(2)}) collective-permute-start(f32[8,512]{1,0:T(8,128)S(1)} %convert_reduce_fusion), channel_id=1, source_target_pairs={{0,1},{1,0},{2,3},{3,2},{4,5},{5,4},{6,7},{7,6},{8,9},{9,8},{10,11... | collective-permute-start | bytes 49160 | tf_op jit(solution)/shard_map/ppermute | solution.py:98
  114.9 0.8 collective-permute-done.2
  115.8 0.6 maximum_select_fusion
  (7 shorter events, 0.0 us)
Async XLA Ops:
  0.6 41.3 %copy-start = (bf16[1024,1024]{1,0:T(8,128)(2,1)S(1)}, bf16[1024,1024]{1,0:T(8,128)(2,1)}, u32[]{:S(2)}) copy-start(bf16[1024,1024]{1,0:T(8,128)(2,1)} %param.7) | copy-start | bytes 6291460
  0.6 41.2 %copy-start.2 = (s32[256,1]{0,1:T(1,128)S(1)}, s32[256,1]{0,1:T(1,128)}, u32[]{:S(2)}) copy-start(s32[256,1]{0,1:T(1,128)} %param.8) | copy-start | bytes 3076
  0.7 38.8 %copy-start.1 = (bf16[8,1024]{1,0:T(8,128)(2,1)S(1)}, bf16[8,1024]{1,0:T(8,128)(2,1)}, u32[]{:S(2)}) copy-start(bf16[8,1024]{1,0:T(8,128)(2,1)} %param.5) | copy-start | bytes 49156
  33.2 33.5 %all-to-all-start.1 = ((bf16[128,4,1024]{2,1,0:T(4,128)(2,1)}), bf16[128,4,1024]{2,1,0:T(4,128)(2,1)S(1)}, u32[]{:S(2)}, u32[]{:S(2)}) async-start(bf16[128,4,1024]{2,1,0:T(4,128)(2,1)} %shard_map.68), calls=%async_computation.1 | async-start | bytes 2097152 | tf_op jit(solution)/shard_map/all_to_all | solution.py:46
  39.4 36.1 %collective-permute-start.1 = (bf16[8,1024]{1,0:T(8,128)(2,1)S(1)}, bf16[8,1024]{1,0:T(8,128)(2,1)S(1)}, u32[]{:S(2)}, u32[]{:S(2)}) collective-permute-start(bf16[8,1024]{1,0:T(8,128)(2,1)S(1)} %copy-done.1), channel_id=1, source_target_pairs={{0,1},{1,0},{2,3},{3,2},{4,5},{5,4},{6,7},{7,6},{8,9},{9,8},{10,11... | collective-permute-start | bytes 49160 | tf_op jit(solution)/shard_map/ppermute | solution.py:86
  70.6 5.8 %collective-permute-start = (bf16[16,1024]{1,0:T(8,128)(2,1)S(1)}, bf16[16,1024]{1,0:T(8,128)(2,1)S(1)}, u32[]{:S(2)}, u32[]{:S(2)}) collective-permute-start(bf16[16,1024]{1,0:T(8,128)(2,1)S(1)} %pad_maximum_fusion), channel_id=1, source_target_pairs={{0,1},{1,0},{2,3},{3,2},{4,5},{5,4},{6,7},{7,6},{8,9},{9,8},{10,11... | collective-permute-start | bytes 98312 | tf_op jit(solution)/shard_map/ppermute | solution.py:85
  111.8 4.0 %collective-permute-start.2 = (f32[8,512]{1,0:T(8,128)S(1)}, f32[8,512]{1,0:T(8,128)S(1)}, u32[]{:S(2)}, u32[]{:S(2)}) collective-permute-start(f32[8,512]{1,0:T(8,128)S(1)} %convert_reduce_fusion), channel_id=1, source_target_pairs={{0,1},{1,0},{2,3},{3,2},{4,5},{5,4},{6,7},{7,6},{8,9},{9,8},{10,11... | collective-permute-start | bytes 49160 | tf_op jit(solution)/shard_map/ppermute | solution.py:98

commit v15 on v12

--- a/solution.py
+++ b/solution.py
@@ -91,9 +91,9 @@
         (((0,), (0,)), ((), ())),
         preferred_element_type=jnp.float32,
     )
-    partial = partial.astype(jnp.bfloat16).reshape(dp_count, out_rows, col_half)
+    partial = partial.astype(jnp.bfloat16).reshape(dp_count, out_rows // 2, 2 * col_half)
     partial = lax.all_to_all(partial, "dp", split_axis=0, concat_axis=0, tiled=True)
-    weight_half = jnp.sum(partial.astype(jnp.float32), axis=0)
+    weight_half = jnp.sum(partial.astype(jnp.float32), axis=0).reshape(out_rows, col_half)
     other_half = lax.ppermute(weight_half, "group", swap)
     weight_grad = jnp.where(
         group_pos == 0,

time: 117 us -> 120 us (1.026)
  local copies, waits for them, and re-layouts: 1.13 us -> 2.65 us
  blocking collectives: 61.9 us -> 63.2 us
    reshape x0 -> x2, local copies, waits for them, and re-layouts: none -> 1.52 us  [the longest x1 1.51 us: local(): partial.astype(jnp.bfloat16).reshape(dp_count, out_rows // 2, 2 * col_half)]
    all_to_all x1, blocking collectives: 34.7 us -> 36 us  [local(): lax.all_to_all(partial, 'dp', split_axis=0, concat_axis=0, tiled=True)]
where the time goes in v15:
time: 120 us; the launch traced here: 119 us
  blocking collectives  63.2 us (53%)
  waiting for transfers between devices  25.3 us (21%)
  starting transfers between devices  16.4 us (14%)
  other arithmetic  4.96 us (4%)
  matrix products  3.48 us (3%)
  local copies, waits for them, and re-layouts  2.65 us (2%)
  Pallas kernels  2.62 us (2%)
    all_to_all x1, blocking collectives, local(): lax.all_to_all(partial, 'dp', split_axis=0, concat_axis=0, tiled=True)  36 us
    all_to_all x1, blocking collectives, local(): lax.all_to_all(requests, 'dp', split_axis=0, concat_axis=0, tiled=True)  27.2 us
    all_to_all x1, waiting for transfers between devices, local(): lax.all_to_all(hidden_block, 'dp', split_axis=0, concat_axis=0, tiled=True)  23.6 us
    all_to_all x1, starting transfers between devices, local(): lax.all_to_all(hidden_block, 'dp', split_axis=0, concat_axis=0, tiled=True)  6.32 us
    ppermute x1, starting transfers between devices, local(): other_parts = lax.ppermute(mixed_parts, 'group', swap)  4.97 us
    ppermute x1, starting transfers between devices, local(): other_half = lax.ppermute(weight_half, 'group', swap)  2.72 us
    pallas_call x1, Pallas kernels, local(): pl.pallas_call(send_kernel, out_shape=jax.ShapeDtypeStruct((dp_count, cap...  2.62 us
  transfers between devices with their start and end apart: 4, of which 3 were waited for; matrix products, arithmetic and copies ran while one was open for 4% of the time, Pallas kernels for 0%

profile of v15, /device:TPU:1, one launch (start us, length us, event | category | flops | bytes accessed | tf_op | source)
XLA Modules:
  0.0 119.3 jit_solution(15804955536779544582)
XLA Ops:
  0.6 0.0 copy-start
  0.6 0.0 copy-start.1
  0.7 0.9 broadcast_in_dim.26
  1.6 0.9 convert_reduce_fusion.1
  2.5 0.7 multiply_add_fusion.2
  3.2 0.1 select_reduce_fusion
  3.3 0.1 all_to_all.13
  3.5 27.2 %all_to_all.21 = s32[128,1,4]{2,1,0:T(1,128)} all-to-all(s32[128,1,4]{2,1,0:T(1,128)S(1)} %bitcast.23), channel_id=1, replica_groups=mesh['dp'=128,'group'=2] {'dp'}, dimensions={0} | all-to-all | bytes 4096 | tf_op jit(solution)/shard_map/all_to_all | solution.py:41
  30.7 2.6 %shard_map.68 = bf16[128,4,1024]{2,1,0:T(4,128)(2,1)} custom-call(s32[128,4]{1,0:T(8,128)} %bitcast.22, bf16[256,1024]{1,0:T(8,128)(2,1)} %hidden_ref.1), custom_call_target="tpu_custom_call" | custom-call | tf_op jit(solution)/shard_map/pallas_call | solution.py:42
  33.3 0.0 copy-start.2
  33.3 6.3 %all-to-all-start.1 = ((bf16[128,4,1024]{2,1,0:T(4,128)(2,1)}), bf16[128,4,1024]{2,1,0:T(4,128)(2,1)S(1)}, u32[]{:S(2)}, u32[]{:S(2)}) async-start(bf16[128,4,1024]{2,1,0:T(4,128)(2,1)} %shard_map.68), calls=%async_computation.1 | async-start | bytes 2097152 | tf_op jit(solution)/shard_map/all_to_all | solution.py:46
  39.6 0.0 copy-done.1
  39.6 2.4 %collective-permute-start.1 = (bf16[8,1024]{1,0:T(8,128)(2,1)S(1)}, bf16[8,1024]{1,0:T(8,128)(2,1)S(1)}, u32[]{:S(2)}, u32[]{:S(2)}) collective-permute-start(bf16[8,1024]{1,0:T(8,128)(2,1)S(1)} %copy-done.1), channel_id=1, source_target_pairs={{0,1},{1,0},{2,3},{3,2},{4,5},{5,4},{6,7},{7,6},{8,9},{9,8},{10,11... | collective-permute-start | bytes 49160 | tf_op jit(solution)/shard_map/ppermute | solution.py:85
  42.0 0.0 copy-done
  42.0 1.2 %fusion.3 = f32[8]{0:T(128)S(1)} fusion(bf16[1024,1024]{1,0:T(8,128)(2,1)S(1)} %copy-done, bf16[8,1024]{1,0:T(8,128)(2,1)S(1)} %copy-done.1, bf16[256,1024]{1,0:T(8,128)(2,1)} %hidden_ref.1, s32[]{:T(128)S(6)} %select_n.20), kind=kOutput, calls=%fused_computation.8 | convolution fusion | flops 16818168 | bytes 2129956 | tf_op jit(solution)/shard_map/dot_general | solution.py:58
  43.2 0.1 copy.19
  43.3 0.0 copy-done.2
  43.3 23.6 %all-to-all-done.1 = bf16[128,4,1024]{2,1,0:T(4,128)(2,1)S(1)} async-done(((bf16[128,4,1024]{2,1,0:T(4,128)(2,1)}), bf16[128,4,1024]{2,1,0:T(4,128)(2,1)S(1)}, u32[]{:S(2)}, u32[]{:S(2)}) %all-to-all-start.1) | async-done | bytes 1048608 | tf_op jit(solution)/shard_map/all_to_all | solution.py:46
  66.9 0.9 fusion
  67.8 0.7 convolution_convert_fusion.1
  68.5 0.2 fusion.22
  68.8 0.2 exponential_reduce_fusion
  69.0 0.5 multiply_subtract_fusion
  69.5 0.1 subtract_exponential_fusion
  69.6 0.1 slice_multiply_fusion
  69.6 0.1 multiply_reduce_fusion
  69.8 0.3 fusion.4
  70.0 0.8 fusion.24
  70.8 5.0 %collective-permute-start = (bf16[16,1024]{1,0:T(8,128)(2,1)S(1)}, bf16[16,1024]{1,0:T(8,128)(2,1)S(1)}, u32[]{:S(2)}, u32[]{:S(2)}) collective-permute-start(bf16[16,1024]{1,0:T(8,128)(2,1)S(1)} %pad_maximum_fusion), channel_id=1, source_target_pairs={{0,1},{1,0},{2,3},{3,2},{4,5},{5,4},{6,7},{7,6},{8,9},{9,8},{10,11... | collective-permute-start | bytes 98312 | tf_op jit(solution)/shard_map/ppermute | solution.py:84
  75.8 0.0 collective-permute-done.1
  75.8 0.9 collective-permute-done
  76.7 0.5 convolution_convert_fusion
  77.1 1.5 %reshape.60 = bf16[128,4,1024]{2,1,0:T(4,128)(2,1)} reshape(bf16[1024,512]{1,0:T(8,128)(2,1)S(1)} %convolution_convert_fusion) | data formatting | bytes 2097152 | tf_op jit(solution)/shard_map/reshape | solution.py:94
  78.6 36.0 %all_to_all.22 = bf16[128,4,1024]{2,1,0:T(4,128)(2,1)S(1)} all-to-all(bf16[128,4,1024]{2,1,0:T(4,128)(2,1)} %reshape.60), channel_id=1, replica_groups=mesh['dp'=128,'group'=2] {'dp'}, dimensions={0} | all-to-all | bytes 2097152 | tf_op jit(solution)/shard_map/all_to_all | solution.py:95
  114.7 0.5 convert_reduce_fusion
  115.1 2.7 %collective-permute-start.2 = (f32[8,512]{1,0:T(8,128)S(1)}, f32[8,512]{1,0:T(8,128)S(1)}, u32[]{:S(2)}, u32[]{:S(2)}) collective-permute-start(f32[8,512]{1,0:T(8,128)S(1)} %reshape.61), channel_id=1, source_target_pairs={{0,1},{1,0},{2,3},{3,2},{4,5},{5,4},{6,7},{7,6},{8,9},{9,8},{10,11... | collective-permute-start | bytes 49160 | tf_op jit(solution)/shard_map/ppermute | solution.py:97
  117.9 0.8 collective-permute-done.2
  118.7 0.6 maximum_select_fusion
  (8 shorter events, 0.0 us)
Async XLA Ops:
  0.6 41.3 %copy-start = (bf16[1024,1024]{1,0:T(8,128)(2,1)S(1)}, bf16[1024,1024]{1,0:T(8,128)(2,1)}, u32[]{:S(2)}) copy-start(bf16[1024,1024]{1,0:T(8,128)(2,1)} %param.7) | copy-start | bytes 6291460
  0.6 39.0 %copy-start.1 = (bf16[8,1024]{1,0:T(8,128)(2,1)S(1)}, bf16[8,1024]{1,0:T(8,128)(2,1)}, u32[]{:S(2)}) copy-start(bf16[8,1024]{1,0:T(8,128)(2,1)} %param.5) | copy-start | bytes 49156
  33.3 10.0 %copy-start.2 = (s32[256,1]{0,1:T(1,128)S(1)}, s32[256,1]{0,1:T(1,128)}, u32[]{:S(2)}) copy-start(s32[256,1]{0,1:T(1,128)} %param.8) | copy-start | bytes 3076
  33.3 33.6 %all-to-all-start.1 = ((bf16[128,4,1024]{2,1,0:T(4,128)(2,1)}), bf16[128,4,1024]{2,1,0:T(4,128)(2,1)S(1)}, u32[]{:S(2)}, u32[]{:S(2)}) async-start(bf16[128,4,1024]{2,1,0:T(4,128)(2,1)} %shard_map.68), calls=%async_computation.1 | async-start | bytes 2097152 | tf_op jit(solution)/shard_map/all_to_all | solution.py:46
  39.6 36.2 %collective-permute-start.1 = (bf16[8,1024]{1,0:T(8,128)(2,1)S(1)}, bf16[8,1024]{1,0:T(8,128)(2,1)S(1)}, u32[]{:S(2)}, u32[]{:S(2)}) collective-permute-start(bf16[8,1024]{1,0:T(8,128)(2,1)S(1)} %copy-done.1), channel_id=1, source_target_pairs={{0,1},{1,0},{2,3},{3,2},{4,5},{5,4},{6,7},{7,6},{8,9},{9,8},{10,11... | collective-permute-start | bytes 49160 | tf_op jit(solution)/shard_map/ppermute | solution.py:85
  70.8 5.8 %collective-permute-start = (bf16[16,1024]{1,0:T(8,128)(2,1)S(1)}, bf16[16,1024]{1,0:T(8,128)(2,1)S(1)}, u32[]{:S(2)}, u32[]{:S(2)}) collective-permute-start(bf16[16,1024]{1,0:T(8,128)(2,1)S(1)} %pad_maximum_fusion), channel_id=1, source_target_pairs={{0,1},{1,0},{2,3},{3,2},{4,5},{5,4},{6,7},{7,6},{8,9},{9,8},{10,11... | collective-permute-start | bytes 98312 | tf_op jit(solution)/shard_map/ppermute | solution.py:84
  115.1 3.6 %collective-permute-start.2 = (f32[8,512]{1,0:T(8,128)S(1)}, f32[8,512]{1,0:T(8,128)S(1)}, u32[]{:S(2)}, u32[]{:S(2)}) collective-permute-start(f32[8,512]{1,0:T(8,128)S(1)} %reshape.61), channel_id=1, source_target_pairs={{0,1},{1,0},{2,3},{3,2},{4,5},{5,4},{6,7},{7,6},{8,9},{9,8},{10,11... | collective-permute-start | bytes 49160 | tf_op jit(solution)/shard_map/ppermute | solution.py:97

commit v16 on v12

--- a/solution.py
+++ b/solution.py
@@ -65,12 +65,13 @@
         jnp.einsum("qd,qjd->qj", queries, neg_keys, preferred_element_type=jnp.float32)
         * score_scale
     )
-    logits = jnp.concatenate([pos_logit[:, None], neg_logit], axis=1)
-    log_total = jnp.log(jnp.sum(jnp.exp(logits), axis=1))
-    query_loss = log_total - pos_logit
-    soft_prob = jnp.exp(logits - log_total[:, None])
-    neg_coef = soft_prob[:, 1:] * score_scale
-    pos_coef = (soft_prob[:, 0] - 1.0) * score_scale
+    pos_exp = jnp.exp(pos_logit)
+    neg_exp = jnp.exp(neg_logit)
+    total = pos_exp + jnp.sum(neg_exp, axis=1)
+    query_loss = jnp.log(total) - pos_logit
+    scaled = score_scale / total
+    neg_coef = neg_exp * scaled[:, None]
+    pos_coef = pos_exp * scaled - score_scale
     mixed = jnp.sum(
         neg_coef[:, :, None] * neg_hidden.reshape(query_rows, neg_count, width).astype(jnp.float32),
         axis=1,

time: 117 us -> 117 us (level)
  no operation moved by 1% of the time
where the time goes in v16:
time: 117 us; the launch traced here: 116 us
  blocking collectives  61.9 us (53%)
  waiting for transfers between devices  25.4 us (22%)
  starting transfers between devices  16.8 us (14%)
  other arithmetic  4.4 us (4%)
  matrix products  3.49 us (3%)
  Pallas kernels  2.62 us (2%)
    all_to_all x1, blocking collectives, local(): lax.all_to_all(partial, 'dp', split_axis=0, concat_axis=0, tiled=True)  34.7 us
    all_to_all x1, blocking collectives, local(): lax.all_to_all(requests, 'dp', split_axis=0, concat_axis=0, tiled=True)  27.2 us
    all_to_all x1, waiting for transfers between devices, local(): lax.all_to_all(hidden_block, 'dp', split_axis=0, concat_axis=0, tiled=True)  23.7 us
    all_to_all x1, starting transfers between devices, local(): lax.all_to_all(hidden_block, 'dp', split_axis=0, concat_axis=0, tiled=True)  6.32 us
    ppermute x1, starting transfers between devices, local(): other_parts = lax.ppermute(mixed_parts, 'group', swap)  4.97 us
    ppermute x1, starting transfers between devices, local(): other_half = lax.ppermute(weight_half, 'group', swap)  3.15 us
    pallas_call x1, Pallas kernels, local(): pl.pallas_call(send_kernel, out_shape=jax.ShapeDtypeStruct((dp_count, cap...  2.62 us
    ppermute x1, starting transfers between devices, local(): other_queries = lax.ppermute(queries, 'group', swap)  2.35 us
  transfers between devices with their start and end apart: 4, of which 3 were waited for; matrix products, arithmetic and copies ran while one was open for 4% of the time, Pallas kernels for 0%

profile of v16, /device:TPU:1, one launch (start us, length us, event | category | flops | bytes accessed | tf_op | source)
XLA Modules:
  0.0 116.3 jit_solution(10252859905789233175)
XLA Ops:
  0.6 0.0 copy-start
  0.6 0.0 copy-start.1
  0.7 0.9 broadcast_in_dim.14
  1.6 0.9 convert_reduce_fusion.1
  2.5 0.7 multiply_add_fusion.2
  3.2 0.1 select_reduce_fusion
  3.3 0.1 all_to_all.13
  3.5 27.2 %all_to_all.21 = s32[128,1,4]{2,1,0:T(1,128)} all-to-all(s32[128,1,4]{2,1,0:T(1,128)S(1)} %bitcast.23), channel_id=1, replica_groups=mesh['dp'=128,'group'=2] {'dp'}, dimensions={0} | all-to-all | bytes 4096 | tf_op jit(solution)/shard_map/all_to_all | solution.py:41
  30.7 2.6 %shard_map.68 = bf16[128,4,1024]{2,1,0:T(4,128)(2,1)} custom-call(s32[128,4]{1,0:T(8,128)} %bitcast.22, bf16[256,1024]{1,0:T(8,128)(2,1)} %hidden_ref.1), custom_call_target="tpu_custom_call" | custom-call | tf_op jit(solution)/shard_map/pallas_call | solution.py:42
  33.3 0.0 copy-start.2
  33.3 6.3 %all-to-all-start.1 = ((bf16[128,4,1024]{2,1,0:T(4,128)(2,1)}), bf16[128,4,1024]{2,1,0:T(4,128)(2,1)S(1)}, u32[]{:S(2)}, u32[]{:S(2)}) async-start(bf16[128,4,1024]{2,1,0:T(4,128)(2,1)} %shard_map.68), calls=%async_computation.1 | async-start | bytes 2097152 | tf_op jit(solution)/shard_map/all_to_all | solution.py:46
  39.6 0.0 copy-done.1
  39.6 2.4 %collective-permute-start.1 = (bf16[8,1024]{1,0:T(8,128)(2,1)S(1)}, bf16[8,1024]{1,0:T(8,128)(2,1)S(1)}, u32[]{:S(2)}, u32[]{:S(2)}) collective-permute-start(bf16[8,1024]{1,0:T(8,128)(2,1)S(1)} %copy-done.1), channel_id=1, source_target_pairs={{0,1},{1,0},{2,3},{3,2},{4,5},{5,4},{6,7},{7,6},{8,9},{9,8},{10,11... | collective-permute-start | bytes 49160 | tf_op jit(solution)/shard_map/ppermute | solution.py:86
  42.0 0.0 copy-done
  42.0 1.2 %fusion.4 = f32[8]{0:T(128)S(1)} fusion(bf16[1024,1024]{1,0:T(8,128)(2,1)S(1)} %copy-done, bf16[8,1024]{1,0:T(8,128)(2,1)S(1)} %copy-done.1, bf16[256,1024]{1,0:T(8,128)(2,1)} %hidden_ref.1, s32[]{:T(128)S(6)} %select_n.21), kind=kOutput, calls=%fused_computation.9 | convolution fusion | flops 16818168 | bytes 2129956 | tf_op jit(solution)/shard_map/dot_general | solution.py:58
  43.2 0.0 copy-done.2
  43.2 23.7 %all-to-all-done.1 = bf16[128,4,1024]{2,1,0:T(4,128)(2,1)S(1)} async-done(((bf16[128,4,1024]{2,1,0:T(4,128)(2,1)}), bf16[128,4,1024]{2,1,0:T(4,128)(2,1)S(1)}, u32[]{:S(2)}, u32[]{:S(2)}) %all-to-all-start.1) | async-done | bytes 1048608 | tf_op jit(solution)/shard_map/all_to_all | solution.py:46
  66.9 0.9 fusion.1
  67.8 0.7 convolution_convert_fusion.1
  68.5 0.2 fusion.23
  68.7 0.1 fusion.28
  68.9 0.5 multiply_add_fusion.4
  69.4 0.1 fusion.27
  69.5 0.3 fusion.5
  69.8 0.8 fusion.25
  70.6 5.0 %collective-permute-start = (bf16[16,1024]{1,0:T(8,128)(2,1)S(1)}, bf16[16,1024]{1,0:T(8,128)(2,1)S(1)}, u32[]{:S(2)}, u32[]{:S(2)}) collective-permute-start(bf16[16,1024]{1,0:T(8,128)(2,1)S(1)} %pad_maximum_fusion), channel_id=1, source_target_pairs={{0,1},{1,0},{2,3},{3,2},{4,5},{5,4},{6,7},{7,6},{8,9},{9,8},{10,11... | collective-permute-start | bytes 98312 | tf_op jit(solution)/shard_map/ppermute | solution.py:85
  75.5 0.0 collective-permute-done.1
  75.5 0.9 collective-permute-done
  76.4 0.5 fusion
  76.9 34.7 %all_to_all.22 = bf16[128,8,512]{2,1,0:T(8,128)(2,1)S(1)} all-to-all(bf16[128,8,512]{2,1,0:T(8,128)(2,1)S(1)} %fusion), channel_id=1, replica_groups=mesh['dp'=128,'group'=2] {'dp'}, dimensions={0} | all-to-all | bytes 2097152 | tf_op jit(solution)/shard_map/all_to_all | solution.py:96
  111.5 0.2 convert_reduce_fusion
  111.7 3.2 %collective-permute-start.2 = (f32[8,512]{1,0:T(8,128)S(1)}, f32[8,512]{1,0:T(8,128)S(1)}, u32[]{:S(2)}, u32[]{:S(2)}) collective-permute-start(f32[8,512]{1,0:T(8,128)S(1)} %convert_reduce_fusion), channel_id=1, source_target_pairs={{0,1},{1,0},{2,3},{3,2},{4,5},{5,4},{6,7},{7,6},{8,9},{9,8},{10,11... | collective-permute-start | bytes 49160 | tf_op jit(solution)/shard_map/ppermute | solution.py:98
  114.9 0.8 collective-permute-done.2
  115.7 0.6 maximum_select_fusion
  (5 shorter events, 0.0 us)
Async XLA Ops:
  0.6 41.4 %copy-start = (bf16[1024,1024]{1,0:T(8,128)(2,1)S(1)}, bf16[1024,1024]{1,0:T(8,128)(2,1)}, u32[]{:S(2)}) copy-start(bf16[1024,1024]{1,0:T(8,128)(2,1)} %param.7) | copy-start | bytes 6291460
  0.6 39.0 %copy-start.1 = (bf16[8,1024]{1,0:T(8,128)(2,1)S(1)}, bf16[8,1024]{1,0:T(8,128)(2,1)}, u32[]{:S(2)}) copy-start(bf16[8,1024]{1,0:T(8,128)(2,1)} %param.5) | copy-start | bytes 49156
  33.3 9.9 %copy-start.2 = (s32[256,1]{0,1:T(1,128)S(1)}, s32[256,1]{0,1:T(1,128)}, u32[]{:S(2)}) copy-start(s32[256,1]{0,1:T(1,128)} %param.8) | copy-start | bytes 3076
  33.3 33.6 %all-to-all-start.1 = ((bf16[128,4,1024]{2,1,0:T(4,128)(2,1)}), bf16[128,4,1024]{2,1,0:T(4,128)(2,1)S(1)}, u32[]{:S(2)}, u32[]{:S(2)}) async-start(bf16[128,4,1024]{2,1,0:T(4,128)(2,1)} %shard_map.68), calls=%async_computation.1 | async-start | bytes 2097152 | tf_op jit(solution)/shard_map/all_to_all | solution.py:46
  39.6 35.9 %collective-permute-start.1 = (bf16[8,1024]{1,0:T(8,128)(2,1)S(1)}, bf16[8,1024]{1,0:T(8,128)(2,1)S(1)}, u32[]{:S(2)}, u32[]{:S(2)}) collective-permute-start(bf16[8,1024]{1,0:T(8,128)(2,1)S(1)} %copy-done.1), channel_id=1, source_target_pairs={{0,1},{1,0},{2,3},{3,2},{4,5},{5,4},{6,7},{7,6},{8,9},{9,8},{10,11... | collective-permute-start | bytes 49160 | tf_op jit(solution)/shard_map/ppermute | solution.py:86
  70.6 5.8 %collective-permute-start = (bf16[16,1024]{1,0:T(8,128)(2,1)S(1)}, bf16[16,1024]{1,0:T(8,128)(2,1)S(1)}, u32[]{:S(2)}, u32[]{:S(2)}) collective-permute-start(bf16[16,1024]{1,0:T(8,128)(2,1)S(1)} %pad_maximum_fusion), channel_id=1, source_target_pairs={{0,1},{1,0},{2,3},{3,2},{4,5},{5,4},{6,7},{7,6},{8,9},{9,8},{10,11... | collective-permute-start | bytes 98312 | tf_op jit(solution)/shard_map/ppermute | solution.py:85
  111.7 4.0 %collective-permute-start.2 = (f32[8,512]{1,0:T(8,128)S(1)}, f32[8,512]{1,0:T(8,128)S(1)}, u32[]{:S(2)}, u32[]{:S(2)}) collective-permute-start(f32[8,512]{1,0:T(8,128)S(1)} %convert_reduce_fusion), channel_id=1, source_target_pairs={{0,1},{1,0},{2,3},{3,2},{4,5},{5,4},{6,7},{7,6},{8,9},{9,8},{10,11... | collective-permute-start | bytes 49160 | tf_op jit(solution)/shard_map/ppermute | solution.py:98

commit v17 on v16

--- a/solution.py
+++ b/solution.py
@@ -48,6 +48,7 @@
         position[:, None, None]
         == (jnp.arange(dp_count * capacity, dtype=jnp.int32).reshape(1, dp_count, capacity))
     ).astype(jnp.bfloat16)
+    pick_back = lax.optimization_barrier(pick_back)
     neg_hidden = jnp.einsum(
         "rkc,kcd->rd", pick_back, returned_hidden, preferred_element_type=jnp.float32
     ).astype(jnp.bfloat16)

time: 117 us -> 117 us (level)
  no operation moved by 1% of the time
where the time goes in v17:
time: 117 us; the launch traced here: 116 us
  blocking collectives  61.9 us (53%)
  waiting for transfers between devices  25.3 us (22%)
  starting transfers between devices  16.7 us (14%)
  other arithmetic  4.61 us (4%)
  matrix products  3.43 us (3%)
  Pallas kernels  2.62 us (2%)
    all_to_all x1, blocking collectives, local(): lax.all_to_all(partial, 'dp', split_axis=0, concat_axis=0, tiled=True)  34.7 us
    all_to_all x1, blocking collectives, local(): lax.all_to_all(requests, 'dp', split_axis=0, concat_axis=0, tiled=True)  27.2 us
    all_to_all x1, waiting for transfers between devices, local(): lax.all_to_all(hidden_block, 'dp', split_axis=0, concat_axis=0, tiled=True)  23.6 us
    all_to_all x1, starting transfers between devices, local(): lax.all_to_all(hidden_block, 'dp', split_axis=0, concat_axis=0, tiled=True)  6.19 us
    ppermute x1, starting transfers between devices, local(): other_parts = lax.ppermute(mixed_parts, 'group', swap)  4.96 us
    ppermute x1, starting transfers between devices, local(): other_half = lax.ppermute(weight_half, 'group', swap)  3.16 us
    pallas_call x1, Pallas kernels, local(): pl.pallas_call(send_kernel, out_shape=jax.ShapeDtypeStruct((dp_count, cap...  2.62 us
    ppermute x1, starting transfers between devices, local(): other_queries = lax.ppermute(queries, 'group', swap)  2.34 us
  transfers between devices with their start and end apart: 4, of which 3 were waited for; matrix products, arithmetic and copies ran while one was open for 4% of the time, Pallas kernels for 0%

profile of v17, /device:TPU:1, one launch (start us, length us, event | category | flops | bytes accessed | tf_op | source)
XLA Modules:
  0.0 116.1 jit_solution(18278627805800019392)
XLA Ops:
  0.6 0.0 copy-start
  0.6 0.0 copy-start.2
  0.7 0.0 copy-start.1
  0.7 1.0 convert_reduce_fusion.1
  1.7 0.8 broadcast_in_dim.14
  2.5 0.7 multiply_add_fusion.2
  3.2 0.1 select_reduce_fusion
  3.3 0.1 all_to_all.13
  3.4 27.2 %all_to_all.21 = s32[128,1,4]{2,1,0:T(1,128)} all-to-all(s32[128,1,4]{2,1,0:T(1,128)S(1)} %bitcast.24), channel_id=1, replica_groups=mesh['dp'=128,'group'=2] {'dp'}, dimensions={0} | all-to-all | bytes 4096 | tf_op jit(solution)/shard_map/all_to_all | solution.py:41
  30.6 2.6 %shard_map.68 = bf16[128,4,1024]{2,1,0:T(4,128)(2,1)} custom-call(s32[128,4]{1,0:T(8,128)} %bitcast.23, bf16[256,1024]{1,0:T(8,128)(2,1)} %hidden_ref.1), custom_call_target="tpu_custom_call" | custom-call | tf_op jit(solution)/shard_map/pallas_call | solution.py:42
  33.2 6.2 %all-to-all-start.1 = ((bf16[128,4,1024]{2,1,0:T(4,128)(2,1)}), bf16[128,4,1024]{2,1,0:T(4,128)(2,1)S(1)}, u32[]{:S(2)}, u32[]{:S(2)}) async-start(bf16[128,4,1024]{2,1,0:T(4,128)(2,1)} %shard_map.68), calls=%async_computation.1 | async-start | bytes 2097152 | tf_op jit(solution)/shard_map/all_to_all | solution.py:46
  39.4 0.0 copy-done.1
  39.4 2.3 %collective-permute-start.1 = (bf16[8,1024]{1,0:T(8,128)(2,1)S(1)}, bf16[8,1024]{1,0:T(8,128)(2,1)S(1)}, u32[]{:S(2)}, u32[]{:S(2)}) collective-permute-start(bf16[8,1024]{1,0:T(8,128)(2,1)S(1)} %copy-done.1), channel_id=1, source_target_pairs={{0,1},{1,0},{2,3},{3,2},{4,5},{5,4},{6,7},{7,6},{8,9},{9,8},{10,11... | collective-permute-start | bytes 49160 | tf_op jit(solution)/shard_map/ppermute | solution.py:87
  41.8 0.0 copy-done.2
  41.8 0.1 compare_convert_fusion
  42.0 0.0 copy-done
  42.0 1.2 %fusion.4 = f32[8]{0:T(128)S(1)} fusion(bf16[1024,1024]{1,0:T(8,128)(2,1)S(1)} %copy-done, bf16[8,1024]{1,0:T(8,128)(2,1)S(1)} %copy-done.1, bf16[256,1024]{1,0:T(8,128)(2,1)} %hidden_ref.1, s32[]{:T(128)S(6)} %select_n.21), kind=kOutput, calls=%fused_computation.9 | convolution fusion | flops 16818168 | bytes 2129956 | tf_op jit(solution)/shard_map/dot_general | solution.py:59
  43.2 23.6 %all-to-all-done.1 = bf16[128,4,1024]{2,1,0:T(4,128)(2,1)S(1)} async-done(((bf16[128,4,1024]{2,1,0:T(4,128)(2,1)}), bf16[128,4,1024]{2,1,0:T(4,128)(2,1)S(1)}, u32[]{:S(2)}, u32[]{:S(2)}) %all-to-all-start.1) | async-done | bytes 1048608 | tf_op jit(solution)/shard_map/all_to_all | solution.py:46
  66.7 0.8 fusion.1
  67.6 0.7 convolution_convert_fusion.1
  68.3 0.2 fusion.20
  68.5 0.1 fusion.25
  68.7 0.5 multiply_add_fusion.4
  69.2 0.1 fusion.24
  69.3 0.3 fusion.5
  69.5 0.8 fusion.22
  70.3 5.0 %collective-permute-start = (bf16[16,1024]{1,0:T(8,128)(2,1)S(1)}, bf16[16,1024]{1,0:T(8,128)(2,1)S(1)}, u32[]{:S(2)}, u32[]{:S(2)}) collective-permute-start(bf16[16,1024]{1,0:T(8,128)(2,1)S(1)} %pad_maximum_fusion), channel_id=1, source_target_pairs={{0,1},{1,0},{2,3},{3,2},{4,5},{5,4},{6,7},{7,6},{8,9},{9,8},{10,11... | collective-permute-start | bytes 98312 | tf_op jit(solution)/shard_map/ppermute | solution.py:86
  75.3 0.0 collective-permute-done.1
  75.3 0.9 collective-permute-done
  76.2 0.5 fusion
  76.6 34.7 %all_to_all.22 = bf16[128,8,512]{2,1,0:T(8,128)(2,1)S(1)} all-to-all(bf16[128,8,512]{2,1,0:T(8,128)(2,1)S(1)} %fusion), channel_id=1, replica_groups=mesh['dp'=128,'group'=2] {'dp'}, dimensions={0} | all-to-all | bytes 2097152 | tf_op jit(solution)/shard_map/all_to_all | solution.py:97
  111.3 0.2 convert_reduce_fusion
  111.5 3.2 %collective-permute-start.2 = (f32[8,512]{1,0:T(8,128)S(1)}, f32[8,512]{1,0:T(8,128)S(1)}, u32[]{:S(2)}, u32[]{:S(2)}) collective-permute-start(f32[8,512]{1,0:T(8,128)S(1)} %convert_reduce_fusion), channel_id=1, source_target_pairs={{0,1},{1,0},{2,3},{3,2},{4,5},{5,4},{6,7},{7,6},{8,9},{9,8},{10,11... | collective-permute-start | bytes 49160 | tf_op jit(solution)/shard_map/ppermute | solution.py:99
  114.6 0.8 collective-permute-done.2
  115.5 0.6 maximum_select_fusion
  (5 shorter events, 0.0 us)
Async XLA Ops:
  0.6 41.3 %copy-start = (bf16[1024,1024]{1,0:T(8,128)(2,1)S(1)}, bf16[1024,1024]{1,0:T(8,128)(2,1)}, u32[]{:S(2)}) copy-start(bf16[1024,1024]{1,0:T(8,128)(2,1)} %param.7) | copy-start | bytes 6291460
  0.6 41.2 %copy-start.2 = (s32[256,1]{0,1:T(1,128)S(1)}, s32[256,1]{0,1:T(1,128)}, u32[]{:S(2)}) copy-start(s32[256,1]{0,1:T(1,128)} %param.8) | copy-start | bytes 3076
  0.7 38.8 %copy-start.1 = (bf16[8,1024]{1,0:T(8,128)(2,1)S(1)}, bf16[8,1024]{1,0:T(8,128)(2,1)}, u32[]{:S(2)}) copy-start(bf16[8,1024]{1,0:T(8,128)(2,1)} %param.5) | copy-start | bytes 49156
  33.2 33.5 %all-to-all-start.1 = ((bf16[128,4,1024]{2,1,0:T(4,128)(2,1)}), bf16[128,4,1024]{2,1,0:T(4,128)(2,1)S(1)}, u32[]{:S(2)}, u32[]{:S(2)}) async-start(bf16[128,4,1024]{2,1,0:T(4,128)(2,1)} %shard_map.68), calls=%async_computation.1 | async-start | bytes 2097152 | tf_op jit(solution)/shard_map/all_to_all | solution.py:46
  39.4 35.9 %collective-permute-start.1 = (bf16[8,1024]{1,0:T(8,128)(2,1)S(1)}, bf16[8,1024]{1,0:T(8,128)(2,1)S(1)}, u32[]{:S(2)}, u32[]{:S(2)}) collective-permute-start(bf16[8,1024]{1,0:T(8,128)(2,1)S(1)} %copy-done.1), channel_id=1, source_target_pairs={{0,1},{1,0},{2,3},{3,2},{4,5},{5,4},{6,7},{7,6},{8,9},{9,8},{10,11... | collective-permute-start | bytes 49160 | tf_op jit(solution)/shard_map/ppermute | solution.py:87
  70.3 5.8 %collective-permute-start = (bf16[16,1024]{1,0:T(8,128)(2,1)S(1)}, bf16[16,1024]{1,0:T(8,128)(2,1)S(1)}, u32[]{:S(2)}, u32[]{:S(2)}) collective-permute-start(bf16[16,1024]{1,0:T(8,128)(2,1)S(1)} %pad_maximum_fusion), channel_id=1, source_target_pairs={{0,1},{1,0},{2,3},{3,2},{4,5},{5,4},{6,7},{7,6},{8,9},{9,8},{10,11... | collective-permute-start | bytes 98312 | tf_op jit(solution)/shard_map/ppermute | solution.py:86
  111.5 4.0 %collective-permute-start.2 = (f32[8,512]{1,0:T(8,128)S(1)}, f32[8,512]{1,0:T(8,128)S(1)}, u32[]{:S(2)}, u32[]{:S(2)}) collective-permute-start(f32[8,512]{1,0:T(8,128)S(1)} %convert_reduce_fusion), channel_id=1, source_target_pairs={{0,1},{1,0},{2,3},{3,2},{4,5},{5,4},{6,7},{7,6},{8,9},{9,8},{10,11... | collective-permute-start | bytes 49160 | tf_op jit(solution)/shard_map/ppermute | solution.py:99

commit v18 on v12

--- a/solution.py
+++ b/solution.py
@@ -67,7 +67,6 @@
     )
     logits = jnp.concatenate([pos_logit[:, None], neg_logit], axis=1)
     log_total = jnp.log(jnp.sum(jnp.exp(logits), axis=1))
-    query_loss = log_total - pos_logit
     soft_prob = jnp.exp(logits - log_total[:, None])
     neg_coef = soft_prob[:, 1:] * score_scale
     pos_coef = (soft_prob[:, 0] - 1.0) * score_scale
@@ -94,6 +93,8 @@
     partial = partial.astype(jnp.bfloat16).reshape(dp_count, out_rows, col_half)
     partial = lax.all_to_all(partial, "dp", split_axis=0, concat_axis=0, tiled=True)
     weight_half = jnp.sum(partial.astype(jnp.float32), axis=0)
+    weight_half, log_total, pos_logit = lax.optimization_barrier((weight_half, log_total, pos_logit))
+    query_loss = log_total - pos_logit
     other_half = lax.ppermute(weight_half, "group", swap)
     weight_grad = jnp.where(
         group_pos == 0,

time: 117 us -> 117 us (level)
  no operation moved by 1% of the time
where the time goes in v18:
time: 117 us; the launch traced here: 116 us
  blocking collectives  61.9 us (53%)
  waiting for transfers between devices  24.8 us (21%)
  starting transfers between devices  16.8 us (14%)
  other arithmetic  4.67 us (4%)
  matrix products  3.48 us (3%)
  Pallas kernels  2.62 us (2%)
    all_to_all x1, blocking collectives, local(): lax.all_to_all(partial, 'dp', split_axis=0, concat_axis=0, tiled=True)  34.7 us
    all_to_all x1, blocking collectives, local(): lax.all_to_all(requests, 'dp', split_axis=0, concat_axis=0, tiled=True)  27.2 us
    all_to_all x1, waiting for transfers between devices, local(): lax.all_to_all(hidden_block, 'dp', split_axis=0, concat_axis=0, tiled=True)  23.6 us
    all_to_all x1, starting transfers between devices, local(): lax.all_to_all(hidden_block, 'dp', split_axis=0, concat_axis=0, tiled=True)  6.32 us
    ppermute x1, starting transfers between devices, local(): other_parts = lax.ppermute(mixed_parts, 'group', swap)  4.97 us
    ppermute x1, starting transfers between devices, local(): other_half = lax.ppermute(weight_half, 'group', swap)  3.15 us
    pallas_call x1, Pallas kernels, local(): pl.pallas_call(send_kernel, out_shape=jax.ShapeDtypeStruct((dp_count, cap...  2.62 us
    ppermute x1, starting transfers between devices, local(): other_queries = lax.ppermute(queries, 'group', swap)  2.35 us
  transfers between devices with their start and end apart: 4, of which 3 were waited for; matrix products, arithmetic and copies ran while one was open for 4% of the time, Pallas kernels for 0%

profile of v18, /device:TPU:1, one launch (start us, length us, event | category | flops | bytes accessed | tf_op | source)
XLA Modules:
  0.0 116.1 jit_solution(16338477260442120976)
XLA Ops:
  0.6 0.0 copy-start
  0.6 0.0 copy-start.1
  0.7 0.9 broadcast_in_dim.26
  1.6 0.9 convert_reduce_fusion.1
  2.5 0.7 multiply_add_fusion.2
  3.2 0.1 select_reduce_fusion
  3.3 0.1 all_to_all.13
  3.5 27.2 %all_to_all.21 = s32[128,1,4]{2,1,0:T(1,128)} all-to-all(s32[128,1,4]{2,1,0:T(1,128)S(1)} %bitcast.25), channel_id=1, replica_groups=mesh['dp'=128,'group'=2] {'dp'}, dimensions={0} | all-to-all | bytes 4096 | tf_op jit(solution)/shard_map/all_to_all | solution.py:41
  30.7 2.6 %shard_map.68 = bf16[128,4,1024]{2,1,0:T(4,128)(2,1)} custom-call(s32[128,4]{1,0:T(8,128)} %bitcast.24, bf16[256,1024]{1,0:T(8,128)(2,1)} %hidden_ref.1), custom_call_target="tpu_custom_call" | custom-call | tf_op jit(solution)/shard_map/pallas_call | solution.py:42
  33.3 0.0 copy-start.2
  33.3 6.3 %all-to-all-start.1 = ((bf16[128,4,1024]{2,1,0:T(4,128)(2,1)}), bf16[128,4,1024]{2,1,0:T(4,128)(2,1)S(1)}, u32[]{:S(2)}, u32[]{:S(2)}) async-start(bf16[128,4,1024]{2,1,0:T(4,128)(2,1)} %shard_map.68), calls=%async_computation.1 | async-start | bytes 2097152 | tf_op jit(solution)/shard_map/all_to_all | solution.py:46
  39.6 0.0 copy-done.1
  39.6 2.4 %collective-permute-start.1 = (bf16[8,1024]{1,0:T(8,128)(2,1)S(1)}, bf16[8,1024]{1,0:T(8,128)(2,1)S(1)}, u32[]{:S(2)}, u32[]{:S(2)}) collective-permute-start(bf16[8,1024]{1,0:T(8,128)(2,1)S(1)} %copy-done.1), channel_id=1, source_target_pairs={{0,1},{1,0},{2,3},{3,2},{4,5},{5,4},{6,7},{7,6},{8,9},{9,8},{10,11... | collective-permute-start | bytes 49160 | tf_op jit(solution)/shard_map/ppermute | solution.py:84
  42.0 0.0 copy-done
  42.0 1.2 %fusion.4 = f32[8]{0:T(128)S(1)} fusion(bf16[1024,1024]{1,0:T(8,128)(2,1)S(1)} %copy-done, bf16[8,1024]{1,0:T(8,128)(2,1)S(1)} %copy-done.1, bf16[256,1024]{1,0:T(8,128)(2,1)} %hidden_ref.1, s32[]{:T(128)S(6)} %select_n.20), kind=kOutput, calls=%fused_computation.9 | convolution fusion | flops 16818168 | bytes 2129956 | tf_op jit(solution)/shard_map/dot_general | solution.py:58
  43.2 0.1 copy.19
  43.3 0.0 copy-done.2
  43.3 23.6 %all-to-all-done.1 = bf16[128,4,1024]{2,1,0:T(4,128)(2,1)S(1)} async-done(((bf16[128,4,1024]{2,1,0:T(4,128)(2,1)}), bf16[128,4,1024]{2,1,0:T(4,128)(2,1)S(1)}, u32[]{:S(2)}, u32[]{:S(2)}) %all-to-all-start.1) | async-done | bytes 1048608 | tf_op jit(solution)/shard_map/all_to_all | solution.py:46
  66.9 0.9 fusion.1
  67.8 0.7 convolution_convert_fusion.1
  68.5 0.2 fusion.23
  68.8 0.2 exponential_reduce_fusion
  69.0 0.1 subtract_exponential_fusion
  69.0 0.1 slice_multiply_fusion
  69.1 0.1 multiply_reduce_fusion
  69.2 0.3 fusion.5
  69.5 0.8 fusion.25
  70.3 5.0 %collective-permute-start = (bf16[16,1024]{1,0:T(8,128)(2,1)S(1)}, bf16[16,1024]{1,0:T(8,128)(2,1)S(1)}, u32[]{:S(2)}, u32[]{:S(2)}) collective-permute-start(bf16[16,1024]{1,0:T(8,128)(2,1)S(1)} %pad_maximum_fusion), channel_id=1, source_target_pairs={{0,1},{1,0},{2,3},{3,2},{4,5},{5,4},{6,7},{7,6},{8,9},{9,8},{10,11... | collective-permute-start | bytes 98312 | tf_op jit(solution)/shard_map/ppermute | solution.py:83
  75.3 0.0 collective-permute-done.1
  75.3 0.9 collective-permute-done
  76.2 0.5 fusion
  76.6 34.7 %all_to_all.22 = bf16[128,8,512]{2,1,0:T(8,128)(2,1)S(1)} all-to-all(bf16[128,8,512]{2,1,0:T(8,128)(2,1)S(1)} %fusion), channel_id=1, replica_groups=mesh['dp'=128,'group'=2] {'dp'}, dimensions={0} | all-to-all | bytes 2097152 | tf_op jit(solution)/shard_map/all_to_all | solution.py:94
  111.3 0.2 convert_reduce_fusion
  111.5 3.2 %collective-permute-start.2 = (f32[8,512]{1,0:T(8,128)S(1)}, f32[8,512]{1,0:T(8,128)S(1)}, u32[]{:S(2)}, u32[]{:S(2)}) collective-permute-start(f32[8,512]{1,0:T(8,128)S(1)} %convert_reduce_fusion), channel_id=1, source_target_pairs={{0,1},{1,0},{2,3},{3,2},{4,5},{5,4},{6,7},{7,6},{8,9},{9,8},{10,11... | collective-permute-start | bytes 49160 | tf_op jit(solution)/shard_map/ppermute | solution.py:98
  114.7 0.5 sub.21
  115.2 0.3 collective-permute-done.2
  115.5 0.6 maximum_select_fusion
  (8 shorter events, 0.0 us)
Async XLA Ops:
  0.6 41.3 %copy-start = (bf16[1024,1024]{1,0:T(8,128)(2,1)S(1)}, bf16[1024,1024]{1,0:T(8,128)(2,1)}, u32[]{:S(2)}) copy-start(bf16[1024,1024]{1,0:T(8,128)(2,1)} %param.7) | copy-start | bytes 6291460
  0.6 39.0 %copy-start.1 = (bf16[8,1024]{1,0:T(8,128)(2,1)S(1)}, bf16[8,1024]{1,0:T(8,128)(2,1)}, u32[]{:S(2)}) copy-start(bf16[8,1024]{1,0:T(8,128)(2,1)} %param.5) | copy-start | bytes 49156
  33.3 10.0 %copy-start.2 = (s32[256,1]{0,1:T(1,128)S(1)}, s32[256,1]{0,1:T(1,128)}, u32[]{:S(2)}) copy-start(s32[256,1]{0,1:T(1,128)} %param.8) | copy-start | bytes 3076
  33.3 33.6 %all-to-all-start.1 = ((bf16[128,4,1024]{2,1,0:T(4,128)(2,1)}), bf16[128,4,1024]{2,1,0:T(4,128)(2,1)S(1)}, u32[]{:S(2)}, u32[]{:S(2)}) async-start(bf16[128,4,1024]{2,1,0:T(4,128)(2,1)} %shard_map.68), calls=%async_computation.1 | async-start | bytes 2097152 | tf_op jit(solution)/shard_map/all_to_all | solution.py:46
  39.6 35.7 %collective-permute-start.1 = (bf16[8,1024]{1,0:T(8,128)(2,1)S(1)}, bf16[8,1024]{1,0:T(8,128)(2,1)S(1)}, u32[]{:S(2)}, u32[]{:S(2)}) collective-permute-start(bf16[8,1024]{1,0:T(8,128)(2,1)S(1)} %copy-done.1), channel_id=1, source_target_pairs={{0,1},{1,0},{2,3},{3,2},{4,5},{5,4},{6,7},{7,6},{8,9},{9,8},{10,11... | collective-permute-start | bytes 49160 | tf_op jit(solution)/shard_map/ppermute | solution.py:84
  70.3 5.8 %collective-permute-start = (bf16[16,1024]{1,0:T(8,128)(2,1)S(1)}, bf16[16,1024]{1,0:T(8,128)(2,1)S(1)}, u32[]{:S(2)}, u32[]{:S(2)}) collective-permute-start(bf16[16,1024]{1,0:T(8,128)(2,1)S(1)} %pad_maximum_fusion), channel_id=1, source_target_pairs={{0,1},{1,0},{2,3},{3,2},{4,5},{5,4},{6,7},{7,6},{8,9},{9,8},{10,11... | collective-permute-start | bytes 98312 | tf_op jit(solution)/shard_map/ppermute | solution.py:83
  111.5 4.0 %collective-permute-start.2 = (f32[8,512]{1,0:T(8,128)S(1)}, f32[8,512]{1,0:T(8,128)S(1)}, u32[]{:S(2)}, u32[]{:S(2)}) collective-permute-start(f32[8,512]{1,0:T(8,128)S(1)} %convert_reduce_fusion), channel_id=1, source_target_pairs={{0,1},{1,0},{2,3},{3,2},{4,5},{5,4},{6,7},{7,6},{8,9},{9,8},{10,11... | collective-permute-start | bytes 49160 | tf_op jit(solution)/shard_map/ppermute | solution.py:98
